TPU v7x, 512 devices: a whole 4x4x16 slice. The times are simulated.
512 devices in a mesh: ctx: 64 (over z, x), ch: 8 (over y, core).
Axes of the slice: x: 4, y: 4, z: 16, core: 2. Of those that a mesh axis runs over, the one named last changes fastest.
Arguments:
- projections: bfloat16 [3, 16384, 8192], P(None, ('ctx', 'ch')), may hold values from -3 to 3
- attention_order: int32 [16384], replicated, may hold values from 0 to 16383, as said below
- doc_lengths: int32 [4], replicated, may hold values from 1 to 8192, 16384 in all
- short_filter: float32 [3, 3, 8192], P(None, None, 'ch'), may hold values from -3.5 to 3.5
- decay_rate: float32 [512, 16], P('ch'), may hold values from 6.1035157e-06 to 0.03
- residue: float32 [512, 16], P('ch'), may hold values from -1.5 to 1.5
- skip_gain: float32 [8192], P('ch'), may hold values from -2.5 to 2.5
Outputs:
- mixed_rows: bfloat16 [16384, 8192], P(('ctx', 'ch'))
Inputs may be any that keep to these rules, and one draw needn't show every extreme that they name: `attention_order`: A permutation of the 16384 positions. For every group a of 256 rows (rows a * 256 to (a + 1) * 256 - 1) and every context block j, the rows a * 256 + j * 4 to a * 256 + (j + 1) * 4 - 1 hold positions of block j, that is j * 256 to (j + 1) * 256 - 1, in any order. `doc_lengths`: the documents lie one after another in the slab; the lengths sum to 16384.
All inputs are finite; a program needn't handle non-finite values.
Results may differ from a plain program's by a relative error of at most 0.0049.
Values may be sent and summed in bfloat16 or wider, within the bound.
No kernel may reach another device: no remote copies, remote signals or barrier semaphores. Data moves between devices by JAX's collectives and lax.ppermute only.
A program may use at most 64 MiB of HBM per device.

v0:
```python
import jax
import jax.numpy as jnp
from jax import lax
from jax.sharding import PartitionSpec as P

highest = lax.Precision.HIGHEST


def from_behind(value, axis, steps):
    count = lax.axis_size(axis)
    first, last = (max(0, -steps), min(count, count - steps))
    return lax.ppermute(value, axis, [(source, source + steps) for source in range(first, last)])


def entering(value, axis, combine, identity):
    devices, here = (lax.axis_size(axis), lax.axis_index(axis))
    everything = jax.tree.map(lambda part: lax.all_gather(part, axis), value)
    start = jax.tree.map(
        lambda part, zero: jnp.broadcast_to(jnp.asarray(zero, part.dtype), part.shape),
        value,
        identity,
    )

    def turn(k, before):
        reached = k < here
        new = combine(before, jax.tree.map(lambda part: part[k], everything))
        return jax.tree.map(lambda a, b: jnp.where(reached, a, b), new, before)

    return lax.fori_loop(0, devices, turn, start)


def doc_index(positions, bounds):
    return jnp.sum((positions[:, None] >= bounds[None, :]).astype(jnp.int32), axis=1)


def combine_states(earlier, later):
    return (earlier[0] * later[0], later[0] * earlier[1] + later[1])


def shards(projections, attention_order, doc_lengths, short_filter, decay_rate, residue, skip_gain):
    block_total = lax.axis_size("ctx")
    block_index = lax.axis_index("ctx")
    channels = short_filter.shape[2]
    row_count = projections.shape[1] * lax.axis_size("ch")
    slot_rows = row_count // block_total
    modes = decay_rate.shape[1]
    groups = decay_rate.shape[0]
    group_width = channels // groups
    first_row = block_index * row_count
    routing = attention_order.reshape(block_total, block_total, slot_rows)
    arrived = lax.dynamic_slice_in_dim(routing, block_index, 1, 1).reshape(row_count) - first_row
    placer = (arrived[None, :] == jnp.arange(row_count, dtype=jnp.int32)[:, None]).astype(
        jnp.bfloat16
    )
    received = lax.all_to_all(
        lax.all_to_all(projections, "ch", split_axis=2, concat_axis=1, tiled=True),
        "ctx",
        split_axis=1,
        concat_axis=1,
        tiled=True,
    )
    ordered = jnp.einsum(
        "tr,prc->ptc", placer, received, preferred_element_type=jnp.float32
    ).astype(jnp.bfloat16)
    earlier_rows = from_behind(ordered[:, row_count - 2 :, :], "ctx", 1)
    bounds = jnp.cumsum(doc_lengths)
    span_docs = doc_index(first_row - 2 + jnp.arange(row_count + 2, dtype=jnp.int32), bounds)
    current = span_docs[2:]
    previous_doc = span_docs[1]
    widened = jnp.concatenate([earlier_rows, ordered], axis=1)
    featured = jnp.zeros((3, row_count, channels), jnp.float32)
    for offset in range(3):
        same_doc = (span_docs[2 - offset : 2 - offset + row_count] == current).astype(jnp.float32)
        featured = (
            featured
            + short_filter[:, offset, None, :]
            * widened[:, 2 - offset : 2 - offset + row_count, :]
            * same_doc[None, :, None]
        )
    gated = lax.optimization_barrier((featured[1] * featured[2]).astype(jnp.bfloat16))
    coefficient = residue * jnp.sqrt(1.0 - jnp.exp(-2.0 * decay_rate))
    steps_float = jnp.arange(row_count, dtype=jnp.float32)
    tokens_index = jnp.arange(row_count, dtype=jnp.int32)
    causal = (
        (tokens_index[:, None] >= tokens_index[None, :]) & (current[:, None] == current[None, :])
    ).astype(jnp.float32)
    end_same = (current == current[row_count - 1]).astype(jnp.float32)
    carry_same = (current == previous_doc).astype(jnp.float32)
    group_batch = 8
    batch_count = groups // group_batch
    rate_blocks = decay_rate.reshape(batch_count, group_batch, modes)
    coeff_blocks = coefficient.reshape(batch_count, group_batch, modes)
    gated_blocks = jnp.moveaxis(
        gated.reshape(row_count, batch_count, group_batch * group_width), 1, 0
    )

    def local_block(inputs):
        rate_rows, coeffs, values = inputs
        values_wide = values.astype(jnp.float32).reshape(row_count, group_batch, group_width)
        falling = coeffs[:, :, None] * jnp.exp(-rate_rows[:, :, None] * steps_float[None, None, :])
        rising = jnp.exp(rate_rows[:, :, None] * steps_float[None, None, :])
        toeplitz = jnp.einsum("bmt,bms->bts", falling, rising, precision=highest) * causal[None]
        filtered_part = jnp.einsum("bts,sbc->tbc", toeplitz, values_wide, precision=highest)
        ending = (
            jnp.exp(-rate_rows[:, :, None] * (row_count - 1.0 - steps_float)[None, None, :])
            * end_same[None, None, :]
        )
        state_part = jnp.einsum("bms,sbc->mbc", ending, values_wide, precision=highest)
        return (
            filtered_part.reshape(row_count, group_batch * group_width),
            state_part.reshape(modes, group_batch * group_width),
        )

    filtered_blocks, state_blocks = lax.map(local_block, (rate_blocks, coeff_blocks, gated_blocks))
    filtered = jnp.moveaxis(filtered_blocks, 0, 1).reshape(row_count, channels)
    state_end = jnp.moveaxis(state_blocks, 0, 1).reshape(modes, channels)
    rate_wide = jnp.repeat(decay_rate.T, group_width, axis=1)
    linking = (previous_doc == current[row_count - 1]).astype(jnp.float32)
    factor = jnp.exp(-rate_wide * row_count) * linking
    carried = entering(
        (factor, state_end),
        "ctx",
        combine_states,
        (jnp.ones_like(factor), jnp.zeros_like(state_end)),
    )[1]
    reaching = coefficient[:, :, None] * jnp.exp(
        -decay_rate[:, :, None] * (steps_float + 1.0)[None, None, :]
    )
    incoming = jnp.einsum(
        "gmt,mgc->tgc", reaching, carried.reshape(modes, groups, group_width), precision=highest
    ).reshape(row_count, channels)
    combined = (
        filtered + incoming * carry_same[:, None] + skip_gain[None, :] * gated.astype(jnp.float32)
    )
    mixed = (featured[0] * combined).astype(jnp.bfloat16)
    returned = jnp.einsum("tr,tc->rc", placer, mixed, preferred_element_type=jnp.float32).astype(
        jnp.bfloat16
    )
    return lax.all_to_all(
        lax.all_to_all(returned, "ctx", split_axis=0, concat_axis=0, tiled=True),
        "ch",
        split_axis=0,
        concat_axis=1,
        tiled=True,
    )


def solution(mesh):
    placed = (
        P(None, ("ctx", "ch"), None),
        P(),
        P(),
        P(None, None, "ch"),
        P("ch", None),
        P("ch", None),
        P("ch"),
    )
    return jax.shard_map(
        shards, mesh=mesh, in_specs=placed, out_specs=P(("ctx", "ch"), None), check_vma=False
    )
```

profile of v0, /device:TPU:1, one launch (start us, length us, event | category | flops | bytes accessed | tf_op | source)
XLA Modules:
  0.0 527.8 jit_solution(16877668202568889552)
XLA Ops:
  6.5 10.6 %copy.55 = bf16[3,32,8192]{1,0,2:T(4,128)(2,1)} copy(bf16[3,32,8192]{2,1,0:T(8,128)(2,1)} %param.11) | data formatting | bytes 3145728 | tf_op args[0]
  17.2 8.9 %reshape.148 = bf16[8,2,49152]{2,1,0:T(2,128)(2,1)S(1)} reshape(bf16[8192,3,32]{2,1,0:T(4,128)(2,1)} %bitcast.91) | data formatting | bytes 3145728
  26.1 29.8 %all_to_all.51 = bf16[8,2,49152]{2,1,0:T(2,128)(2,1)S(1)} all-to-all(bf16[8,2,49152]{2,1,0:T(2,128)(2,1)S(1)} %reshape.148), channel_id=1, replica_groups=mesh['ctx'=64,'ch'=8] {'ch'}, dimensions={0} | all-to-all | bytes 3145728 | tf_op jit(solution)/shard_map/all_to_all | solution.py:56
  55.9 7.6 %reshape.149 = bf16[8192,3,32]{2,1,0:T(4,128)(2,1)} reshape(bf16[8,2,49152]{2,1,0:T(2,128)(2,1)S(1)} %all_to_all.51) | data formatting | bytes 3145728
  63.5 13.2 %copy.56 = bf16[3,8,32,1024]{3,0,2,1:T(4,128)(2,1)} copy(bf16[3,8,32,1024]{2,0,3,1:T(4,128)(2,1)} %bitcast.90) | data formatting | bytes 3145728 | tf_op jit(solution)/shard_map/all_to_all | solution.py:56
  76.7 14.9 %all-to-all-start.1 = ((bf16[3,256,1024]{2,0,1:T(4,128)(2,1)}), bf16[3,256,1024]{2,0,1:T(4,128)(2,1)S(1)}, u32[]{:S(2)}, u32[]{:S(2)}) async-start(bf16[3,256,1024]{2,0,1:T(4,128)(2,1)} %bitcast.3), calls=%async_computation.1 | async-start | bytes 4194304 | tf_op jit(solution)/shard_map/all_to_all | solution.py:55
  95.0 3.5 reshape.129
  98.5 1.1 subtract_reduce_fusion
  99.7 91.8 %all-to-all-done.1 = bf16[3,256,1024]{2,0,1:T(4,128)(2,1)S(1)} async-done(((bf16[3,256,1024]{2,0,1:T(4,128)(2,1)}), bf16[3,256,1024]{2,0,1:T(4,128)(2,1)S(1)}, u32[]{:S(2)}, u32[]{:S(2)}) %all-to-all-start.1) | async-done | bytes 1572896 | tf_op jit(solution)/shard_map/all_to_all | solution.py:55
  191.5 1.3 fusion.28
  192.8 1.2 copy-done
  194.0 5.8 %collective-permute-start = (bf16[3,2,1024]{2,1,0:T(2,128)(2,1)S(1)}, bf16[3,2,1024]{2,1,0:T(2,128)(2,1)S(1)}, u32[]{:S(2)}, u32[]{:S(2)}) collective-permute-start(bf16[3,2,1024]{2,1,0:T(2,128)(2,1)S(1)} %slice.59), channel_id=1, source_target_pairs={{0,8},{8,16},{16,24},{24,32},{32,40},{40,48},{48,56},{56,64},{64,7... | collective-permute-start | bytes 36872 | tf_op jit(solution)/shard_map/ppermute | solution.py:12
  199.7 1.3 compare_convert_fusion
  201.2 3.4 multiply_add_fusion
  204.7 0.9 fusion.39
  205.6 2.1 copy.68
  207.7 45.4 %while.28 = (s32[]{:T(128)}, f32[8,256,128]{1,2,0:T(8,128)}, f32[8,16,128]{1,2,0:T(8,128)}, bf16[8,256,128]{1,2,0:T(8,128)(2,1)}, f32[8,8,16]{2,1,0:T(8,128)S(1)...) while((s32[]{:T(128)}, f32[8,256,128]{1,2,0:T(8,128)}, ...), condition=%wide.region_3.4_spmd.clone.clone, body=%wide.region_2.3_spmd.clone.clone.sunk | while | flops 208568704 | bytes 5465705 | solution.py:114
  207.7 2.0 fusion.75
  210.6 1.1 fusion.77
  213.4 2.0 fusion.75
  216.3 1.1 fusion.77
  219.0 2.0 fusion.75
  222.0 1.1 fusion.77
  224.7 2.0 fusion.75
  227.7 1.1 fusion.77
  230.4 2.0 fusion.75
  233.3 1.1 fusion.77
  236.1 2.0 fusion.75
  239.0 1.1 fusion.77
  241.8 2.0 fusion.75
  244.7 1.1 fusion.77
  247.4 2.0 fusion.75
  250.4 1.1 fusion.77
  253.1 1.8 copy.70
  255.0 2.6 copy.69
  257.7 135.3 %all-gather.5.cloned.1.call-done = f32[64,16,1024]{2,1,0:T(8,128)} async-done(((f32[1,16,1024]{2,1,0:T(8,128)}), f32[64,16,1024]{2,1,0:T(8,128)}) %all-gather.5.cloned.1.call-update) | async-done | bytes 4194320 | tf_op jit(solution)/shard_map/all_gather | solution.py:17
  393.0 59.9 %while.29 = (s32[]{:T(128)}, f32[16,1024]{1,0:T(8,128)S(1)}, s32[]{:T(128)}, f32[64,16,1024]{2,1,0:T(8,128)}, f32[64,16,1024]{2,1,0:T(8,128)}, /*index=5*/s32[]{:T(128)}, s32[]{:T(128)}) while((s32[]{:T(128)}, f32[16,1024]{1,0:T(8,128)S(1)}, s32[]{:T(128)}, f32[64,16,1024]{2,1,0:T(8,128)}, f32[64,16,1024]{2,1,0:T(8,128)}, ...), condition=%wide.region_5.6_spmd.clone, body=%wide.region_4.5_spmd.clone.sunk | while | flops 65540 | bytes 262245 | solution.py:29
  393.9 0.9 fusion.79
  394.8 0.9 fusion.79
  395.8 0.9 fusion.79
  396.7 0.9 fusion.79
  397.6 0.9 fusion.79
  398.6 0.9 fusion.79
  399.5 0.9 fusion.79
  400.5 0.9 fusion.79
  401.4 0.9 fusion.79
  402.3 0.9 fusion.79
  403.3 0.9 fusion.79
  406.1 0.9 fusion.79
  414.5 0.9 fusion.79
  415.4 0.9 fusion.79
  423.9 0.9 fusion.79
  432.3 0.9 fusion.79
  433.2 0.9 fusion.79
  441.7 0.9 fusion.79
  450.1 0.9 fusion.79
  451.0 0.9 fusion.79
  452.9 1.0 copy.71
  453.9 3.2 fusion.34
  457.1 2.5 copy.66
  459.7 3.0 convolution_convert_fusion.1
  462.7 1.2 all_to_all.41
  464.0 31.0 %all_to_all.52 = bf16[64,4,1024]{2,1,0:T(4,128)(2,1)S(1)} all-to-all(bf16[64,4,1024]{2,1,0:T(4,128)(2,1)S(1)} %all_to_all.41), channel_id=1, replica_groups=mesh['ctx'=64,'ch'=8] {'ctx'}, dimensions={0} | all-to-all | bytes 1048576 | tf_op jit(solution)/shard_map/all_to_all | solution.py:140
  495.1 25.1 %all_to_all.53 = bf16[8,32,1024]{2,1,0:T(8,128)(2,1)S(1)} all-to-all(bf16[8,32,1024]{2,1,0:T(8,128)(2,1)S(1)} %all_to_all.43), channel_id=1, replica_groups=mesh['ctx'=64,'ch'=8] {'ch'}, dimensions={0} | all-to-all | bytes 1048576 | tf_op jit(solution)/shard_map/all_to_all | solution.py:139
  (149 shorter events, 64.1 us)
Async XLA Ops:
  76.7 15.0 %copy-start.6 = (s32[4]{0:T(128)S(1)}, s32[4]{0:T(128)}, u32[]{:S(2)}) copy-start(s32[4]{0:T(128)} %param.13) | copy-start | bytes 52
  76.7 17.1 %copy-start.2 = (f32[64,16]{0,1:T(8,128)S(1)}, f32[64,16]{0,1:T(8,128)}, u32[]{:S(2)}) copy-start(f32[64,16]{0,1:T(8,128)} %param.15) | copy-start | bytes 12292
  76.7 17.1 %copy-start.4 = (f32[64,16]{0,1:T(8,128)S(1)}, f32[64,16]{0,1:T(8,128)}, u32[]{:S(2)}) copy-start(f32[64,16]{0,1:T(8,128)} %param.16) | copy-start | bytes 12292
  76.7 18.3 %copy-start.1 = (s32[16384]{0:T(1024)S(1)}, s32[16384]{0:T(1024)}, u32[]{:S(2)}) copy-start(s32[16384]{0:T(1024)} %param.12) | copy-start | bytes 196612
  76.7 23.0 %copy-start.3 = (f32[3,3,1024]{2,1,0:T(4,128)S(1)}, f32[3,3,1024]{2,1,0:T(4,128)}, u32[]{:S(2)}) copy-start(f32[3,3,1024]{2,1,0:T(4,128)} %param.14) | copy-start | bytes 110596
  76.7 114.8 %all-to-all-start.1 = ((bf16[3,256,1024]{2,0,1:T(4,128)(2,1)}), bf16[3,256,1024]{2,0,1:T(4,128)(2,1)S(1)}, u32[]{:S(2)}, u32[]{:S(2)}) async-start(bf16[3,256,1024]{2,0,1:T(4,128)(2,1)} %bitcast.3), calls=%async_computation.1 | async-start | bytes 4194304 | tf_op jit(solution)/shard_map/all_to_all | solution.py:55
  91.6 166.0 %all-gather.3.cloned.1.call-start = ((), (), s32[]{:S(2)}) async-start(), calls=%async_computation.4 | async-start | bytes 4259840 | tf_op jit(solution)/shard_map/all_gather | solution.py:17
  94.9 298.0 %all-gather.5.cloned.1.call-start = ((), (), s32[]{:S(2)}) async-start(), calls=%async_computation.5 | async-start | bytes 4259840 | tf_op jit(solution)/shard_map/all_gather | solution.py:17
  192.7 1.2 copy-start
  194.0 7.3 %collective-permute-start = (bf16[3,2,1024]{2,1,0:T(2,128)(2,1)S(1)}, bf16[3,2,1024]{2,1,0:T(2,128)(2,1)S(1)}, u32[]{:S(2)}, u32[]{:S(2)}) collective-permute-start(bf16[3,2,1024]{2,1,0:T(2,128)(2,1)S(1)} %slice.59), channel_id=1, source_target_pairs={{0,8},{8,16},{16,24},{24,32},{32,40},{40,48},{48,56},{56,64},{64,7... | collective-permute-start | bytes 36872 | tf_op jit(solution)/shard_map/ppermute | solution.py:12
  257.7 202.0 %copy-start.5 = (f32[1024]{0:T(1024)S(1)}, f32[1024]{0:T(1024)}, u32[]{:S(2)}) copy-start(f32[1024]{0:T(1024)} %param.17) | copy-start | bytes 12292
Sparse Core Ops, SparseCore 0:
  95.4 153.8 all-gather.2
  255.1 137.8 all-gather.4
where the time goes:
time: 533 us; the launch traced here: 528 us
  waiting for transfers between devices  227 us (43%)
  blocking collectives  85.9 us (16%)
  local copies, waits for them, and re-layouts  76.6 us (14%)
  other arithmetic  66.4 us (12%)
  matrix products  34.7 us (7%)
  starting transfers between devices  20.8 us (4%)
  between operations  14.8 us (3%)
    all_gather x2, waiting for transfers between devices, entering(): everything = jax.tree.map(lambda part: lax.all_gather(part, axis), value)  135 us
    all_to_all x1, waiting for transfers between devices, shards(): lax.all_to_all(lax.all_to_all(projections, 'ch', split_axis=2, concat_axi...  91.8 us
    select_n x64, other arithmetic, turn(): return jax.tree.map(lambda a, b: jnp.where(reached, a, b), new, before)  58.6 us
    all_to_all x1, blocking collectives, shards(): lax.all_to_all(returned, 'ctx', split_axis=0, concat_axis=0, tiled=True)  31 us
    all_to_all x1, blocking collectives, shards(): lax.all_to_all(projections, 'ch', split_axis=2, concat_axis=1, tiled=True)  29.8 us
    unnamed x20, local copies, waits for them, and re-layouts  28.4 us
    all_to_all x1, blocking collectives, shards(): lax.all_to_all(lax.all_to_all(returned, 'ctx', split_axis=0, concat_axis=...  25.1 us
    dot_general x8, matrix products, local_block(): jnp.einsum('bmt,bms->bts', falling, rising, precision=highest)  15.8 us
  transfers between devices with their start and end apart: 4, of which 2 were waited for; matrix products, arithmetic and copies ran while one was open for 12% of the time, Pallas kernels for 0%

commit v1 on v0

v1 whole, which is shorter than its diff:
```python
import jax
import jax.numpy as jnp
from jax import lax
from jax.sharding import PartitionSpec as P

highest = lax.Precision.HIGHEST


def doc_index(positions, bounds):
    found = jnp.sum((positions[:, None] >= bounds[None, :]).astype(jnp.int32), axis=1)
    return jnp.where(positions >= 0, found, -1)


def shards(projections, attention_order, doc_lengths, short_filter, decay_rate, residue, skip_gain):
    n_ctx = lax.axis_size("ctx")
    n_ch = lax.axis_size("ch")
    here_ctx = lax.axis_index("ctx")
    here_ch = lax.axis_index("ch")
    feeds, rows_here, channels = projections.shape
    tokens = attention_order.shape[0]
    block = tokens // n_ctx
    slot = block // n_ctx
    chunks = rows_here // slot
    span = chunks * block
    width = channels // n_ctx
    local_groups, modes = decay_rate.shape
    local_channels = short_filter.shape[2]
    group_width = local_channels // local_groups
    groups = width // group_width
    n_docs = doc_lengths.shape[0]

    sizes = (short_filter.size, decay_rate.size, residue.size, skip_gain.size)
    flat = jnp.concatenate(
        [short_filter.reshape(-1), decay_rate.reshape(-1), residue.reshape(-1), skip_gain.reshape(-1)]
    )
    every = lax.all_gather(flat, "ch")
    o1 = sizes[0]
    o2 = o1 + sizes[1]
    o3 = o2 + sizes[2]
    sf_all = jnp.transpose(every[:, :o1].reshape(n_ch, 3, 3, local_channels), (1, 2, 0, 3)).reshape(
        3, 3, n_ch * local_channels
    )
    sf = lax.dynamic_slice_in_dim(sf_all, here_ctx * width, width, 2)
    rate = lax.dynamic_slice_in_dim(every[:, o1:o2].reshape(n_ch * local_groups, modes), here_ctx * groups, groups, 0)
    res = lax.dynamic_slice_in_dim(every[:, o2:o3].reshape(n_ch * local_groups, modes), here_ctx * groups, groups, 0)
    skip = lax.dynamic_slice_in_dim(every[:, o3:].reshape(n_ch * local_channels), here_ctx * width, width, 0)
    coefficient = res * jnp.sqrt(1.0 - jnp.exp(-2.0 * rate))

    received = lax.all_to_all(projections, "ctx", 2, 1, tiled=True)
    received = received.reshape(feeds, n_ctx, chunks, slot, width)
    received = jnp.transpose(received, (0, 2, 1, 3, 4)).reshape(feeds, chunks, n_ctx * slot, width)
    routing = attention_order.reshape(n_ctx, tokens // slot // n_ctx, slot)
    mine = lax.dynamic_slice_in_dim(routing, here_ch * chunks, chunks, 1)
    offsets = jnp.transpose(mine, (1, 0, 2)).reshape(chunks, n_ctx * slot)
    offsets = offsets - (here_ch * chunks + jnp.arange(chunks, dtype=jnp.int32))[:, None] * block
    placer = (offsets[:, None, :] == jnp.arange(block, dtype=jnp.int32)[None, :, None]).astype(jnp.bfloat16)
    ordered = jnp.einsum("kwr,pkrc->pkwc", placer, received, preferred_element_type=jnp.float32)
    ordered = ordered.astype(jnp.bfloat16).reshape(feeds, span, width)

    earlier = lax.ppermute(ordered[:, span - 2 :, :], "ch", [(i, i + 1) for i in range(n_ch - 1)])
    widened = jnp.concatenate([earlier, ordered], axis=1).astype(jnp.float32)
    bounds = jnp.cumsum(doc_lengths).astype(jnp.int32)
    span_docs = doc_index(here_ch * span - 2 + jnp.arange(span + 2, dtype=jnp.int32), bounds)
    current = span_docs[2:]
    keep_one = (span_docs[1 : 1 + span] == current).astype(jnp.float32)[None, :, None]
    keep_two = (span_docs[0:span] == current).astype(jnp.float32)[None, :, None]
    featured = (
        sf[:, 0, None, :] * widened[:, 2:]
        + sf[:, 1, None, :] * widened[:, 1 : 1 + span] * keep_one
        + sf[:, 2, None, :] * widened[:, 0:span] * keep_two
    )
    gated = (featured[1] * featured[2]).astype(jnp.bfloat16)

    steps = jnp.arange(block, dtype=jnp.float32)
    falling = coefficient[:, None, :] * jnp.exp(-rate[:, None, :] * steps[None, :, None])
    rising = jnp.exp(rate[:, :, None] * steps[None, None, :])
    lower = steps[:, None] >= steps[None, :]
    toeplitz = jnp.where(
        lower[None], jnp.einsum("gtm,gms->gts", falling, rising, precision=highest), 0.0
    )
    toe_hi = toeplitz.astype(jnp.bfloat16)
    toe_lo = (toeplitz - toe_hi.astype(jnp.float32)).astype(jnp.bfloat16)
    toe_both = jnp.concatenate([toe_hi, toe_lo], axis=2)
    x = gated.reshape(chunks, block, groups, group_width)
    docs_k = current.reshape(chunks, block)
    doc_ids = jnp.arange(n_docs, dtype=jnp.int32)
    in_doc = docs_k[None] == doc_ids[:, None, None]
    xd = jnp.where(in_doc[:, :, :, None, None], x[None], jnp.zeros((), jnp.bfloat16))
    xd = jnp.concatenate([xd, xd], axis=2)
    per_doc = jnp.einsum("gts,dksgc->dktgc", toe_both, xd, preferred_element_type=jnp.float32)
    intra = jnp.sum(jnp.where(in_doc[:, :, :, None, None], per_doc, 0.0), axis=0)

    x32 = x.astype(jnp.float32)
    ends_doc = docs_k[:, block - 1]
    at_end = (docs_k == ends_doc[:, None]).astype(jnp.float32)
    towards_end = jnp.exp(-rate[:, :, None] * (block - 1.0 - steps)[None, None, :])
    chunk_state = jnp.einsum(
        "gms,ksgc->kgmc", towards_end, x32 * at_end[:, :, None, None], precision=highest
    )
    chunk_ids = jnp.arange(chunks, dtype=jnp.int32)
    lag = (chunk_ids[:, None] - chunk_ids[None, :]).astype(jnp.float32)
    linked = (chunk_ids[:, None] >= chunk_ids[None, :]) & (ends_doc[:, None] == ends_doc[None, :])
    carry_weight = jnp.where(
        linked[:, :, None, None],
        jnp.exp(-rate[None, None] * (block * jnp.maximum(lag, 0.0))[:, :, None, None]),
        0.0,
    )
    local_state = jnp.sum(carry_weight[:, :, :, :, None] * chunk_state[None], axis=1)

    previous_doc = span_docs[1]
    span_factor = jnp.exp(-rate * float(span)) * (previous_doc == current[span - 1]).astype(jnp.float32)
    packed = jnp.concatenate([span_factor.reshape(-1), local_state[chunks - 1].reshape(-1)])
    gathered = lax.all_gather(packed, "ch")
    factors = gathered[:, : groups * modes].reshape(n_ch, groups, modes, 1)
    states = gathered[:, groups * modes :].reshape(n_ch, groups, modes, group_width)
    entering = jnp.zeros((groups, modes, group_width), jnp.float32)
    for source in range(n_ch):
        entering = jnp.where(source < here_ch, factors[source] * entering + states[source], entering)

    reach = jnp.exp(-rate[None] * (block * (chunk_ids + 1.0))[:, None, None])
    joined = (previous_doc == ends_doc).astype(jnp.float32)[:, None, None, None]
    total_state = local_state + reach[..., None] * joined * entering[None]
    before = jnp.concatenate([entering[None], total_state[: chunks - 1]], axis=0)
    start_prev_doc = jnp.concatenate([previous_doc[None], docs_k[: chunks - 1, block - 1]])
    from_before = (docs_k == start_prev_doc[:, None]).astype(jnp.float32)
    decaying = coefficient[:, None, :] * jnp.exp(-rate[:, None, :] * (steps + 1.0)[None, :, None])
    incoming = jnp.einsum("gtm,kgmc->ktgc", decaying, before, precision=highest)
    filtered = intra + incoming * from_before[:, :, None, None]

    gated32 = gated.astype(jnp.float32)
    combined = filtered.reshape(span, width) + skip[None, :] * gated32
    mixed = (featured[0] * combined).astype(jnp.bfloat16)

    back = jnp.einsum(
        "kwr,kwc->krc", placer, mixed.reshape(chunks, block, width), preferred_element_type=jnp.float32
    ).astype(jnp.bfloat16)
    back = jnp.transpose(back.reshape(chunks, n_ctx, slot, width), (1, 0, 2, 3)).reshape(
        n_ctx * rows_here, width
    )
    return lax.all_to_all(back, "ctx", 0, 1, tiled=True)


def solution(mesh):
    placed = (
        P(None, ("ctx", "ch"), None),
        P(),
        P(),
        P(None, None, "ch"),
        P("ch", None),
        P("ch", None),
        P("ch"),
    )
    return jax.shard_map(
        shards, mesh=mesh, in_specs=placed, out_specs=P(("ctx", "ch"), None), check_vma=False
    )
```

time: 533 us -> 229 us (0.43)
  waiting for transfers between devices: 227 us -> 42.7 us
  other arithmetic: 66.4 us -> 11.4 us
  matrix products: 34.7 us -> 10.3 us
  blocking collectives: 85.9 us -> 64.2 us
  between operations: 14.8 us -> 1.95 us
  local copies, waits for them, and re-layouts: 76.6 us -> 68.7 us
  starting transfers between devices: 20.8 us -> 27.7 us
    all_gather x2 -> x0, waiting for transfers between devices: 135 us -> none  [entering(): everything = jax.tree.map(lambda part: lax.all_gather(part, axis), value)]
    select_n x64 -> x5, other arithmetic: 58.6 us -> 1.22 us  [the longest x1 0.86 us: shards(): jnp.where(in_doc[:, :, :, None, None], x[None], jnp.zeros((), jnp.bfloat16))]
    all_to_all x3 -> x1, blocking collectives: 85.9 us -> 36.5 us  [shards(): return lax.all_to_all(back, 'ctx', 0, 1, tiled=True)]
    all_to_all x1, waiting for transfers between devices: 91.8 us -> 42.7 us  [shards(): received = lax.all_to_all(projections, 'ctx', 2, 1, tiled=True)]
    all_gather x0 -> x2, blocking collectives: none -> 27.7 us  [the longest x1 14.3 us: shards(): every = lax.all_gather(flat, 'ch')]
    dot_general x27 -> x6, matrix products: 34.7 us -> 10.3 us  [the longest x1 3.08 us: shards(): jnp.einsum('gtm,gms->gts', falling, rising, precision=highest)]
    dynamic_update_slice x16 -> x0, local copies, waits for them, and re-layouts: 10.4 us -> none  [shards(): lax.map(local_block, (rate_blocks, coeff_blocks, gated_blocks))]
    squeeze x0 -> x33, local copies, waits for them, and re-layouts: none -> 8.57 us  [the longest x32 8.24 us: shards(): states[source]]
  transfers between devices with their start and end apart: 4 -> 2, of which waited for: 2 -> 1; matrix products, arithmetic and copies ran while one was open for 12% -> 7% of each run, Pallas kernels for 0% -> 0%
where the time goes in v1:
time: 229 us; the launch traced here: 227 us
  local copies, waits for them, and re-layouts  68.7 us (30%)
  blocking collectives  64.2 us (28%)
  waiting for transfers between devices  42.7 us (19%)
  starting transfers between devices  27.7 us (12%)
  other arithmetic  11.4 us (5%)
  matrix products  10.3 us (4%)
    all_to_all x1, waiting for transfers between devices, shards(): received = lax.all_to_all(projections, 'ctx', 2, 1, tiled=True)  42.7 us
    all_to_all x1, blocking collectives, shards(): return lax.all_to_all(back, 'ctx', 0, 1, tiled=True)  36.5 us
    unnamed x51, local copies, waits for them, and re-layouts  34.8 us
    all_to_all x1, starting transfers between devices, shards(): received = lax.all_to_all(projections, 'ctx', 2, 1, tiled=True)  19.2 us
    all_gather x1, blocking collectives, shards(): every = lax.all_gather(flat, 'ch')  14.3 us
    all_gather x1, blocking collectives, shards(): gathered = lax.all_gather(packed, 'ch')  13.4 us
    ppermute x1, starting transfers between devices, shards(): lax.ppermute(ordered[:, span - 2:, :], 'ch', [(i, i + 1) for i in range(n...  8.44 us
    squeeze x32, local copies, waits for them, and re-layouts, shards(): states[source]  8.24 us
  transfers between devices with their start and end apart: 2, of which 1 were waited for; matrix products, arithmetic and copies ran while one was open for 7% of the time, Pallas kernels for 0%

profile of v1, /device:TPU:1, one launch (start us, length us, event | category | flops | bytes accessed | tf_op | source)
XLA Modules:
  0.0 226.8 jit_solution(8212360753389914165)
XLA Ops:
  0.0 10.6 %copy.175 = bf16[3,32,8192]{1,0,2:T(4,128)(2,1)} copy(bf16[3,32,8192]{2,1,0:T(8,128)(2,1)} %param.7) | data formatting | bytes 3145728 | tf_op args[0]
  10.6 13.1 %reshape.607 = bf16[64,2,6144]{2,1,0:T(2,128)(2,1)} reshape(bf16[8192,3,32]{2,1,0:T(4,128)(2,1)} %bitcast.109) | data formatting | bytes 3145728
  23.8 19.2 %all-to-all-start = ((bf16[64,2,6144]{2,1,0:T(2,128)(2,1)}), bf16[64,2,6144]{2,1,0:T(2,128)(2,1)S(1)}, u32[]{:S(2)}, u32[]{:S(2)}) async-start(bf16[64,2,6144]{2,1,0:T(2,128)(2,1)} %reshape.607), calls=%async_computation | async-start | bytes 3145728 | tf_op jit(solution)/shard_map/all_to_all | solution.py:49
  43.0 3.5 %reshape.471 = s32[64,64,4]{2,1,0:T(8,128)} reshape(s32[16384]{0:T(1024)S(1)} %copy-done.2) | data formatting | bytes 131072 | tf_op jit(solution)/shard_map/reshape | solution.py:52
  46.6 1.0 dynamic-slice_bitcast_fusion
  47.5 0.4 copy.170
  48.1 0.2 reduce-window.8
  48.7 14.3 %all-gather = f32[98304]{0:T(1024)S(1)} all-gather(f32[12288]{0:T(1024)S(1)} %pad_maximum_fusion), channel_id=2, replica_groups=mesh['ctx'=64,'ch'=8] {'ch'}, dimensions={0}, use_global_device_ids=true | all-gather | bytes 442368 | tf_op jit(solution)/shard_map/all_gather | solution.py:36
  63.1 0.2 reshape.477
  63.5 0.6 fusion.63
  65.3 0.1 reshape.484
  65.4 0.1 reshape.483
  65.6 0.2 slice_reduce_fusion
  65.8 0.6 pad_add_fusion
  66.4 0.2 slice_reduce_fusion.1
  66.7 0.5 compare_convert_fusion.2
  67.4 0.6 iota_compare_fusion.5
  68.0 0.7 compare_convert_fusion
  68.7 0.7 exponential_multiply_fusion
  69.4 0.2 exponential_select_fusion
  69.6 3.1 %subtract_convert_fusion = (bf16[8,256,256]{1,2,0:T(8,128)(2,1)}, bf16[8,256,256]{1,2,0:T(8,128)(2,1)S(1)}) fusion(pred[256,256]{0,1:T(8,128)(4,1)S(1)} %iota_compare_fusion.4, f32[8,16]{1,0:T(8,128)S(1)} %get-tuple-element.22, f32[8,16]{1,0:T(8,128)S(1)} %get-tuple-element.46, f32[8,16]{1,0:T(8,128)S(1)} %get-tuple-element.45), kind=kOutput, calls=%fused_computation.16 | convolution fusion | flops 103907328 | bytes 2164224 | tf_op jit(solution)/shard_map/gtm,gms->gts/dot_general | solution.py:79
  72.7 1.2 select_convert_fusion
  73.8 42.7 %all-to-all-done = bf16[64,2,6144]{2,1,0:T(2,128)(2,1)S(1)} async-done(((bf16[64,2,6144]{2,1,0:T(2,128)(2,1)}), bf16[64,2,6144]{2,1,0:T(2,128)(2,1)S(1)}, u32[]{:S(2)}, u32[]{:S(2)}) %all-to-all-start) | async-done | bytes 1572896 | tf_op jit(solution)/shard_map/all_to_all | solution.py:49
  116.6 9.4 %reshape.608 = bf16[8192,3,32]{2,1,0:T(4,128)(2,1)} reshape(bf16[64,2,6144]{2,1,0:T(2,128)(2,1)S(1)} %all-to-all-done) | data formatting | bytes 3145728
  126.0 8.0 %copy.216 = bf16[3,32,64,128]{3,2,1,0:T(8,128)(2,1)S(1)} copy(bf16[3,32,64,128]{1,0,3,2:T(4,128)(2,1)} %bitcast.108) | data formatting | bytes 3145728 | tf_op jit(solution)/shard_map/all_to_all | solution.py:49
  134.0 1.4 copy.177
  135.4 1.4 fusion.17
  136.9 0.1 copy.179
  137.0 8.4 %collective-permute-start = (bf16[3,2,128]{2,1,0:T(2,128)(2,1)S(1)}, bf16[3,2,128]{2,1,0:T(2,128)(2,1)S(1)}, u32[]{:S(2)}, u32[]{:S(2)}) collective-permute-start(bf16[3,2,128]{2,1,0:T(2,128)(2,1)S(1)} %slice.195), channel_id=1, source_target_pairs={{0,1},{1,2},{2,3},{3,4},{4,5},{5,6},{6,7},{8,9},{9,10},{10,11},{11... | collective-permute-start | bytes 4616 | tf_op jit(solution)/shard_map/ppermute | solution.py:60
  145.4 0.6 iota_add_fusion.1
  146.1 0.7 dynamic_slice.19
  146.8 0.3 maximum_convert_fusion
  147.1 1.3 fusion.5
  148.4 0.2 fusion.23
  148.6 0.2 copy.180
  148.8 0.1 copy.222
  149.1 1.3 convolution_bitcast_fusion
  150.4 0.2 copy.184
  150.6 1.3 multiply_reduce_fusion
  151.9 0.8 slice.228
  152.8 13.4 %all-gather.2 = f32[8,1,2176]{2,1,0:T(1,128)S(1)} all-gather(f32[1,1,2176]{2,1,0:T(1,128)S(1)} %reshape.492), channel_id=3, replica_groups=mesh['ctx'=64,'ch'=8] {'ch'}, dimensions={0}, use_global_device_ids=true | all-gather | bytes 78336 | tf_op jit(solution)/shard_map/all_gather | solution.py:113
  166.2 0.7 slice_reduce_fusion.16
  166.9 0.3 copy.204
  167.3 1.2 copy.220
  170.1 0.7 mul.508
  170.8 0.7 mul.506
  171.4 0.7 mul.504
  172.1 0.7 mul.502
  172.8 0.7 mul.500
  174.3 0.8 squeeze.68
  175.2 1.4 squeeze.67
  176.6 0.9 copy.186
  177.5 1.4 squeeze.66
  178.9 1.5 copy.185
  180.5 0.9 broadcast_select_fusion
  181.4 2.9 %select_reduce_fusion = f32[8,8,16,256]{3,2,1,0:T(8,128)S(1)} fusion(pred[4,8,256]{2,1,0:T(8,128)(4,1)} %iota_compare_fusion.5, bf16[8,256,256]{1,2,0:T(8,128)(2,1)} %get-tuple-element.47, bf16[8,256,256]{1,2,0:T(8,128)(2,1)} %select_convert_fusion, bf16[4,8,256,8,16]{2,4,1,0,3:T(8,128)(2,1)S(1)} %broadcast_select_fusion), kind=kOutput, calls=%fused_computation.5 | convolution fusion | flops 1088159744 | bytes 5251072 | tf_op jit(solution)/shard_map/gts,dksgc->dktgc/dot_general | solution.py:90
  184.6 1.1 fusion.21
  185.8 1.2 copy.203
  187.0 1.5 fusion.25
  188.5 0.5 fusion.22
  189.1 0.1 copy.206
  189.2 0.3 copy.207
  189.5 36.5 %all_to_all.34 = bf16[64,32,128]{2,1,0:T(8,128)(2,1)S(1)} all-to-all(bf16[64,32,128]{2,1,0:T(8,128)(2,1)S(1)} %copy.207), channel_id=1, replica_groups=mesh['ctx'=64,'ch'=8] {'ctx'}, dimensions={0} | all-to-all | bytes 1048576 | tf_op jit(solution)/shard_map/all_to_all | solution.py:140
  226.0 0.8 copy_bitcast_fusion
  (113 shorter events, 4.2 us)
Async XLA Ops:
  23.7 19.3 %copy-start.2 = (s32[16384]{0:T(1024)S(1)}, s32[16384]{0:T(1024)}, u32[]{:S(2)}) copy-start(s32[16384]{0:T(1024)} %param.8) | copy-start | bytes 196612
  23.7 24.3 %copy-start.19 = (s32[4]{0:T(128)S(1)}, s32[4]{0:T(128)}, u32[]{:S(2)}) copy-start(s32[4]{0:T(128)} %param.9) | copy-start | bytes 52
  23.7 24.5 %copy-start.14 = (f32[64,16]{0,1:T(8,128)S(1)}, f32[64,16]{0,1:T(8,128)}, u32[]{:S(2)}) copy-start(f32[64,16]{0,1:T(8,128)} %param.12) | copy-start | bytes 12292
  23.7 24.7 %copy-start.15 = (f32[64,16]{0,1:T(8,128)S(1)}, f32[64,16]{0,1:T(8,128)}, u32[]{:S(2)}) copy-start(f32[64,16]{0,1:T(8,128)} %param.11) | copy-start | bytes 12292
  23.8 24.8 %copy-start.3 = (f32[3,3,1024]{2,1,0:T(4,128)S(1)}, f32[3,3,1024]{2,1,0:T(4,128)}, u32[]{:S(2)}) copy-start(f32[3,3,1024]{2,1,0:T(4,128)} %param.10) | copy-start | bytes 110596
  23.8 24.9 %copy-start.16 = (f32[1024]{0:T(1024)S(1)}, f32[1024]{0:T(1024)}, u32[]{:S(2)}) copy-start(f32[1024]{0:T(1024)} %param.13) | copy-start | bytes 12292
  23.8 92.8 %all-to-all-start = ((bf16[64,2,6144]{2,1,0:T(2,128)(2,1)}), bf16[64,2,6144]{2,1,0:T(2,128)(2,1)S(1)}, u32[]{:S(2)}, u32[]{:S(2)}) async-start(bf16[64,2,6144]{2,1,0:T(2,128)(2,1)} %reshape.607), calls=%async_computation | async-start | bytes 3145728 | tf_op jit(solution)/shard_map/all_to_all | solution.py:49
  48.1 87.3 %copy-start.9 = (s32[8,256]{1,0:T(8,128)}, s32[8,256]{1,0:T(8,128)S(1)}, u32[]{:S(2)}) copy-start(s32[8,256]{1,0:T(8,128)S(1)} %copy.171) | copy-start | bytes 24580
  67.3 58.7 %copy-start.12 = (f32[8,16]{1,0:T(8,128)}, f32[8,16]{1,0:T(8,128)S(1)}, u32[]{:S(2)}) copy-start(f32[8,16]{1,0:T(8,128)S(1)} %get-tuple-element.45) | copy-start | bytes 1540
  137.0 9.8 %collective-permute-start = (bf16[3,2,128]{2,1,0:T(2,128)(2,1)S(1)}, bf16[3,2,128]{2,1,0:T(2,128)(2,1)S(1)}, u32[]{:S(2)}, u32[]{:S(2)}) collective-permute-start(bf16[3,2,128]{2,1,0:T(2,128)(2,1)S(1)} %slice.195), channel_id=1, source_target_pairs={{0,1},{1,2},{2,3},{3,4},{4,5},{5,6},{6,7},{8,9},{9,10},{10,11},{11... | collective-permute-start | bytes 4616 | tf_op jit(solution)/shard_map/ppermute | solution.py:60
  181.3 3.0 %copy-start.4 = (f32[8,16]{1,0:T(8,128)S(1)}, f32[8,16]{1,0:T(8,128)}, u32[]{:S(2)}) copy-start(f32[8,16]{1,0:T(8,128)} %mul.508) | copy-start | bytes 1540
  181.3 3.0 %copy-start.5 = (f32[8,16]{1,0:T(8,128)S(1)}, f32[8,16]{1,0:T(8,128)}, u32[]{:S(2)}) copy-start(f32[8,16]{1,0:T(8,128)} %mul.506) | copy-start | bytes 1540
  181.3 3.0 %copy-start.6 = (f32[8,16]{1,0:T(8,128)S(1)}, f32[8,16]{1,0:T(8,128)}, u32[]{:S(2)}) copy-start(f32[8,16]{1,0:T(8,128)} %mul.504) | copy-start | bytes 1540
  181.4 3.0 %copy-start.7 = (f32[8,16]{1,0:T(8,128)S(1)}, f32[8,16]{1,0:T(8,128)}, u32[]{:S(2)}) copy-start(f32[8,16]{1,0:T(8,128)} %mul.502) | copy-start | bytes 1540
  181.4 3.0 %copy-start.8 = (f32[8,16]{1,0:T(8,128)S(1)}, f32[8,16]{1,0:T(8,128)}, u32[]{:S(2)}) copy-start(f32[8,16]{1,0:T(8,128)} %mul.500) | copy-start | bytes 1540
  181.4 3.1 %copy-start.1 = (f32[8,8,16]{2,0,1:T(8,128)S(1)}, f32[8,8,16]{2,0,1:T(8,128)}, u32[]{:S(2)}) copy-start(f32[8,8,16]{2,0,1:T(8,128)} %exponential_multiply_fusion) | copy-start | bytes 12292
  181.4 3.1 %copy-start = (f32[1,8,16,16]{2,3,0,1:T(8,128)S(1)}, f32[1,8,16,16]{2,3,0,1:T(8,128)}, u32[]{:S(2)}) copy-start(f32[1,8,16,16]{2,3,0,1:T(8,128)} %copy.185) | copy-start | bytes 24580
  181.4 3.2 %copy-start.11 = (f32[8,256]{1,0:T(8,128)S(1)}, f32[8,256]{1,0:T(8,128)}, u32[]{:S(2)}) copy-start(f32[8,256]{1,0:T(8,128)} %get-tuple-element.43) | copy-start | bytes 24580
  181.4 3.2 %copy-start.13 = (f32[8,16]{1,0:T(8,128)S(1)}, f32[8,16]{1,0:T(8,128)}, u32[]{:S(2)}) copy-start(f32[8,16]{1,0:T(8,128)} %copy-done.12) | copy-start | bytes 1540
  181.4 3.2 %copy-start.17 = (f32[256]{0:T(256)S(1)}, f32[256]{0:T(256)}, u32[]{:S(2)}) copy-start(f32[256]{0:T(256)} %iota_add_fusion.1) | copy-start | bytes 3076
  184.6 2.4 %copy-start.18 = (f32[128]{0:T(128)S(1)}, f32[128]{0:T(128)}, u32[]{:S(2)}) copy-start(f32[128]{0:T(128)} %dynamic_slice.19) | copy-start | bytes 1540
  185.8 2.7 %copy-start.10 = (s32[8,256]{1,0:T(8,128)S(1)}, s32[8,256]{1,0:T(8,128)}, u32[]{:S(2)}) copy-start(s32[8,256]{1,0:T(8,128)} %copy-done.9) | copy-start | bytes 24580

commit v2 on v1

--- a/solution.py
+++ b/solution.py
@@ -46,19 +46,19 @@
     skip = lax.dynamic_slice_in_dim(every[:, o3:].reshape(n_ch * local_channels), here_ctx * width, width, 0)
     coefficient = res * jnp.sqrt(1.0 - jnp.exp(-2.0 * rate))
 
-    received = lax.all_to_all(projections, "ctx", 2, 1, tiled=True)
-    received = received.reshape(feeds, n_ctx, chunks, slot, width)
-    received = jnp.transpose(received, (0, 2, 1, 3, 4)).reshape(feeds, chunks, n_ctx * slot, width)
-    routing = attention_order.reshape(n_ctx, tokens // slot // n_ctx, slot)
-    mine = lax.dynamic_slice_in_dim(routing, here_ch * chunks, chunks, 1)
-    offsets = jnp.transpose(mine, (1, 0, 2)).reshape(chunks, n_ctx * slot)
-    offsets = offsets - (here_ch * chunks + jnp.arange(chunks, dtype=jnp.int32))[:, None] * block
-    placer = (offsets[:, None, :] == jnp.arange(block, dtype=jnp.int32)[None, :, None]).astype(jnp.bfloat16)
-    ordered = jnp.einsum("kwr,pkrc->pkwc", placer, received, preferred_element_type=jnp.float32)
-    ordered = ordered.astype(jnp.bfloat16).reshape(feeds, span, width)
+    sending = jnp.transpose(projections.reshape(feeds, rows_here, n_ctx, width), (2, 1, 0, 3))
+    sending = sending.reshape(n_ctx, rows_here, feeds * width)
+    received = lax.all_to_all(sending, "ctx", 0, 0, tiled=True).reshape(n_ctx * rows_here, feeds * width)
+    routing = attention_order.reshape(n_ctx, tokens // n_ctx)
+    mine = lax.dynamic_slice_in_dim(routing, here_ch * rows_here, rows_here, 1).reshape(n_ctx * rows_here)
+    placer = (
+        (mine - here_ch * span)[None, :] == jnp.arange(span, dtype=jnp.int32)[:, None]
+    ).astype(jnp.bfloat16)
+    ordered = jnp.dot(placer, received, preferred_element_type=jnp.float32).astype(jnp.bfloat16)
 
-    earlier = lax.ppermute(ordered[:, span - 2 :, :], "ch", [(i, i + 1) for i in range(n_ch - 1)])
-    widened = jnp.concatenate([earlier, ordered], axis=1).astype(jnp.float32)
+    earlier = lax.ppermute(ordered[span - 2 :, :], "ch", [(i, i + 1) for i in range(n_ch - 1)])
+    widened = jnp.concatenate([earlier, ordered], axis=0).astype(jnp.float32)
+    widened = jnp.stack([widened[:, p * width : (p + 1) * width] for p in range(feeds)])
     bounds = jnp.cumsum(doc_lengths).astype(jnp.int32)
     span_docs = doc_index(here_ch * span - 2 + jnp.arange(span + 2, dtype=jnp.int32), bounds)
     current = span_docs[2:]
@@ -131,13 +131,9 @@
     combined = filtered.reshape(span, width) + skip[None, :] * gated32
     mixed = (featured[0] * combined).astype(jnp.bfloat16)
 
-    back = jnp.einsum(
-        "kwr,kwc->krc", placer, mixed.reshape(chunks, block, width), preferred_element_type=jnp.float32
-    ).astype(jnp.bfloat16)
-    back = jnp.transpose(back.reshape(chunks, n_ctx, slot, width), (1, 0, 2, 3)).reshape(
-        n_ctx * rows_here, width
-    )
-    return lax.all_to_all(back, "ctx", 0, 1, tiled=True)
+    back = jnp.dot(placer.T, mixed, preferred_element_type=jnp.float32).astype(jnp.bfloat16)
+    returned = lax.all_to_all(back.reshape(n_ctx, rows_here, width), "ctx", 0, 0, tiled=True)
+    return jnp.transpose(returned, (1, 0, 2)).reshape(rows_here, n_ctx * width)
 
 
 def solution(mesh):

time: 229 us -> 242 us (1.057)
  matrix products: 10.3 us -> 19.6 us
  waiting for transfers between devices: 42.7 us -> 47.4 us
  local copies, waits for them, and re-layouts: 68.7 us -> 65.1 us
    unnamed x51 -> x70, local copies, waits for them, and re-layouts: 34.8 us -> 6.67 us
    squeeze x32, local copies, waits for them, and re-layouts: 8.24 us -> 32.5 us  [shards(): states[source]]
    all_to_all x3 -> x0, local copies, waits for them, and re-layouts: 9.13 us -> none  [the longest x1 7.96 us: shards(): received = lax.all_to_all(projections, 'ctx', 2, 1, tiled=True)]
    dot_general x2, matrix products: 1.95 us -> 10.4 us  [the longest x1 5.89 us: shards(): jnp.dot(placer.T, mixed, preferred_element_type=jnp.float32)]
    all_to_all x1, waiting for transfers between devices: 42.7 us -> 47.4 us  [shards(): lax.all_to_all(sending, 'ctx', 0, 0, tiled=True)]
    mul x8, local copies, waits for them, and re-layouts: 3.61 us -> 8.04 us  [shards(): factors[source] * entering + states[source]]
    reshape x2 -> x5, local copies, waits for them, and re-layouts: 3.63 us -> 7.3 us  [the longest x1 2.55 us: shards(): sending = sending.reshape(n_ctx, rows_here, feeds * width)]
    transpose x3 -> x0, local copies, waits for them, and re-layouts: 2.84 us -> none  [the longest x1 1.43 us: shards(): jnp.transpose(received, (0, 2, 1, 3, 4))]
  transfers between devices with their start and end apart: 2 -> 2, of which waited for: 1 -> 1; matrix products, arithmetic and copies ran while one was open for 7% -> 5% of each run, Pallas kernels for 0% -> 0%
where the time goes in v2:
time: 242 us; the launch traced here: 239 us
  local copies, waits for them, and re-layouts  65.1 us (27%)
  blocking collectives  64.2 us (27%)
  waiting for transfers between devices  47.4 us (20%)
  starting transfers between devices  27.5 us (11%)
  matrix products  19.6 us (8%)
  other arithmetic  12.9 us (5%)
    all_to_all x1, waiting for transfers between devices, shards(): lax.all_to_all(sending, 'ctx', 0, 0, tiled=True)  47.4 us
    all_to_all x1, blocking collectives, shards(): lax.all_to_all(back.reshape(n_ctx, rows_here, width), 'ctx', 0, 0, tiled=...  36.5 us
    squeeze x32, local copies, waits for them, and re-layouts, shards(): states[source]  32.5 us
    all_to_all x1, starting transfers between devices, shards(): lax.all_to_all(sending, 'ctx', 0, 0, tiled=True)  19.1 us
    all_gather x1, blocking collectives, shards(): every = lax.all_gather(flat, 'ch')  14.3 us
    all_gather x1, blocking collectives, shards(): gathered = lax.all_gather(packed, 'ch')  13.5 us
    ppermute x1, starting transfers between devices, shards(): lax.ppermute(ordered[span - 2:, :], 'ch', [(i, i + 1) for i in range(n_ch...  8.45 us
    mul x8, local copies, waits for them, and re-layouts, shards(): factors[source] * entering + states[source]  8.04 us
  transfers between devices with their start and end apart: 2, of which 1 were waited for; matrix products, arithmetic and copies ran while one was open for 5% of the time, Pallas kernels for 0%

profile of v2, /device:TPU:1, one launch (start us, length us, event | category | flops | bytes accessed | tf_op | source)
XLA Modules:
  0.0 238.8 jit_solution(15634600842636483487)
XLA Ops:
  0.0 1.8 copy.150
  1.8 1.4 copy.160
  3.3 2.6 %reshape.448 = bf16[64,32,384]{2,1,0:T(8,128)(2,1)} reshape(bf16[64,32,3,128]{3,2,1,0:T(4,128)(2,1)S(1)} %bitcast.103) | data formatting | bytes 3145728 | tf_op jit(solution)/shard_map/reshape | solution.py:50
  5.8 19.1 %all-to-all-start = ((bf16[64,32,384]{2,1,0:T(8,128)(2,1)}), bf16[64,32,384]{2,1,0:T(8,128)(2,1)S(1)}, u32[]{:S(2)}, u32[]{:S(2)}) async-start(bf16[64,32,384]{2,1,0:T(8,128)(2,1)} %reshape.448), calls=%async_computation | async-start | bytes 3145728 | tf_op jit(solution)/shard_map/all_to_all | solution.py:51
  25.7 14.3 %all-gather = f32[98304]{0:T(1024)S(1)} all-gather(f32[12288]{0:T(1024)S(1)} %pad_maximum_fusion.1), channel_id=2, replica_groups=mesh['ctx'=64,'ch'=8] {'ch'}, dimensions={0}, use_global_device_ids=true | all-gather | bytes 442368 | tf_op jit(solution)/shard_map/all_gather | solution.py:36
  42.9 0.7 pad_add_fusion
  45.3 0.7 compare_convert_fusion
  45.9 0.7 exponential_multiply_fusion
  46.8 3.0 %subtract_convert_fusion = (bf16[8,256,256]{1,2,0:T(8,128)(2,1)}, bf16[8,256,256]{1,2,0:T(8,128)(2,1)S(1)}) fusion(pred[256,256]{0,1:T(8,128)(4,1)S(1)} %iota_compare_fusion.7, f32[8,16]{1,0:T(8,128)S(1)} %get-tuple-element.22, f32[8,16]{1,0:T(8,128)S(1)} %get-tuple-element.47, f32[8,16]{1,0:T(8,128)S(1)} %get-tuple-element.46), kind=kOutput, calls=%fused_computation.25 | convolution fusion | flops 103907328 | bytes 2164224 | tf_op jit(solution)/shard_map/gtm,gms->gts/dot_general | solution.py:79
  49.9 1.2 select_convert_fusion
  51.1 47.4 %all-to-all-done = bf16[64,32,384]{2,1,0:T(8,128)(2,1)S(1)} async-done(((bf16[64,32,384]{2,1,0:T(8,128)(2,1)}), bf16[64,32,384]{2,1,0:T(8,128)(2,1)S(1)}, u32[]{:S(2)}, u32[]{:S(2)}) %all-to-all-start) | async-done | bytes 1572896 | tf_op jit(solution)/shard_map/all_to_all | solution.py:51
  98.5 4.5 %fusion.12 = bf16[2048,384]{1,0:T(8,128)(2,1)S(1)} fusion(bf16[2048,384]{1,0:T(8,128)(2,1)S(1)} %bitcast.111, s32[2048]{0:T(1024)S(1)} %sub.50), kind=kOutput, calls=%fused_computation.19 | convolution fusion | flops 3226206208 | bytes 3153920 | tf_op jit(solution)/shard_map/dot_general | solution.py:57
  103.0 8.5 %collective-permute-start = (bf16[2,384]{1,0:T(2,128)(2,1)S(1)}, bf16[2,384]{1,0:T(2,128)(2,1)S(1)}, u32[]{:S(2)}, u32[]{:S(2)}) collective-permute-start(bf16[2,384]{1,0:T(2,128)(2,1)S(1)} %slice.207), channel_id=1, source_target_pairs={{0,1},{1,2},{2,3},{3,4},{4,5},{5,6},{6,7},{8,9},{9,10},{10,11},{11... | collective-permute-start | bytes 4616 | tf_op jit(solution)/shard_map/ppermute | solution.py:59
  112.1 0.6 dynamic_slice.19
  113.5 1.3 fusion.9
  114.8 0.9 fusion.18
  115.7 2.0 copy.117
  117.7 1.1 copy.151
  118.9 0.9 copy.118
  119.9 2.1 convolution_bitcast_fusion
  122.0 2.1 copy.121
  124.0 2.2 multiply_reduce_fusion
  126.2 0.8 slice.243
  127.2 13.5 %all-gather.2 = f32[8,1,2176]{2,1,0:T(1,128)S(1)} all-gather(f32[1,1,2176]{2,1,0:T(1,128)S(1)} %reshape.462), channel_id=3, replica_groups=mesh['ctx'=64,'ch'=8] {'ch'}, dimensions={0}, use_global_device_ids=true | all-gather | bytes 78336 | tf_op jit(solution)/shard_map/all_gather | solution.py:113
  140.6 1.3 slice_reduce_fusion.16
  142.6 2.0 copy.148
  145.2 0.8 squeeze.77
  146.1 1.4 squeeze.76
  147.5 0.9 copy.132
  148.4 1.4 squeeze.75
  149.8 1.6 copy.131
  151.4 0.7 squeeze.74
  152.1 1.5 copy.130
  153.6 0.8 mul.503
  154.4 0.7 mul.498
  155.2 1.3 mul.496
  156.5 1.3 mul.494
  157.8 1.3 mul.492
  159.1 1.3 mul.490
  160.4 1.3 mul.488
  161.7 1.4 squeeze.73
  163.0 1.5 copy.129
  164.6 1.4 squeeze.72
  166.0 1.5 copy.128
  167.5 1.4 squeeze.71
  168.9 1.5 copy.127
  170.4 1.4 squeeze.70
  171.8 1.5 copy.126
  173.4 1.4 squeeze.69
  174.8 1.5 copy.125
  176.3 1.4 squeeze.68
  177.7 1.5 copy.124
  179.2 1.4 squeeze.67
  180.6 1.5 copy.123
  182.2 1.4 squeeze.66
  183.6 1.5 copy.122
  185.1 1.2 broadcast_select_fusion
  186.5 3.0 %select_reduce_fusion = f32[8,8,16,256]{3,2,1,0:T(8,128)S(1)} fusion(pred[4,8,256]{2,1,0:T(8,128)(4,1)} %iota_compare_fusion.8, bf16[8,256,256]{1,2,0:T(8,128)(2,1)} %get-tuple-element.48, bf16[8,256,256]{1,2,0:T(8,128)(2,1)} %select_convert_fusion, bf16[4,8,256,8,16]{2,4,1,0,3:T(8,128)(2,1)S(1)} %broadcast_select_fusion), kind=kOutput, calls=%fused_computation.10 | convolution fusion | flops 1088159744 | bytes 5251072 | tf_op jit(solution)/shard_map/gts,dksgc->dktgc/dot_general | solution.py:90
  189.9 1.1 fusion.17
  191.6 1.4 copy.152
  193.0 2.5 %copy.140 = f32[2048,128]{1,0:T(8,128)} copy(f32[2048,128]{0,1:T(8,128)} %bitcast.108) | data formatting | bytes 2097152 | tf_op jit(solution)/shard_map/reshape | solution.py:131
  195.6 5.9 %fusion.13 = bf16[2048,128]{1,0:T(8,128)(2,1)S(1)} fusion(s32[2048]{0:T(1024)S(1)} %copy-done.25, f32[3,2048,128]{2,1,0:T(8,128)S(1)} %fusion.9, f32[2048,128]{1,0:T(8,128)} %copy.140, bf16[1,2048,128]{2,1,0:T(8,128)(2,1)} %fusion.18, f32[128]{0:T(128)S(1)} %copy-done.29), kind=kOutput, calls=%fused_computation.20 | convolution fusion | flops 1079508992 | bytes 3154432 | tf_op jit(solution)/shard_map/dot_general | solution.py:134
  201.5 36.5 %all_to_all.10 = bf16[64,32,128]{2,1,0:T(8,128)(2,1)S(1)} all-to-all(bf16[64,32,128]{2,1,0:T(8,128)(2,1)S(1)} %bitcast.113), channel_id=1, replica_groups=mesh['ctx'=64,'ch'=8] {'ctx'}, dimensions={0} | all-to-all | bytes 1048576 | tf_op jit(solution)/shard_map/all_to_all | solution.py:135
  238.0 0.8 copy_bitcast_fusion.1
  (126 shorter events, 8.0 us)
Async XLA Ops:
  3.2 21.7 %copy-start.12 = (s32[16384]{0:T(1024)S(1)}, s32[16384]{0:T(1024)}, u32[]{:S(2)}) copy-start(s32[16384]{0:T(1024)} %param.8) | copy-start | bytes 196612
  3.2 21.9 %copy-start.28 = (s32[4]{0:T(128)S(1)}, s32[4]{0:T(128)}, u32[]{:S(2)}) copy-start(s32[4]{0:T(128)} %param.9) | copy-start | bytes 52
  3.2 22.1 %copy-start.22 = (f32[64,16]{0,1:T(8,128)S(1)}, f32[64,16]{0,1:T(8,128)}, u32[]{:S(2)}) copy-start(f32[64,16]{0,1:T(8,128)} %param.12) | copy-start | bytes 12292
  3.2 22.2 %copy-start.23 = (f32[64,16]{0,1:T(8,128)S(1)}, f32[64,16]{0,1:T(8,128)}, u32[]{:S(2)}) copy-start(f32[64,16]{0,1:T(8,128)} %param.11) | copy-start | bytes 12292
  3.2 22.4 %copy-start.13 = (f32[3,3,1024]{2,1,0:T(4,128)S(1)}, f32[3,3,1024]{2,1,0:T(4,128)}, u32[]{:S(2)}) copy-start(f32[3,3,1024]{2,1,0:T(4,128)} %param.10) | copy-start | bytes 110596
  3.3 22.4 %copy-start.26 = (f32[1024]{0:T(1024)S(1)}, f32[1024]{0:T(1024)}, u32[]{:S(2)}) copy-start(f32[1024]{0:T(1024)} %param.13) | copy-start | bytes 12292
  5.8 92.7 %all-to-all-start = ((bf16[64,32,384]{2,1,0:T(8,128)(2,1)}), bf16[64,32,384]{2,1,0:T(8,128)(2,1)S(1)}, u32[]{:S(2)}, u32[]{:S(2)}) async-start(bf16[64,32,384]{2,1,0:T(8,128)(2,1)} %reshape.448), calls=%async_computation | async-start | bytes 3145728 | tf_op jit(solution)/shard_map/all_to_all | solution.py:51
  25.1 73.3 %copy-start.24 = (s32[2048]{0:T(1024)}, s32[2048]{0:T(1024)S(1)}, u32[]{:S(2)}) copy-start(s32[2048]{0:T(1024)S(1)} %sub.50) | copy-start | bytes 24580
  44.6 58.4 %copy-start.20 = (f32[8,16]{1,0:T(8,128)}, f32[8,16]{1,0:T(8,128)S(1)}, u32[]{:S(2)}) copy-start(f32[8,16]{1,0:T(8,128)S(1)} %get-tuple-element.46) | copy-start | bytes 1540
  103.0 9.7 %collective-permute-start = (bf16[2,384]{1,0:T(2,128)(2,1)S(1)}, bf16[2,384]{1,0:T(2,128)(2,1)S(1)}, u32[]{:S(2)}, u32[]{:S(2)}) collective-permute-start(bf16[2,384]{1,0:T(2,128)(2,1)S(1)} %slice.207), channel_id=1, source_target_pairs={{0,1},{1,2},{2,3},{3,4},{4,5},{5,6},{6,7},{8,9},{9,10},{10,11},{11... | collective-permute-start | bytes 4616 | tf_op jit(solution)/shard_map/ppermute | solution.py:59
  186.3 3.2 %copy-start.1 = (f32[8,16,16]{1,2,0:T(8,128)S(1)}, f32[8,16,16]{1,2,0:T(8,128)}, u32[]{:S(2)}) copy-start(f32[8,16,16]{1,2,0:T(8,128)} %copy.131) | copy-start | bytes 24580
  186.3 3.2 %copy-start.3 = (f32[8,16,16]{1,2,0:T(8,128)S(1)}, f32[8,16,16]{1,2,0:T(8,128)}, u32[]{:S(2)}) copy-start(f32[8,16,16]{1,2,0:T(8,128)} %copy.130) | copy-start | bytes 24580
  186.3 3.2 %copy-start.14 = (f32[8,16]{1,0:T(8,128)S(1)}, f32[8,16]{1,0:T(8,128)}, u32[]{:S(2)}) copy-start(f32[8,16]{1,0:T(8,128)} %mul.496) | copy-start | bytes 1540
  186.3 3.2 %copy-start.15 = (f32[8,16]{1,0:T(8,128)S(1)}, f32[8,16]{1,0:T(8,128)}, u32[]{:S(2)}) copy-start(f32[8,16]{1,0:T(8,128)} %mul.494) | copy-start | bytes 1540
  186.4 3.2 %copy-start.16 = (f32[8,16]{1,0:T(8,128)S(1)}, f32[8,16]{1,0:T(8,128)}, u32[]{:S(2)}) copy-start(f32[8,16]{1,0:T(8,128)} %mul.492) | copy-start | bytes 1540
  186.4 3.2 %copy-start.17 = (f32[8,16]{1,0:T(8,128)S(1)}, f32[8,16]{1,0:T(8,128)}, u32[]{:S(2)}) copy-start(f32[8,16]{1,0:T(8,128)} %mul.490) | copy-start | bytes 1540
  186.4 3.2 %copy-start.18 = (f32[8,16]{1,0:T(8,128)S(1)}, f32[8,16]{1,0:T(8,128)}, u32[]{:S(2)}) copy-start(f32[8,16]{1,0:T(8,128)} %mul.488) | copy-start | bytes 1540
  186.4 3.3 %copy-start = (f32[7,8,16,16]{2,3,0,1:T(8,128)S(1)}, f32[7,8,16,16]{2,3,0,1:T(8,128)}, u32[]{:S(2)}) copy-start(f32[7,8,16,16]{2,3,0,1:T(8,128)} %copy.148) | copy-start | bytes 172036
  186.4 3.3 %copy-start.11 = (f32[8,8,16]{2,0,1:T(8,128)S(1)}, f32[8,8,16]{2,0,1:T(8,128)}, u32[]{:S(2)}) copy-start(f32[8,8,16]{2,0,1:T(8,128)} %exponential_multiply_fusion) | copy-start | bytes 12292
  186.4 3.3 %copy-start.2 = (f32[1,8,16,16]{2,3,0,1:T(8,128)S(1)}, f32[1,8,16,16]{2,3,0,1:T(8,128)}, u32[]{:S(2)}) copy-start(f32[1,8,16,16]{2,3,0,1:T(8,128)} %copy.129) | copy-start | bytes 24580
  186.4 3.3 %copy-start.4 = (f32[1,8,16,16]{2,3,0,1:T(8,128)S(1)}, f32[1,8,16,16]{2,3,0,1:T(8,128)}, u32[]{:S(2)}) copy-start(f32[1,8,16,16]{2,3,0,1:T(8,128)} %copy.128) | copy-start | bytes 24580
  186.4 3.3 %copy-start.5 = (f32[1,8,16,16]{2,3,0,1:T(8,128)S(1)}, f32[1,8,16,16]{2,3,0,1:T(8,128)}, u32[]{:S(2)}) copy-start(f32[1,8,16,16]{2,3,0,1:T(8,128)} %copy.127) | copy-start | bytes 24580
  186.4 3.3 %copy-start.6 = (f32[1,8,16,16]{2,3,0,1:T(8,128)S(1)}, f32[1,8,16,16]{2,3,0,1:T(8,128)}, u32[]{:S(2)}) copy-start(f32[1,8,16,16]{2,3,0,1:T(8,128)} %copy.126) | copy-start | bytes 24580
  186.4 3.3 %copy-start.7 = (f32[1,8,16,16]{2,3,0,1:T(8,128)S(1)}, f32[1,8,16,16]{2,3,0,1:T(8,128)}, u32[]{:S(2)}) copy-start(f32[1,8,16,16]{2,3,0,1:T(8,128)} %copy.125) | copy-start | bytes 24580
  186.5 3.3 %copy-start.8 = (f32[1,8,16,16]{2,3,0,1:T(8,128)S(1)}, f32[1,8,16,16]{2,3,0,1:T(8,128)}, u32[]{:S(2)}) copy-start(f32[1,8,16,16]{2,3,0,1:T(8,128)} %copy.124) | copy-start | bytes 24580
  186.5 3.3 %copy-start.9 = (f32[1,8,16,16]{2,3,0,1:T(8,128)S(1)}, f32[1,8,16,16]{2,3,0,1:T(8,128)}, u32[]{:S(2)}) copy-start(f32[1,8,16,16]{2,3,0,1:T(8,128)} %copy.123) | copy-start | bytes 24580
  186.5 3.3 %copy-start.10 = (f32[1,8,16,16]{2,3,0,1:T(8,128)S(1)}, f32[1,8,16,16]{2,3,0,1:T(8,128)}, u32[]{:S(2)}) copy-start(f32[1,8,16,16]{2,3,0,1:T(8,128)} %copy.122) | copy-start | bytes 24580
  186.5 3.4 %copy-start.19 = (f32[8,256]{1,0:T(8,128)S(1)}, f32[8,256]{1,0:T(8,128)}, u32[]{:S(2)}) copy-start(f32[8,256]{1,0:T(8,128)} %get-tuple-element.44) | copy-start | bytes 24580
  186.5 3.4 %copy-start.21 = (f32[8,16]{1,0:T(8,128)S(1)}, f32[8,16]{1,0:T(8,128)}, u32[]{:S(2)}) copy-start(f32[8,16]{1,0:T(8,128)} %copy-done.20) | copy-start | bytes 1540
  186.5 3.4 %copy-start.27 = (f32[256]{0:T(256)S(1)}, f32[256]{0:T(256)}, u32[]{:S(2)}) copy-start(f32[256]{0:T(256)} %iota_add_fusion.1) | copy-start | bytes 3076
  191.0 4.6 %copy-start.25 = (s32[2048]{0:T(1024)S(1)}, s32[2048]{0:T(1024)}, u32[]{:S(2)}) copy-start(s32[2048]{0:T(1024)} %copy-done.24) | copy-start | bytes 24580
  191.0 4.6 %copy-start.29 = (f32[128]{0:T(128)S(1)}, f32[128]{0:T(128)}, u32[]{:S(2)}) copy-start(f32[128]{0:T(128)} %dynamic_slice.19) | copy-start | bytes 1540

commit v3 on v2

--- a/solution.py
+++ b/solution.py
@@ -108,14 +108,15 @@
     local_state = jnp.sum(carry_weight[:, :, :, :, None] * chunk_state[None], axis=1)
 
     previous_doc = span_docs[1]
-    span_factor = jnp.exp(-rate * float(span)) * (previous_doc == current[span - 1]).astype(jnp.float32)
-    packed = jnp.concatenate([span_factor.reshape(-1), local_state[chunks - 1].reshape(-1)])
-    gathered = lax.all_gather(packed, "ch")
-    factors = gathered[:, : groups * modes].reshape(n_ch, groups, modes, 1)
-    states = gathered[:, groups * modes :].reshape(n_ch, groups, modes, group_width)
-    entering = jnp.zeros((groups, modes, group_width), jnp.float32)
-    for source in range(n_ch):
-        entering = jnp.where(source < here_ch, factors[source] * entering + states[source], entering)
+    gathered = lax.all_gather(local_state[chunks - 1], "ch")
+    span_ids = jnp.arange(n_ch, dtype=jnp.int32)
+    span_end_doc = doc_index((span_ids + 1) * span - 1, bounds)
+    distance = jnp.maximum(here_ch - 1 - span_ids, 0).astype(jnp.float32)
+    counted = (span_ids < here_ch) & (span_end_doc == previous_doc)
+    span_weight = jnp.where(
+        counted[:, None, None], jnp.exp(-rate[None] * (float(span) * distance)[:, None, None]), 0.0
+    )
+    entering = jnp.sum(span_weight[..., None] * gathered, axis=0)
 
     reach = jnp.exp(-rate[None] * (block * (chunk_ids + 1.0))[:, None, None])
     joined = (previous_doc == ends_doc).astype(jnp.float32)[:, None, None, None]

time: 242 us -> 198 us (0.82)
  local copies, waits for them, and re-layouts: 65.1 us -> 23 us
  other arithmetic: 12.9 us -> 10.1 us
  waiting for transfers between devices: 47.4 us -> 50 us
    squeeze x32 -> x0, local copies, waits for them, and re-layouts: 32.5 us -> none  [shards(): states[source]]
    mul x9 -> x0, local copies, waits for them, and re-layouts: 8.05 us -> none  [the longest x8 8.04 us: shards(): factors[source] * entering + states[source]]
    unnamed x70 -> x24, local copies, waits for them, and re-layouts: 6.67 us -> 6.52 us
  transfers between devices with their start and end apart: 2 -> 2, of which waited for: 1 -> 2; matrix products, arithmetic and copies ran while one was open for 5% -> 5% of each run, Pallas kernels for 0% -> 0%
where the time goes in v3:
time: 198 us; the launch traced here: 196 us
  blocking collectives  65.5 us (33%)
  waiting for transfers between devices  50 us (25%)
  starting transfers between devices  27.6 us (14%)
  local copies, waits for them, and re-layouts  23 us (12%)
  matrix products  19.5 us (10%)
  other arithmetic  10.1 us (5%)
    all_to_all x1, waiting for transfers between devices, shards(): lax.all_to_all(sending, 'ctx', 0, 0, tiled=True)  49.6 us
    all_to_all x1, blocking collectives, shards(): lax.all_to_all(back.reshape(n_ctx, rows_here, width), 'ctx', 0, 0, tiled=...  36.5 us
    all_to_all x1, starting transfers between devices, shards(): lax.all_to_all(sending, 'ctx', 0, 0, tiled=True)  19.1 us
    all_gather x1, blocking collectives, shards(): gathered = lax.all_gather(local_state[chunks - 1], 'ch')  14.5 us
    all_gather x1, blocking collectives, shards(): every = lax.all_gather(flat, 'ch')  14.5 us
    ppermute x1, starting transfers between devices, shards(): lax.ppermute(ordered[span - 2:, :], 'ch', [(i, i + 1) for i in range(n_ch...  8.48 us
    unnamed x24, local copies, waits for them, and re-layouts  6.52 us
    dot_general x1, matrix products, shards(): jnp.dot(placer.T, mixed, preferred_element_type=jnp.float32)  5.9 us
  transfers between devices with their start and end apart: 2, of which 2 were waited for; matrix products, arithmetic and copies ran while one was open for 5% of the time, Pallas kernels for 0%

profile of v3, /device:TPU:1, one launch (start us, length us, event | category | flops | bytes accessed | tf_op | source)
XLA Modules:
  0.0 196.1 jit_solution(17237811365448935584)
XLA Ops:
  0.0 1.8 copy.92
  1.8 1.4 copy.104
  3.3 2.6 %reshape.299 = bf16[64,32,384]{2,1,0:T(8,128)(2,1)} reshape(bf16[64,32,3,128]{3,2,1,0:T(4,128)(2,1)S(1)} %bitcast.87) | data formatting | bytes 3145728 | tf_op jit(solution)/shard_map/reshape | solution.py:50
  5.8 19.1 %all-to-all-start = ((bf16[64,32,384]{2,1,0:T(8,128)(2,1)}), bf16[64,32,384]{2,1,0:T(8,128)(2,1)S(1)}, u32[]{:S(2)}, u32[]{:S(2)}) async-start(bf16[64,32,384]{2,1,0:T(8,128)(2,1)} %reshape.299), calls=%async_computation | async-start | bytes 3145728 | tf_op jit(solution)/shard_map/all_to_all | solution.py:51
  24.9 0.2 reduce-window.8
  25.1 0.1 convert_reduce_fusion
  25.2 0.1 slice.111
  25.3 0.6 slice.119
  25.9 0.1 dynamic-slice_subtract_fusion
  26.0 0.1 sub.68
  26.1 0.1 copy.67
  26.2 0.1 reshape.295
  26.2 0.1 copy.66
  26.3 0.1 reshape.294
  26.5 14.5 %all-gather = f32[98304]{0:T(1024)S(1)} all-gather(f32[12288]{0:T(1024)S(1)} %pad_maximum_fusion.1), channel_id=2, replica_groups=mesh['ctx'=64,'ch'=8] {'ch'}, dimensions={0}, use_global_device_ids=true | all-gather | bytes 442368 | tf_op jit(solution)/shard_map/all_gather | solution.py:36
  40.9 0.1 reshape.310
  41.0 0.2 reshape.296
  41.3 0.2 copy.68
  41.5 0.2 reshape.297
  41.7 0.1 reshape.303
  41.8 0.1 reshape.304
  42.0 0.2 slice_reduce_fusion
  42.2 0.7 pad_add_fusion
  43.0 0.1 constant_dynamic-slice_fusion.1
  43.0 0.2 slice_reduce_fusion.1
  43.2 0.1 convert_reduce_fusion.1
  43.4 0.1 fusion.56
  43.5 0.7 compare_convert_fusion.2
  44.2 0.1 fusion.54
  44.3 0.1 exponential_multiply_fusion
  44.4 0.2 exponential_select_fusion
  44.6 3.0 %subtract_convert_fusion = (bf16[8,256,256]{1,2,0:T(8,128)(2,1)}, bf16[8,256,256]{1,2,0:T(8,128)(2,1)S(1)}) fusion(pred[256,256]{0,1:T(8,128)(4,1)S(1)} %iota_compare_fusion.7, f32[8,16]{1,0:T(8,128)S(1)} %get-tuple-element.6, f32[8,16]{1,0:T(8,128)S(1)} %neg.12, f32[8,16]{1,0:T(8,128)S(1)} %get-tuple-element.5), kind=kOutput, calls=%fused_computation.25 | convolution fusion | flops 103907328 | bytes 2164224 | tf_op jit(solution)/shard_map/gtm,gms->gts/dot_general | solution.py:79
  47.6 1.2 select_convert_fusion
  48.8 49.6 %all-to-all-done = bf16[64,32,384]{2,1,0:T(8,128)(2,1)S(1)} async-done(((bf16[64,32,384]{2,1,0:T(8,128)(2,1)}), bf16[64,32,384]{2,1,0:T(8,128)(2,1)S(1)}, u32[]{:S(2)}, u32[]{:S(2)}) %all-to-all-start) | async-done | bytes 1572896 | tf_op jit(solution)/shard_map/all_to_all | solution.py:51
  98.5 4.5 %fusion.12 = bf16[2048,384]{1,0:T(8,128)(2,1)S(1)} fusion(bf16[2048,384]{1,0:T(8,128)(2,1)S(1)} %bitcast.95, s32[2048]{0:T(1024)S(1)} %sub.68), kind=kOutput, calls=%fused_computation.19 | convolution fusion | flops 3226206208 | bytes 3153920 | tf_op jit(solution)/shard_map/dot_general | solution.py:57
  103.0 8.5 %collective-permute-start = (bf16[2,384]{1,0:T(2,128)(2,1)S(1)}, bf16[2,384]{1,0:T(2,128)(2,1)S(1)}, u32[]{:S(2)}, u32[]{:S(2)}) collective-permute-start(bf16[2,384]{1,0:T(2,128)(2,1)S(1)} %slice.104), channel_id=1, source_target_pairs={{0,1},{1,2},{2,3},{3,4},{4,5},{5,6},{6,7},{8,9},{9,10},{10,11},{11... | collective-permute-start | bytes 4616 | tf_op jit(solution)/shard_map/ppermute | solution.py:59
  111.5 0.1 dynamic_slice.19
  111.6 0.4 collective-permute-done
  112.0 0.3 maximum_convert_fusion
  112.3 0.2 slice_bitcast_fusion.2
  112.5 0.2 pad_maximum_fusion
  112.7 1.3 fusion.9
  114.0 0.9 fusion.18
  114.9 2.0 %copy.70 = bf16[1,2048,128]{1,2,0:T(8,128)(2,1)} copy(bf16[1,2048,128]{2,1,0:T(8,128)(2,1)} %fusion.18) | data formatting | bytes 1048576 | tf_op jit(solution)/shard_map/convert_element_type | solution.py:72
  116.9 1.1 copy.93
  118.1 0.9 copy.71
  119.0 0.1 convert_multiply_fusion.1
  119.1 2.1 %convolution_bitcast_fusion = f32[8,8,16,16]{2,3,0,1:T(8,128)} fusion(f32[8,256,8,16]{1,0,3,2:T(8,128)S(1)} %convert_multiply_fusion.1, f32[256]{0:T(256)S(1)} %iota_subtract_fusion, f32[8,16]{1,0:T(8,128)S(1)} %neg.12), kind=kOutput, calls=%fused_computation.32 | convolution fusion | flops 50364416 | bytes 1115648 | tf_op jit(solution)/shard_map/gms,ksgc->kgmc/dot_general | solution.py:97
  121.2 2.1 %copy.75 = f32[8,8,16,16]{3,2,1,0:T(8,128)} copy(f32[8,8,16,16]{2,3,0,1:T(8,128)} %convolution_bitcast_fusion) | data formatting | bytes 131072 | tf_op jit(solution)/shard_map/gms,ksgc->kgmc/transpose | solution.py:97
  123.2 2.2 %multiply_reduce_fusion = f32[8,8,16,16]{3,2,1,0:T(8,128)S(1)} fusion(f32[8,8,16,16]{3,2,1,0:T(8,128)} %copy.75, f32[8,8,8,16]{3,2,1,0:T(8,128)S(1)} %exponential_select_fusion), kind=kLoop, calls=%fused_computation.9 | loop fusion | flops 245760 | bytes 163840 | tf_op jit(solution)/shard_map/reduce_sum | solution.py:108
  125.5 0.8 slice.123
  126.3 2.0 %copy.90 = f32[7,8,16,16]{2,3,0,1:T(8,128)} copy(f32[7,8,16,16]{3,2,1,0:T(8,128)} %slice.123) | data formatting | bytes 114688
  128.3 14.5 %all_gather.11 = f32[8,8,16,16]{3,2,1,0:T(8,128)S(1)} all-gather(f32[1,8,16,16]{3,2,1,0:T(8,128)S(1)} %slice.121), channel_id=1, replica_groups=mesh['ctx'=64,'ch'=8] {'ch'}, dimensions={0}, use_global_device_ids=true | all-gather | bytes 73728 | tf_op jit(solution)/shard_map/all_gather | solution.py:111
  142.8 0.2 multiply_reduce_fusion.1
  143.0 0.1 copy.76
  143.1 1.2 broadcast_select_fusion
  144.3 2.9 %select_reduce_fusion = f32[8,8,16,256]{3,2,1,0:T(8,128)S(1)} fusion(pred[4,8,256]{2,1,0:T(8,128)(4,1)S(1)} %iota_compare_fusion.8, bf16[8,256,256]{1,2,0:T(8,128)(2,1)} %get-tuple-element.22, bf16[8,256,256]{1,2,0:T(8,128)(2,1)} %select_convert_fusion, bf16[4,8,256,8,16]{2,4,1,0,3:T(8,128)(2,1)S(1)} %broadcast_select_fusion), kind=kOutput, calls=%fused_computation.10 | convolution fusion | flops 1088159744 | bytes 5251072 | tf_op jit(solution)/shard_map/gts,dksgc->dktgc/dot_general | solution.py:90
  147.3 1.1 fusion.17
  148.4 0.6 copy.79
  149.0 1.3 copy.94
  150.3 2.6 %copy.80 = f32[2048,128]{1,0:T(8,128)} copy(f32[2048,128]{0,1:T(8,128)} %bitcast.92) | data formatting | bytes 2097152 | tf_op jit(solution)/shard_map/reshape | solution.py:132
  152.9 5.9 %fusion.13 = bf16[2048,128]{1,0:T(8,128)(2,1)S(1)} fusion(s32[2048]{0:T(1024)S(1)} %sub.68, f32[3,2048,128]{2,1,0:T(8,128)S(1)} %fusion.9, f32[2048,128]{1,0:T(8,128)} %copy.80, bf16[1,2048,128]{2,1,0:T(8,128)(2,1)} %fusion.18, f32[128]{0:T(128)S(1)} %dynamic_slice.19), kind=kOutput, calls=%fused_computation.20 | convolution fusion | flops 1079508992 | bytes 3154432 | tf_op jit(solution)/shard_map/dot_general | solution.py:135
  158.8 36.5 %all_to_all.10 = bf16[64,32,128]{2,1,0:T(8,128)(2,1)S(1)} all-to-all(bf16[64,32,128]{2,1,0:T(8,128)(2,1)S(1)} %bitcast.98), channel_id=1, replica_groups=mesh['ctx'=64,'ch'=8] {'ctx'}, dimensions={0} | all-to-all | bytes 1048576 | tf_op jit(solution)/shard_map/all_to_all | solution.py:136
  195.3 0.8 copy_bitcast_fusion.1
  (39 shorter events, 0.4 us)
Async XLA Ops:
  3.2 21.7 %copy-start.6 = (s32[4]{0:T(128)S(1)}, s32[4]{0:T(128)}, u32[]{:S(2)}) copy-start(s32[4]{0:T(128)} %param.9) | copy-start | bytes 52
  3.2 22.7 %copy-start.1 = (s32[16384]{0:T(1024)S(1)}, s32[16384]{0:T(1024)}, u32[]{:S(2)}) copy-start(s32[16384]{0:T(1024)} %param.8) | copy-start | bytes 196612
  3.2 22.9 %copy-start.3 = (f32[64,16]{0,1:T(8,128)S(1)}, f32[64,16]{0,1:T(8,128)}, u32[]{:S(2)}) copy-start(f32[64,16]{0,1:T(8,128)} %param.12) | copy-start | bytes 12292
  3.2 23.0 %copy-start.4 = (f32[64,16]{0,1:T(8,128)S(1)}, f32[64,16]{0,1:T(8,128)}, u32[]{:S(2)}) copy-start(f32[64,16]{0,1:T(8,128)} %param.11) | copy-start | bytes 12292
  3.2 23.2 %copy-start.2 = (f32[3,3,1024]{2,1,0:T(4,128)S(1)}, f32[3,3,1024]{2,1,0:T(4,128)}, u32[]{:S(2)}) copy-start(f32[3,3,1024]{2,1,0:T(4,128)} %param.10) | copy-start | bytes 110596
  3.3 23.2 %copy-start.5 = (f32[1024]{0:T(1024)S(1)}, f32[1024]{0:T(1024)}, u32[]{:S(2)}) copy-start(f32[1024]{0:T(1024)} %param.13) | copy-start | bytes 12292
  5.8 92.7 %all-to-all-start = ((bf16[64,32,384]{2,1,0:T(8,128)(2,1)}), bf16[64,32,384]{2,1,0:T(8,128)(2,1)S(1)}, u32[]{:S(2)}, u32[]{:S(2)}) async-start(bf16[64,32,384]{2,1,0:T(8,128)(2,1)} %reshape.299), calls=%async_computation | async-start | bytes 3145728 | tf_op jit(solution)/shard_map/all_to_all | solution.py:51
  103.0 9.0 %collective-permute-start = (bf16[2,384]{1,0:T(2,128)(2,1)S(1)}, bf16[2,384]{1,0:T(2,128)(2,1)S(1)}, u32[]{:S(2)}, u32[]{:S(2)}) collective-permute-start(bf16[2,384]{1,0:T(2,128)(2,1)S(1)} %slice.104), channel_id=1, source_target_pairs={{0,1},{1,2},{2,3},{3,4},{4,5},{5,6},{6,7},{8,9},{9,10},{10,11},{11... | collective-permute-start | bytes 4616 | tf_op jit(solution)/shard_map/ppermute | solution.py:59
  144.3 2.9 %copy-start = (f32[7,8,16,16]{2,3,0,1:T(8,128)S(1)}, f32[7,8,16,16]{2,3,0,1:T(8,128)}, u32[]{:S(2)}) copy-start(f32[7,8,16,16]{2,3,0,1:T(8,128)} %copy.90) | copy-start | bytes 172036

commit v4 on v3

--- a/solution.py
+++ b/solution.py
@@ -46,30 +46,42 @@
     skip = lax.dynamic_slice_in_dim(every[:, o3:].reshape(n_ch * local_channels), here_ctx * width, width, 0)
     coefficient = res * jnp.sqrt(1.0 - jnp.exp(-2.0 * rate))
 
-    sending = jnp.transpose(projections.reshape(feeds, rows_here, n_ctx, width), (2, 1, 0, 3))
-    sending = sending.reshape(n_ctx, rows_here, feeds * width)
-    received = lax.all_to_all(sending, "ctx", 0, 0, tiled=True).reshape(n_ctx * rows_here, feeds * width)
     routing = attention_order.reshape(n_ctx, tokens // n_ctx)
     mine = lax.dynamic_slice_in_dim(routing, here_ch * rows_here, rows_here, 1).reshape(n_ctx * rows_here)
     placer = (
         (mine - here_ch * span)[None, :] == jnp.arange(span, dtype=jnp.int32)[:, None]
     ).astype(jnp.bfloat16)
-    ordered = jnp.dot(placer, received, preferred_element_type=jnp.float32).astype(jnp.bfloat16)
 
-    earlier = lax.ppermute(ordered[span - 2 :, :], "ch", [(i, i + 1) for i in range(n_ch - 1)])
-    widened = jnp.concatenate([earlier, ordered], axis=0).astype(jnp.float32)
-    widened = jnp.stack([widened[:, p * width : (p + 1) * width] for p in range(feeds)])
+    arrived = []
+
+    def arrive(part):
+        count = part.shape[0]
+        sending = jnp.transpose(part.reshape(count, rows_here, n_ctx, width), (2, 1, 0, 3))
+        sending = sending.reshape(n_ctx, rows_here, count * width)
+        received = lax.all_to_all(sending, "ctx", 0, 0, tiled=True).reshape(n_ctx * rows_here, count * width)
+        arrived.append(received)
+        ordered = jnp.dot(placer, received, preferred_element_type=jnp.float32).astype(jnp.bfloat16)
+        earlier = lax.ppermute(ordered[span - 2 :, :], "ch", [(i, i + 1) for i in range(n_ch - 1)])
+        widened = jnp.concatenate([earlier, ordered], axis=0).astype(jnp.float32)
+        return [widened[:, p * width : (p + 1) * width] for p in range(count)]
+
     bounds = jnp.cumsum(doc_lengths).astype(jnp.int32)
     span_docs = doc_index(here_ch * span - 2 + jnp.arange(span + 2, dtype=jnp.int32), bounds)
     current = span_docs[2:]
-    keep_one = (span_docs[1 : 1 + span] == current).astype(jnp.float32)[None, :, None]
-    keep_two = (span_docs[0:span] == current).astype(jnp.float32)[None, :, None]
-    featured = (
-        sf[:, 0, None, :] * widened[:, 2:]
-        + sf[:, 1, None, :] * widened[:, 1 : 1 + span] * keep_one
-        + sf[:, 2, None, :] * widened[:, 0:span] * keep_two
-    )
-    gated = (featured[1] * featured[2]).astype(jnp.bfloat16)
+    keep_one = (span_docs[1 : 1 + span] == current).astype(jnp.float32)[:, None]
+    keep_two = (span_docs[0:span] == current).astype(jnp.float32)[:, None]
+
+    def feature(p, rows):
+        return (
+            sf[p, 0, None, :] * rows[2:]
+            + sf[p, 1, None, :] * rows[1 : 1 + span] * keep_one
+            + sf[p, 2, None, :] * rows[0:span] * keep_two
+        )
+
+    key_rows, value_rows = arrive(projections[1:3])
+    featured_key = feature(1, key_rows)
+    featured_value = feature(2, value_rows)
+    gated = (featured_key * featured_value).astype(jnp.bfloat16)
 
     steps = jnp.arange(block, dtype=jnp.float32)
     falling = coefficient[:, None, :] * jnp.exp(-rate[:, None, :] * steps[None, :, None])
@@ -130,7 +142,9 @@
 
     gated32 = gated.astype(jnp.float32)
     combined = filtered.reshape(span, width) + skip[None, :] * gated32
-    mixed = (featured[0] * combined).astype(jnp.bfloat16)
+    _, query_part = lax.optimization_barrier((arrived[0], projections[0:1]))
+    (query_rows,) = arrive(query_part)
+    mixed = (feature(0, query_rows) * combined).astype(jnp.bfloat16)
 
     back = jnp.dot(placer.T, mixed, preferred_element_type=jnp.float32).astype(jnp.bfloat16)
     returned = lax.all_to_all(back.reshape(n_ctx, rows_here, width), "ctx", 0, 0, tiled=True)

time: 198 us -> 180 us (0.909)
  local copies, waits for them, and re-layouts: 23 us -> 11 us
  waiting for transfers between devices: 50 us -> 38.9 us
  starting transfers between devices: 27.6 us -> 36.7 us
  other arithmetic: 10.1 us -> 6.76 us
    all_to_all x1 -> x2, waiting for transfers between devices: 49.6 us -> 38.9 us  [arrive(): lax.all_to_all(sending, 'ctx', 0, 0, tiled=True)]
    all_to_all x1 -> x2, starting transfers between devices: 19.1 us -> 25.2 us  [arrive(): lax.all_to_all(sending, 'ctx', 0, 0, tiled=True)]
    unnamed x24 -> x25, local copies, waits for them, and re-layouts: 6.52 us -> 1.57 us
    ppermute x1 -> x2, starting transfers between devices: 8.48 us -> 11.5 us  [arrive(): lax.ppermute(ordered[span - 2:, :], 'ch', [(i, i + 1) for i in range(n_ch...]
    convert_element_type x2 -> x1, local copies, waits for them, and re-layouts: 2.93 us -> 0.21 us  [shards(): gated = (featured_key * featured_value).astype(jnp.bfloat16)]
    dot_general x1 -> x2, matrix products: 4.51 us -> 7.21 us  [arrive(): jnp.dot(placer, received, preferred_element_type=jnp.float32)]
    reshape x1, local copies, waits for them, and re-layouts: 2.59 us -> 0.32 us  [shards(): combined = filtered.reshape(span, width) + skip[None, :] * gated32]
    reshape x3 -> x4, local copies, waits for them, and re-layouts: 4.13 us -> 3.76 us  [the longest x3 2.68 us: arrive(): sending = sending.reshape(n_ctx, rows_here, count * width)]
  transfers between devices with their start and end apart: 2 -> 4, of which waited for: 2 -> 2; matrix products, arithmetic and copies ran while one was open for 5% -> 11% of each run, Pallas kernels for 0% -> 0%
where the time goes in v4:
time: 180 us
  blocking collectives  65.1 us (36%)
  waiting for transfers between devices  38.9 us (22%)
  starting transfers between devices  36.7 us (20%)
  matrix products  20.7 us (12%)
  local copies, waits for them, and re-layouts  11 us (6%)
  other arithmetic  6.76 us (4%)
    all_to_all x2, waiting for transfers between devices, arrive(): lax.all_to_all(sending, 'ctx', 0, 0, tiled=True)  38.9 us
    all_to_all x1, blocking collectives, shards(): lax.all_to_all(back.reshape(n_ctx, rows_here, width), 'ctx', 0, 0, tiled=...  38.1 us
    all_to_all x2, starting transfers between devices, arrive(): lax.all_to_all(sending, 'ctx', 0, 0, tiled=True)  25.2 us
    all_gather x1, blocking collectives, shards(): every = lax.all_gather(flat, 'ch')  14.3 us
    all_gather x1, blocking collectives, shards(): gathered = lax.all_gather(local_state[chunks - 1], 'ch')  12.8 us
    ppermute x2, starting transfers between devices, arrive(): lax.ppermute(ordered[span - 2:, :], 'ch', [(i, i + 1) for i in range(n_ch...  11.5 us
    dot_general x2, matrix products, arrive(): jnp.dot(placer, received, preferred_element_type=jnp.float32)  7.21 us
    dot_general x1, matrix products, shards(): jnp.dot(placer.T, mixed, preferred_element_type=jnp.float32)  5.22 us
  transfers between devices with their start and end apart: 4, of which 2 were waited for; matrix products, arithmetic and copies ran while one was open for 11% of the time, Pallas kernels for 0%

profile of v4, /device:TPU:1, one launch (start us, length us, event | category | flops | bytes accessed | tf_op | source)
XLA Modules:
  0.0 179.7 jit_solution(4681875149898698801)
XLA Ops:
  0.0 1.2 slice-done
  1.2 0.3 copy.89
  1.5 1.1 copy.99
  2.6 1.5 reshape.300
  4.1 19.2 %all-to-all-start = ((bf16[64,32,256]{2,1,0:T(8,128)(2,1)}), bf16[64,32,256]{2,1,0:T(8,128)(2,1)S(1)}, u32[]{:S(2)}, u32[]{:S(2)}) async-start(bf16[64,32,256]{2,1,0:T(8,128)(2,1)} %reshape.300), calls=%async_computation | async-start | bytes 2097152 | tf_op jit(solution)/shard_map/all_to_all | solution.py:61
  23.5 0.2 reduce-window.8
  23.6 0.1 convert_reduce_fusion
  23.7 0.1 dynamic-slice_subtract_fusion
  23.9 0.6 slice.164
  24.6 0.1 copy.67
  24.7 0.1 reshape.296
  24.7 0.1 copy.66
  24.8 0.1 reshape.295
  25.0 14.3 %all-gather = f32[98304]{0:T(1024)S(1)} all-gather(f32[12288]{0:T(1024)S(1)} %pad_maximum_fusion), channel_id=2, replica_groups=mesh['ctx'=64,'ch'=8] {'ch'}, dimensions={0}, use_global_device_ids=true | all-gather | bytes 442368 | tf_op jit(solution)/shard_map/all_gather | solution.py:36
  39.2 0.1 reshape.313
  39.4 0.1 reshape.307
  39.5 0.1 reshape.308
  39.7 0.2 reshape.298
  39.9 0.2 slice_reduce_fusion.1
  40.1 0.1 convert_reduce_fusion.1
  40.2 0.7 compare_convert_fusion.2
  40.8 0.1 exponential_multiply_fusion
  41.0 0.1 dynamic_slice.19
  41.0 0.2 slice_reduce_fusion
  41.2 0.7 pad_add_fusion
  42.0 0.1 fusion.66
  42.1 0.1 fusion.65
  42.2 0.1 fusion.63
  42.4 0.2 exponential_select_fusion
  42.6 3.0 %subtract_convert_fusion = (bf16[8,256,256]{1,2,0:T(8,128)(2,1)}, bf16[8,256,256]{1,2,0:T(8,128)(2,1)S(1)}) fusion(pred[256,256]{0,1:T(8,128)(4,1)S(1)} %iota_compare_fusion.10, f32[8,16]{1,0:T(8,128)S(1)} %get-tuple-element.8, f32[8,16]{1,0:T(8,128)S(1)} %neg.12, f32[8,16]{1,0:T(8,128)S(1)} %get-tuple-element.7), kind=kOutput, calls=%fused_computation.19 | convolution fusion | flops 103907328 | bytes 2164224 | tf_op jit(solution)/shard_map/gtm,gms->gts/dot_general | solution.py:91
  45.6 1.2 select_convert_fusion
  46.9 28.1 %all-to-all-done = bf16[64,32,256]{2,1,0:T(8,128)(2,1)S(1)} async-done(((bf16[64,32,256]{2,1,0:T(8,128)(2,1)}), bf16[64,32,256]{2,1,0:T(8,128)(2,1)S(1)}, u32[]{:S(2)}, u32[]{:S(2)}) %all-to-all-start) | async-done | bytes 1048608 | tf_op jit(solution)/shard_map/all_to_all | solution.py:61
  75.0 0.1 copy.91
  75.1 3.2 %fusion.10 = bf16[2048,256]{1,0:T(8,128)(2,1)S(1)} fusion(bf16[2048,256]{1,0:T(8,128)(2,1)S(1)} %bitcast.103, s32[2048]{0:T(1024)S(1)} %sub.68), kind=kOutput, calls=%fused_computation.13 | convolution fusion | flops 2152202240 | bytes 2105344 | tf_op jit(solution)/shard_map/dot_general | solution.py:63
  78.3 7.7 %collective-permute-start.1 = (bf16[2,256]{1,0:T(2,128)(2,1)S(1)}, bf16[2,256]{1,0:T(2,128)(2,1)S(1)}, u32[]{:S(2)}, u32[]{:S(2)}) collective-permute-start(bf16[2,256]{1,0:T(2,128)(2,1)S(1)} %slice.155), channel_id=1, source_target_pairs={{0,1},{1,2},{2,3},{3,4},{4,5},{5,6},{6,7},{8,9},{9,10},{10,11},{11... | collective-permute-start | bytes 3080 | tf_op jit(solution)/shard_map/ppermute | solution.py:64
  86.1 1.1 copy.69
  87.2 6.0 %all-to-all-start.1 = ((bf16[64,32,128]{2,1,0:T(8,128)(2,1)}), bf16[64,32,128]{2,1,0:T(8,128)(2,1)}, u32[]{:S(2)}, u32[]{:S(2)}) async-start(bf16[64,32,128]{2,1,0:T(8,128)(2,1)} %copy.69), calls=%async_computation.1 | async-start | bytes 1048576 | tf_op jit(solution)/shard_map/all_to_all | solution.py:61
  93.2 0.2 maximum_convert_fusion
  93.5 0.9 fusion.20
  94.4 0.2 copy.70
  94.6 0.1 copy.90
  94.7 0.1 copy.71
  94.9 0.1 convert_multiply_fusion
  95.0 1.3 convolution_bitcast_fusion
  96.3 0.2 copy.75
  96.5 1.3 multiply_reduce_fusion
  97.8 0.2 copy.87
  98.0 12.8 %all_gather.11 = f32[8,8,16,16]{3,2,1,0:T(8,128)S(1)} all-gather(f32[1,8,16,16]{3,2,1,0:T(8,128)S(1)} %slice.166), channel_id=1, replica_groups=mesh['ctx'=64,'ch'=8] {'ch'}, dimensions={0}, use_global_device_ids=true | all-gather | bytes 73728 | tf_op jit(solution)/shard_map/all_gather | solution.py:123
  110.8 0.2 multiply_reduce_fusion.1
  111.0 0.1 copy.76
  111.1 0.2 broadcast_select_fusion
  111.3 2.9 %select_reduce_fusion = f32[8,8,16,256]{3,2,1,0:T(8,128)S(1)} fusion(pred[4,8,256]{2,1,0:T(8,128)(4,1)S(1)} %iota_compare_fusion.11, bf16[8,256,256]{1,2,0:T(8,128)(2,1)} %get-tuple-element.27, bf16[8,256,256]{1,2,0:T(8,128)(2,1)} %select_convert_fusion, bf16[4,8,256,8,16]{2,4,1,0,3:T(8,128)(2,1)S(1)} %broadcast_select_fusion), kind=kOutput, calls=%fused_computation.12 | convolution fusion | flops 1088159744 | bytes 5251072 | tf_op jit(solution)/shard_map/gts,dksgc->dktgc/dot_general | solution.py:102
  114.2 10.8 %all-to-all-done.1 = bf16[64,32,128]{2,1,0:T(8,128)(2,1)} async-done(((bf16[64,32,128]{2,1,0:T(8,128)(2,1)}), bf16[64,32,128]{2,1,0:T(8,128)(2,1)}, u32[]{:S(2)}, u32[]{:S(2)}) %all-to-all-start.1) | async-done | bytes 524320 | tf_op jit(solution)/shard_map/all_to_all | solution.py:61
  124.9 4.0 %fusion.11 = bf16[2048,128]{1,0:T(8,128)(2,1)S(1)} fusion(bf16[2048,128]{1,0:T(8,128)(2,1)} %bitcast.7, s32[2048]{0:T(1024)S(1)} %sub.68), kind=kOutput, calls=%fused_computation.14 | convolution fusion | flops 1078198272 | bytes 1056768 | tf_op jit(solution)/shard_map/dot_general | solution.py:63
  129.0 3.8 %collective-permute-start = (bf16[2,128]{1,0:T(2,128)(2,1)S(1)}, bf16[2,128]{1,0:T(2,128)(2,1)S(1)}, u32[]{:S(2)}, u32[]{:S(2)}) collective-permute-start(bf16[2,128]{1,0:T(2,128)(2,1)S(1)} %slice.148), channel_id=1, source_target_pairs={{0,1},{1,2},{2,3},{3,4},{4,5},{5,6},{6,7},{8,9},{9,10},{10,11},{11... | collective-permute-start | bytes 1544 | tf_op jit(solution)/shard_map/ppermute | solution.py:64
  132.8 1.1 fusion.16
  133.9 0.6 copy.79
  134.5 0.3 copy.92
  134.8 0.3 copy.80
  135.2 0.3 copy-done.1
  135.5 0.1 maximum_convert_fusion.1
  135.6 5.2 %fusion.12 = bf16[2048,128]{1,0:T(8,128)(2,1)S(1)} fusion(s32[2048]{0:T(1024)S(1)} %sub.68, f32[2050,128]{1,0:T(8,128)S(1)} %maximum_convert_fusion.1, f32[2048,128]{1,0:T(8,128)S(1)} %copy.80, bf16[2048,128]{1,0:T(8,128)(2,1)S(1)} %fusion.20, f32[128]{0:T(128)S(1)} %dynamic_slice.19, f32[2048]{0:T(1024)S(1)} %get-tuple-element.22, ...), kind=kOutput, calls=%fused_computation.15 | convolution fusion | flops 1081344000 | bytes 5269504 | tf_op jit(solution)/shard_map/dot_general | solution.py:149
  140.9 38.1 %all_to_all.15 = bf16[64,32,128]{2,1,0:T(8,128)(2,1)S(1)} all-to-all(bf16[64,32,128]{2,1,0:T(8,128)(2,1)S(1)} %bitcast.105), channel_id=1, replica_groups=mesh['ctx'=64,'ch'=8] {'ctx'}, dimensions={0} | all-to-all | bytes 1048576 | tf_op jit(solution)/shard_map/all_to_all | solution.py:150
  178.9 0.8 copy_bitcast_fusion.1
  (48 shorter events, 0.7 us)
Async XLA Ops:
  0.0 1.2 slice-start
  2.6 20.8 %copy-start.2 = (s32[16384]{0:T(1024)S(1)}, s32[16384]{0:T(1024)}, u32[]{:S(2)}) copy-start(s32[16384]{0:T(1024)} %param.8) | copy-start | bytes 196612
  2.6 20.8 %copy-start.7 = (s32[4]{0:T(128)S(1)}, s32[4]{0:T(128)}, u32[]{:S(2)}) copy-start(s32[4]{0:T(128)} %param.9) | copy-start | bytes 52
  4.1 20.4 %copy-start.4 = (f32[64,16]{0,1:T(8,128)S(1)}, f32[64,16]{0,1:T(8,128)}, u32[]{:S(2)}) copy-start(f32[64,16]{0,1:T(8,128)} %param.12) | copy-start | bytes 12292
  4.1 20.6 %copy-start.5 = (f32[64,16]{0,1:T(8,128)S(1)}, f32[64,16]{0,1:T(8,128)}, u32[]{:S(2)}) copy-start(f32[64,16]{0,1:T(8,128)} %param.11) | copy-start | bytes 12292
  4.1 20.8 %copy-start.3 = (f32[3,3,1024]{2,1,0:T(4,128)S(1)}, f32[3,3,1024]{2,1,0:T(4,128)}, u32[]{:S(2)}) copy-start(f32[3,3,1024]{2,1,0:T(4,128)} %param.10) | copy-start | bytes 110596
  4.1 20.8 %copy-start.6 = (f32[1024]{0:T(1024)S(1)}, f32[1024]{0:T(1024)}, u32[]{:S(2)}) copy-start(f32[1024]{0:T(1024)} %param.13) | copy-start | bytes 12292
  4.1 70.9 %all-to-all-start = ((bf16[64,32,256]{2,1,0:T(8,128)(2,1)}), bf16[64,32,256]{2,1,0:T(8,128)(2,1)S(1)}, u32[]{:S(2)}, u32[]{:S(2)}) async-start(bf16[64,32,256]{2,1,0:T(8,128)(2,1)} %reshape.300), calls=%async_computation | async-start | bytes 2097152 | tf_op jit(solution)/shard_map/all_to_all | solution.py:61
  42.6 32.4 %slice-start.1 = ((bf16[3,32,8192]{2,1,0:T(8,128)(2,1)}), bf16[1,32,8192]{2,1,0:T(8,128)(2,1)S(1)}, s32[]{:S(2)}) async-start(bf16[3,32,8192]{2,1,0:T(8,128)(2,1)} %param.7), calls=%async_computation.4 | async-start | bytes 1048576 | tf_op jit(solution)/shard_map/slice | solution.py:145
  78.3 14.9 %collective-permute-start.1 = (bf16[2,256]{1,0:T(2,128)(2,1)S(1)}, bf16[2,256]{1,0:T(2,128)(2,1)S(1)}, u32[]{:S(2)}, u32[]{:S(2)}) collective-permute-start(bf16[2,256]{1,0:T(2,128)(2,1)S(1)} %slice.155), channel_id=1, source_target_pairs={{0,1},{1,2},{2,3},{3,4},{4,5},{5,6},{6,7},{8,9},{9,10},{10,11},{11... | collective-permute-start | bytes 3080 | tf_op jit(solution)/shard_map/ppermute | solution.py:64
  87.2 37.7 %all-to-all-start.1 = ((bf16[64,32,128]{2,1,0:T(8,128)(2,1)}), bf16[64,32,128]{2,1,0:T(8,128)(2,1)}, u32[]{:S(2)}, u32[]{:S(2)}) async-start(bf16[64,32,128]{2,1,0:T(8,128)(2,1)} %copy.69), calls=%async_computation.1 | async-start | bytes 1048576 | tf_op jit(solution)/shard_map/all_to_all | solution.py:61
  129.0 5.5 %copy-start = (bf16[2048,128]{1,0:T(8,128)(2,1)}, bf16[2048,128]{1,0:T(8,128)(2,1)S(1)}, u32[]{:S(2)}) copy-start(bf16[2048,128]{1,0:T(8,128)(2,1)S(1)} %fusion.11) | copy-start | bytes 1572868
  129.0 6.2 %collective-permute-start = (bf16[2,128]{1,0:T(2,128)(2,1)S(1)}, bf16[2,128]{1,0:T(2,128)(2,1)S(1)}, u32[]{:S(2)}, u32[]{:S(2)}) collective-permute-start(bf16[2,128]{1,0:T(2,128)(2,1)S(1)} %slice.148), channel_id=1, source_target_pairs={{0,1},{1,2},{2,3},{3,4},{4,5},{5,6},{6,7},{8,9},{9,10},{10,11},{11... | collective-permute-start | bytes 1544 | tf_op jit(solution)/shard_map/ppermute | solution.py:64
  134.5 1.0 copy-start.1

commit v5 on v4

--- a/solution.py
+++ b/solution.py
@@ -11,10 +11,19 @@
     return jnp.where(positions >= 0, found, -1)
 
 
+def ctx_exchange(value):
+    n_z, n_x = lax.axis_size("cz"), lax.axis_size("cx")
+    rest = value.shape[1:]
+    value = value.reshape((n_z, n_x) + rest)
+    value = lax.all_to_all(value, "cx", 1, 1, tiled=True)
+    value = lax.all_to_all(value, "cz", 0, 0, tiled=True)
+    return value.reshape((n_z * n_x,) + rest)
+
+
 def shards(projections, attention_order, doc_lengths, short_filter, decay_rate, residue, skip_gain):
-    n_ctx = lax.axis_size("ctx")
+    n_ctx = lax.axis_size("cz") * lax.axis_size("cx")
     n_ch = lax.axis_size("ch")
-    here_ctx = lax.axis_index("ctx")
+    here_ctx = lax.axis_index("cz") * lax.axis_size("cx") + lax.axis_index("cx")
     here_ch = lax.axis_index("ch")
     feeds, rows_here, channels = projections.shape
     tokens = attention_order.shape[0]
@@ -58,7 +67,7 @@
         count = part.shape[0]
         sending = jnp.transpose(part.reshape(count, rows_here, n_ctx, width), (2, 1, 0, 3))
         sending = sending.reshape(n_ctx, rows_here, count * width)
-        received = lax.all_to_all(sending, "ctx", 0, 0, tiled=True).reshape(n_ctx * rows_here, count * width)
+        received = ctx_exchange(sending).reshape(n_ctx * rows_here, count * width)
         arrived.append(received)
         ordered = jnp.dot(placer, received, preferred_element_type=jnp.float32).astype(jnp.bfloat16)
         earlier = lax.ppermute(ordered[span - 2 :, :], "ch", [(i, i + 1) for i in range(n_ch - 1)])
@@ -147,13 +156,17 @@
     mixed = (feature(0, query_rows) * combined).astype(jnp.bfloat16)
 
     back = jnp.dot(placer.T, mixed, preferred_element_type=jnp.float32).astype(jnp.bfloat16)
-    returned = lax.all_to_all(back.reshape(n_ctx, rows_here, width), "ctx", 0, 0, tiled=True)
+    returned = ctx_exchange(back.reshape(n_ctx, rows_here, width))
     return jnp.transpose(returned, (1, 0, 2)).reshape(rows_here, n_ctx * width)
 
 
 def solution(mesh):
+    n_ctx, n_ch = mesh.devices.shape
+    n_x = 4 if n_ctx % 4 == 0 else 1
+    split = jax.sharding.Mesh(mesh.devices.reshape(n_ctx // n_x, n_x, n_ch), ("cz", "cx", "ch"))
+    rows = ("cz", "cx", "ch")
     placed = (
-        P(None, ("ctx", "ch"), None),
+        P(None, rows, None),
         P(),
         P(),
         P(None, None, "ch"),
@@ -161,6 +174,4 @@
         P("ch", None),
         P("ch"),
     )
-    return jax.shard_map(
-        shards, mesh=mesh, in_specs=placed, out_specs=P(("ctx", "ch"), None), check_vma=False
-    )
+    return jax.shard_map(shards, mesh=split, in_specs=placed, out_specs=P(rows, None), check_vma=False)

time: 180 us -> 213 us (1.18)
  the two profiles are of different devices: /device:TPU:1 before, /device:TPU:40 now
where the time goes in v5:
time: 213 us; the launch traced here: 212 us
  blocking collectives  74.2 us (35%)
  waiting for transfers between devices  58.3 us (27%)
  starting transfers between devices  36.6 us (17%)
  matrix products  19.3 us (9%)
  local copies, waits for them, and re-layouts  14.7 us (7%)
  other arithmetic  8.67 us (4%)
    all_to_all x2, waiting for transfers between devices, ctx_exchange(): value = lax.all_to_all(value, 'cz', 0, 0, tiled=True)  36 us
    all_to_all x1, blocking collectives, ctx_exchange(): value = lax.all_to_all(value, 'cz', 0, 0, tiled=True)  35.9 us
    all_to_all x2, starting transfers between devices, ctx_exchange(): value = lax.all_to_all(value, 'cz', 0, 0, tiled=True)  24.7 us
    all_to_all x2, waiting for transfers between devices, ctx_exchange(): value = lax.all_to_all(value, 'cx', 1, 1, tiled=True)  22 us
    all_gather x1, blocking collectives, shards(): every = lax.all_gather(flat, 'ch')  13.2 us
    all_to_all x1, blocking collectives, ctx_exchange(): value = lax.all_to_all(value, 'cx', 1, 1, tiled=True)  12.6 us
    all_gather x1, blocking collectives, shards(): gathered = lax.all_gather(local_state[chunks - 1], 'ch')  12.5 us
    all_to_all x2, starting transfers between devices, ctx_exchange(): value = lax.all_to_all(value, 'cx', 1, 1, tiled=True)  7.78 us
  transfers between devices with their start and end apart: 6, of which 5 were waited for; matrix products, arithmetic and copies ran while one was open for 10% of the time, Pallas kernels for 0%

profile of v5, /device:TPU:40, one launch (start us, length us, event | category | flops | bytes accessed | tf_op | source)
XLA Modules:
  0.0 212.4 jit_solution(15252943979707963598)
XLA Ops:
  0.0 1.2 slice-done
  1.2 0.3 copy.139
  1.5 1.1 copy.149
  2.6 0.7 reshape_reshape.15
  3.4 1.1 copy.111
  4.5 4.3 %all-to-all-start = ((bf16[16,4,32,256]{3,2,0,1:T(8,128)(2,1)}), bf16[16,4,32,256]{3,2,0,1:T(8,128)(2,1)S(1)}, u32[]{:S(2)}, u32[]{:S(2)}) async-start(bf16[16,4,32,256]{3,2,0,1:T(8,128)(2,1)} %copy.111), calls=%async_computation | async-start | bytes 2097152 | tf_op jit(solution)/shard_map/all_to_all | solution.py:18
  8.8 0.2 reduce-window.8
  9.1 0.6 slice.164
  10.3 13.6 %all-to-all-done = bf16[16,4,32,256]{3,2,0,1:T(8,128)(2,1)S(1)} async-done(((bf16[16,4,32,256]{3,2,0,1:T(8,128)(2,1)}), bf16[16,4,32,256]{3,2,0,1:T(8,128)(2,1)S(1)}, u32[]{:S(2)}, u32[]{:S(2)}) %all-to-all-start) | async-done | bytes 1048608 | tf_op jit(solution)/shard_map/all_to_all | solution.py:18
  23.8 1.1 copy.112
  24.9 15.2 %all-to-all-start.1 = ((bf16[16,4,32,256]{3,2,1,0:T(8,128)(2,1)}), bf16[16,4,32,256]{3,2,1,0:T(8,128)(2,1)S(1)}, u32[]{:S(2)}, u32[]{:S(2)}) async-start(bf16[16,4,32,256]{3,2,1,0:T(8,128)(2,1)} %copy.112), calls=%async_computation.1 | async-start | bytes 2097152 | tf_op jit(solution)/shard_map/all_to_all | solution.py:19
  40.2 13.2 %all-gather = f32[98304]{0:T(1024)S(1)} all-gather(f32[12288]{0:T(1024)S(1)} %pad_maximum_fusion), channel_id=2, replica_groups=mesh['cz'=16,'cx'=4,'ch'=8] {'ch'}, dimensions={0}, use_global_device_ids=true | all-gather | bytes 442368 | tf_op jit(solution)/shard_map/all_gather | solution.py:45
  53.5 0.1 reshape.291
  53.6 0.1 reshape.292
  53.8 0.2 reshape.286
  54.0 0.2 slice_reduce_fusion
  54.2 0.7 pad_add_fusion
  54.9 0.6 iota_subtract_fusion
  55.5 0.7 fusion.66
  56.2 0.2 slice_reduce_fusion.1
  56.7 0.7 compare_convert_fusion.2
  57.3 0.6 iota_compare_fusion.11
  57.9 0.7 fusion.63
  58.6 0.7 compare_convert_fusion
  59.4 0.2 exponential_select_fusion
  59.6 3.0 %subtract_convert_fusion = (bf16[8,256,256]{1,2,0:T(8,128)(2,1)}, bf16[8,256,256]{1,2,0:T(8,128)(2,1)S(1)}) fusion(pred[256,256]{0,1:T(8,128)(4,1)S(1)} %iota_compare_fusion.10, f32[8,16]{1,0:T(8,128)S(1)} %get-tuple-element.8, f32[8,16]{1,0:T(8,128)S(1)} %neg.12, f32[8,16]{1,0:T(8,128)S(1)} %get-tuple-element.7), kind=kOutput, calls=%fused_computation.19 | convolution fusion | flops 103907328 | bytes 2164224 | tf_op jit(solution)/shard_map/gtm,gms->gts/dot_general | solution.py:100
  62.6 0.2 select_convert_fusion
  62.8 24.6 %all-to-all-done.1 = bf16[16,4,32,256]{3,2,1,0:T(8,128)(2,1)S(1)} async-done(((bf16[16,4,32,256]{3,2,1,0:T(8,128)(2,1)}), bf16[16,4,32,256]{3,2,1,0:T(8,128)(2,1)S(1)}, u32[]{:S(2)}, u32[]{:S(2)}) %all-to-all-start.1) | async-done | bytes 1048608 | tf_op jit(solution)/shard_map/all_to_all | solution.py:19
  87.4 3.2 %fusion.10 = bf16[2048,256]{1,0:T(8,128)(2,1)S(1)} fusion(bf16[2048,256]{1,0:T(8,128)(2,1)S(1)} %bitcast.103, s32[2048]{0:T(1024)S(1)} %sub.68), kind=kOutput, calls=%fused_computation.13 | convolution fusion | flops 2152202240 | bytes 2105344 | tf_op jit(solution)/shard_map/dot_general | solution.py:72
  90.6 1.9 collective-permute-start.1
  92.5 0.6 iota_add_fusion.1
  93.2 0.1 copy.141
  93.3 1.1 copy.114
  94.5 3.5 %all-to-all-start.2 = ((bf16[16,4,32,128]{3,2,0,1:T(8,128)(2,1)}), bf16[16,4,32,128]{3,2,0,1:T(8,128)(2,1)S(1)}, u32[]{:S(2)}, u32[]{:S(2)}) async-start(bf16[16,4,32,128]{3,2,0,1:T(8,128)(2,1)} %copy.114), calls=%async_computation.2 | async-start | bytes 1048576 | tf_op jit(solution)/shard_map/all_to_all | solution.py:18
  98.0 0.2 maximum_convert_fusion
  98.3 0.9 fusion.20
  99.3 0.2 copy.116
  99.5 0.1 copy.140
  99.6 0.1 copy.117
  99.7 8.4 %all-to-all-done.2 = bf16[16,4,32,128]{3,2,0,1:T(8,128)(2,1)S(1)} async-done(((bf16[16,4,32,128]{3,2,0,1:T(8,128)(2,1)}), bf16[16,4,32,128]{3,2,0,1:T(8,128)(2,1)S(1)}, u32[]{:S(2)}, u32[]{:S(2)}) %all-to-all-start.2) | async-done | bytes 524320 | tf_op jit(solution)/shard_map/all_to_all | solution.py:18
  108.1 0.9 copy.115
  109.0 9.5 %all-to-all-start.3 = ((bf16[16,4,32,128]{3,2,1,0:T(8,128)(2,1)}), bf16[16,4,32,128]{3,2,1,0:T(8,128)(2,1)}, u32[]{:S(2)}, u32[]{:S(2)}) async-start(bf16[16,4,32,128]{3,2,1,0:T(8,128)(2,1)} %copy.115), calls=%async_computation.3 | async-start | bytes 1048576 | tf_op jit(solution)/shard_map/all_to_all | solution.py:19
  118.6 1.3 convolution_bitcast_fusion
  119.9 0.2 copy.121
  120.1 1.3 multiply_reduce_fusion
  121.5 0.2 copy.137
  121.7 12.5 %all_gather.11 = f32[8,8,16,16]{3,2,1,0:T(8,128)S(1)} all-gather(f32[1,8,16,16]{3,2,1,0:T(8,128)S(1)} %slice.166), channel_id=1, replica_groups=mesh['cz'=16,'cx'=4,'ch'=8] {'ch'}, dimensions={0}, use_global_device_ids=true | all-gather | bytes 73728 | tf_op jit(solution)/shard_map/all_gather | solution.py:132
  134.1 0.2 multiply_reduce_fusion.1
  134.5 0.2 broadcast_select_fusion
  134.6 1.0 copy-done.25
  135.6 1.5 select_reduce_fusion
  137.2 11.4 %all-to-all-done.3 = bf16[16,4,32,128]{3,2,1,0:T(8,128)(2,1)} async-done(((bf16[16,4,32,128]{3,2,1,0:T(8,128)(2,1)}), bf16[16,4,32,128]{3,2,1,0:T(8,128)(2,1)}, u32[]{:S(2)}, u32[]{:S(2)}) %all-to-all-start.3) | async-done | bytes 524320 | tf_op jit(solution)/shard_map/all_to_all | solution.py:19
  148.6 4.0 %fusion.11 = bf16[2048,128]{1,0:T(8,128)(2,1)S(1)} fusion(bf16[2048,128]{1,0:T(8,128)(2,1)} %bitcast.7, s32[2048]{0:T(1024)S(1)} %copy-done.11), kind=kOutput, calls=%fused_computation.14 | convolution fusion | flops 1078198272 | bytes 1056768 | tf_op jit(solution)/shard_map/dot_general | solution.py:72
  152.6 2.1 %collective-permute-start = (bf16[2,128]{1,0:T(2,128)(2,1)S(1)}, bf16[2,128]{1,0:T(2,128)(2,1)S(1)}, u32[]{:S(2)}, u32[]{:S(2)}) collective-permute-start(bf16[2,128]{1,0:T(2,128)(2,1)S(1)} %slice.148), channel_id=1, source_target_pairs={{0,1},{1,2},{2,3},{3,4},{4,5},{5,6},{6,7},{8,9},{9,10},{10,11},{11... | collective-permute-start | bytes 1544 | tf_op jit(solution)/shard_map/ppermute | solution.py:73
  154.8 1.1 fusion.16
  155.9 0.6 copy.125
  156.5 0.3 copy.142
  156.9 0.3 copy.126
  157.2 0.3 collective-permute-done
  157.6 0.1 maximum_convert_fusion.1
  157.7 5.2 %fusion.12 = bf16[2048,128]{1,0:T(8,128)(2,1)S(1)} fusion(s32[2048]{0:T(1024)S(1)} %copy-done.11, f32[2050,128]{1,0:T(8,128)S(1)} %maximum_convert_fusion.1, f32[2048,128]{1,0:T(8,128)S(1)} %copy.126, bf16[2048,128]{1,0:T(8,128)(2,1)S(1)} %fusion.20, f32[128]{0:T(128)S(1)} %dynamic_slice.19, f32[2048]{0:T(1024)S(1)} %copy-done.4, f32[128]{0:T(128)S(1)} %copy-done.22, ...), kind=kOutput, calls=%fused_computation.15 | convolution fusion | flops 1081344000 | bytes 5269504 | tf_op jit(solution)/shard_map/dot_general | solution.py:158
  162.9 12.6 %all_to_all.30 = bf16[16,4,32,128]{3,2,0,1:T(8,128)(2,1)S(1)} all-to-all(bf16[16,4,32,128]{3,2,0,1:T(8,128)(2,1)S(1)} %copy.127), channel_id=1, replica_groups=mesh['cz'=16,'cx'=4,'ch'=8] {'cx'}, dimensions={1} | all-to-all | bytes 1048576 | tf_op jit(solution)/shard_map/all_to_all | solution.py:18
  175.6 35.9 %all_to_all.31 = bf16[16,4,32,128]{3,2,1,0:T(8,128)(2,1)S(1)} all-to-all(bf16[16,4,32,128]{3,2,1,0:T(8,128)(2,1)S(1)} %copy.128), channel_id=1, replica_groups=mesh['cz'=16,'cx'=4,'ch'=8] {'cz'}, dimensions={0} | all-to-all | bytes 1048576 | tf_op jit(solution)/shard_map/all_to_all | solution.py:19
  211.5 0.9 copy.150
  (93 shorter events, 1.8 us)
Async XLA Ops:
  0.0 1.2 slice-start
  3.3 5.5 %copy-start.24 = (s32[4]{0:T(128)S(1)}, s32[4]{0:T(128)}, u32[]{:S(2)}) copy-start(s32[4]{0:T(128)} %param.9) | copy-start | bytes 52
  3.3 6.4 %copy-start.2 = (s32[16384]{0:T(1024)S(1)}, s32[16384]{0:T(1024)}, u32[]{:S(2)}) copy-start(s32[16384]{0:T(1024)} %param.8) | copy-start | bytes 196612
  3.3 6.6 %copy-start.8 = (f32[64,16]{0,1:T(8,128)S(1)}, f32[64,16]{0,1:T(8,128)}, u32[]{:S(2)}) copy-start(f32[64,16]{0,1:T(8,128)} %param.12) | copy-start | bytes 12292
  3.3 6.7 %copy-start.9 = (f32[64,16]{0,1:T(8,128)S(1)}, f32[64,16]{0,1:T(8,128)}, u32[]{:S(2)}) copy-start(f32[64,16]{0,1:T(8,128)} %param.11) | copy-start | bytes 12292
  3.4 6.9 %copy-start.3 = (f32[3,3,1024]{2,1,0:T(4,128)S(1)}, f32[3,3,1024]{2,1,0:T(4,128)}, u32[]{:S(2)}) copy-start(f32[3,3,1024]{2,1,0:T(4,128)} %param.10) | copy-start | bytes 110596
  4.5 19.4 %all-to-all-start = ((bf16[16,4,32,256]{3,2,0,1:T(8,128)(2,1)}), bf16[16,4,32,256]{3,2,0,1:T(8,128)(2,1)S(1)}, u32[]{:S(2)}, u32[]{:S(2)}) async-start(bf16[16,4,32,256]{3,2,0,1:T(8,128)(2,1)} %copy.111), calls=%async_computation | async-start | bytes 2097152 | tf_op jit(solution)/shard_map/all_to_all | solution.py:18
  9.9 77.5 %copy-start.10 = (s32[2048]{0:T(1024)}, s32[2048]{0:T(1024)S(1)}, u32[]{:S(2)}) copy-start(s32[2048]{0:T(1024)S(1)} %sub.68) | copy-start | bytes 24580
  10.3 29.9 %copy-start.12 = (f32[1024]{0:T(1024)S(1)}, f32[1024]{0:T(1024)}, u32[]{:S(2)}) copy-start(f32[1024]{0:T(1024)} %param.13) | copy-start | bytes 12292
  24.9 62.5 %all-to-all-start.1 = ((bf16[16,4,32,256]{3,2,1,0:T(8,128)(2,1)}), bf16[16,4,32,256]{3,2,1,0:T(8,128)(2,1)S(1)}, u32[]{:S(2)}, u32[]{:S(2)}) async-start(bf16[16,4,32,256]{3,2,1,0:T(8,128)(2,1)} %copy.112), calls=%async_computation.1 | async-start | bytes 2097152 | tf_op jit(solution)/shard_map/all_to_all | solution.py:19
  87.4 5.8 %slice-start.1 = ((bf16[3,32,8192]{2,1,0:T(8,128)(2,1)}), bf16[1,32,8192]{2,1,0:T(8,128)(2,1)S(1)}, s32[]{:S(2)}) async-start(bf16[3,32,8192]{2,1,0:T(8,128)(2,1)} %param.7), calls=%async_computation.7 | async-start | bytes 1048576 | tf_op jit(solution)/shard_map/slice | solution.py:154
  90.6 7.4 %collective-permute-start.1 = (bf16[2,256]{1,0:T(2,128)(2,1)S(1)}, bf16[2,256]{1,0:T(2,128)(2,1)S(1)}, u32[]{:S(2)}, u32[]{:S(2)}) collective-permute-start(bf16[2,256]{1,0:T(2,128)(2,1)S(1)} %slice.155), channel_id=1, source_target_pairs={{0,1},{1,2},{2,3},{3,4},{4,5},{5,6},{6,7},{8,9},{9,10},{10,11},{11... | collective-permute-start | bytes 3080 | tf_op jit(solution)/shard_map/ppermute | solution.py:73
  94.5 3.8 %copy-start.4 = (f32[2048]{0:T(1024)S(1)}, f32[2048]{0:T(1024)}, u32[]{:S(2)}) copy-start(f32[2048]{0:T(1024)} %get-tuple-element.22) | copy-start | bytes 24580
  94.5 3.8 %copy-start.13 = (f32[128]{0:T(128)S(1)}, f32[128]{0:T(128)}, u32[]{:S(2)}) copy-start(f32[128]{0:T(128)} %get-tuple-element.10) | copy-start | bytes 1540
  94.5 3.8 %copy-start.14 = (f32[128]{0:T(128)S(1)}, f32[128]{0:T(128)}, u32[]{:S(2)}) copy-start(f32[128]{0:T(128)} %get-tuple-element.11) | copy-start | bytes 1540
  94.5 3.8 %copy-start.15 = (f32[128]{0:T(128)S(1)}, f32[128]{0:T(128)}, u32[]{:S(2)}) copy-start(f32[128]{0:T(128)} %get-tuple-element.12) | copy-start | bytes 1540
  94.5 3.8 %copy-start.16 = (f32[128]{0:T(128)S(1)}, f32[128]{0:T(128)}, u32[]{:S(2)}) copy-start(f32[128]{0:T(128)} %get-tuple-element.13) | copy-start | bytes 1540
  94.5 3.8 %copy-start.17 = (f32[128]{0:T(128)S(1)}, f32[128]{0:T(128)}, u32[]{:S(2)}) copy-start(f32[128]{0:T(128)} %get-tuple-element.14) | copy-start | bytes 1540
  94.5 3.8 %copy-start.18 = (f32[128]{0:T(128)S(1)}, f32[128]{0:T(128)}, u32[]{:S(2)}) copy-start(f32[128]{0:T(128)} %get-tuple-element.17) | copy-start | bytes 1540
  94.5 13.6 %all-to-all-start.2 = ((bf16[16,4,32,128]{3,2,0,1:T(8,128)(2,1)}), bf16[16,4,32,128]{3,2,0,1:T(8,128)(2,1)S(1)}, u32[]{:S(2)}, u32[]{:S(2)}) async-start(bf16[16,4,32,128]{3,2,0,1:T(8,128)(2,1)} %copy.114), calls=%async_computation.2 | async-start | bytes 1048576 | tf_op jit(solution)/shard_map/all_to_all | solution.py:18
  99.5 19.0 %copy-start.6 = (f32[8,256]{1,0:T(8,128)S(1)}, f32[8,256]{1,0:T(8,128)}, u32[]{:S(2)}) copy-start(f32[8,256]{1,0:T(8,128)} %get-tuple-element.24) | copy-start | bytes 24580
  99.6 19.0 %copy-start.20 = (f32[256]{0:T(256)S(1)}, f32[256]{0:T(256)}, u32[]{:S(2)}) copy-start(f32[256]{0:T(256)} %iota_subtract_fusion) | copy-start | bytes 3076
  109.0 39.6 %all-to-all-start.3 = ((bf16[16,4,32,128]{3,2,1,0:T(8,128)(2,1)}), bf16[16,4,32,128]{3,2,1,0:T(8,128)(2,1)}, u32[]{:S(2)}, u32[]{:S(2)}) async-start(bf16[16,4,32,128]{3,2,1,0:T(8,128)(2,1)} %copy.115), calls=%async_computation.3 | async-start | bytes 1048576 | tf_op jit(solution)/shard_map/all_to_all | solution.py:19
  121.4 13.0 %copy-start.7 = (pred[4,8,256]{2,1,0:T(8,128)(4,1)S(1)}, pred[4,8,256]{2,1,0:T(8,128)(4,1)}, u32[]{:S(2)}) copy-start(pred[4,8,256]{2,1,0:T(8,128)(4,1)} %iota_compare_fusion.11) | copy-start | bytes 24580
  134.4 1.2 copy-start.25
  135.6 12.9 %copy-start.11 = (s32[2048]{0:T(1024)S(1)}, s32[2048]{0:T(1024)}, u32[]{:S(2)}) copy-start(s32[2048]{0:T(1024)} %copy-done.10) | copy-start | bytes 24580
  148.6 6.2 %copy-start.5 = (f32[8,256]{1,0:T(8,128)S(1)}, f32[8,256]{1,0:T(8,128)}, u32[]{:S(2)}) copy-start(f32[8,256]{1,0:T(8,128)} %get-tuple-element.23) | copy-start | bytes 24580
  148.6 6.2 %copy-start.19 = (f32[256]{0:T(256)S(1)}, f32[256]{0:T(256)}, u32[]{:S(2)}) copy-start(f32[256]{0:T(256)} %iota_add_fusion.1) | copy-start | bytes 3076
  152.6 3.9 %copy-start = (bf16[2048,128]{1,0:T(8,128)(2,1)}, bf16[2048,128]{1,0:T(8,128)(2,1)S(1)}, u32[]{:S(2)}) copy-start(bf16[2048,128]{1,0:T(8,128)(2,1)S(1)} %fusion.11) | copy-start | bytes 1572868
  152.6 4.9 %collective-permute-start = (bf16[2,128]{1,0:T(2,128)(2,1)S(1)}, bf16[2,128]{1,0:T(2,128)(2,1)S(1)}, u32[]{:S(2)}, u32[]{:S(2)}) collective-permute-start(bf16[2,128]{1,0:T(2,128)(2,1)S(1)} %slice.148), channel_id=1, source_target_pairs={{0,1},{1,2},{2,3},{3,4},{4,5},{5,6},{6,7},{8,9},{9,10},{10,11},{11... | collective-permute-start | bytes 1544 | tf_op jit(solution)/shard_map/ppermute | solution.py:73
  156.5 1.0 copy-start.1
  156.9 0.8 copy-start.21
  156.9 0.8 copy-start.22
  156.9 0.8 copy-start.23

commit v6 on v4

--- a/solution.py
+++ b/solution.py
@@ -143,10 +143,24 @@
     gated32 = gated.astype(jnp.float32)
     combined = filtered.reshape(span, width) + skip[None, :] * gated32
     _, query_part = lax.optimization_barrier((arrived[0], projections[0:1]))
-    (query_rows,) = arrive(query_part)
+    sending = jnp.transpose(query_part.reshape(1, rows_here, n_ctx, width), (2, 1, 0, 3))
+    sending = sending.reshape(n_ctx, rows_here, width)
+    received = lax.all_to_all(sending, "ctx", 0, 0, tiled=True).reshape(n_ctx * rows_here, width)
+    query = jnp.dot(placer, received, preferred_element_type=jnp.float32).astype(jnp.bfloat16)
+    query_halo = lax.ppermute(query[span - 2 :, :], "ch", [(i, i + 1) for i in range(n_ch - 1)])
+    query_rows = jnp.concatenate([jnp.zeros((2, width), jnp.bfloat16), query], axis=0).astype(jnp.float32)
     mixed = (feature(0, query_rows) * combined).astype(jnp.bfloat16)
+    head = jnp.concatenate([query_halo, query[0:2]], axis=0).astype(jnp.float32)
+    head_feature = (
+        sf[0, 0, None, :] * head[2:4]
+        + sf[0, 1, None, :] * head[1:3] * keep_one[0:2]
+        + sf[0, 2, None, :] * head[0:2] * keep_two[0:2]
+    )
+    head_mixed = (head_feature * combined[0:2]).astype(jnp.bfloat16)
 
     back = jnp.dot(placer.T, mixed, preferred_element_type=jnp.float32).astype(jnp.bfloat16)
+    where_row = (mine - here_ch * span)[:, None]
+    back = jnp.where(where_row == 0, head_mixed[0:1], jnp.where(where_row == 1, head_mixed[1:2], back))
     returned = lax.all_to_all(back.reshape(n_ctx, rows_here, width), "ctx", 0, 0, tiled=True)
     return jnp.transpose(returned, (1, 0, 2)).reshape(rows_here, n_ctx * width)
 

time: 180 us -> 186 us (1.033)
  waiting for transfers between devices: 38.9 us -> 23.6 us
  blocking collectives: 65.1 us -> 72.5 us
  local copies, waits for them, and re-layouts: 11 us -> 17.8 us
  other arithmetic: 6.76 us -> 13.2 us
    all_to_all x2 -> x1, waiting for transfers between devices: 38.9 us -> 22.6 us  [arrive(): lax.all_to_all(sending, 'ctx', 0, 0, tiled=True)]
    all_to_all x1, blocking collectives: 38.1 us -> 45.2 us  [shards(): lax.all_to_all(back.reshape(n_ctx, rows_here, width), 'ctx', 0, 0, tiled=...]
    all_to_all x0 -> x1, starting transfers between devices: none -> 5.99 us  [shards(): lax.all_to_all(sending, 'ctx', 0, 0, tiled=True)]
    all_to_all x2 -> x1, starting transfers between devices: 25.2 us -> 19.2 us  [arrive(): lax.all_to_all(sending, 'ctx', 0, 0, tiled=True)]
    dot_general x0 -> x1, matrix products: none -> 4.11 us  [shards(): jnp.dot(placer, received, preferred_element_type=jnp.float32)]
    dot_general x2 -> x1, matrix products: 7.21 us -> 3.18 us  [arrive(): jnp.dot(placer, received, preferred_element_type=jnp.float32)]
    ppermute x2 -> x1, starting transfers between devices: 11.5 us -> 7.71 us  [arrive(): lax.ppermute(ordered[span - 2:, :], 'ch', [(i, i + 1) for i in range(n_ch...]
    ppermute x0 -> x1, starting transfers between devices: none -> 3.76 us  [shards(): lax.ppermute(query[span - 2:, :], 'ch', [(i, i + 1) for i in range(n_ch -...]
  transfers between devices with their start and end apart: 4 -> 4, of which waited for: 2 -> 3; matrix products, arithmetic and copies ran while one was open for 11% -> 18% of each run, Pallas kernels for 0% -> 0%
where the time goes in v6:
time: 186 us; the launch traced here: 185 us
  blocking collectives  72.5 us (39%)
  starting transfers between devices  36.7 us (20%)
  waiting for transfers between devices  23.6 us (13%)
  matrix products  20.6 us (11%)
  local copies, waits for them, and re-layouts  17.8 us (10%)
  other arithmetic  13.2 us (7%)
    all_to_all x1, blocking collectives, shards(): lax.all_to_all(back.reshape(n_ctx, rows_here, width), 'ctx', 0, 0, tiled=...  45.2 us
    all_to_all x1, waiting for transfers between devices, arrive(): lax.all_to_all(sending, 'ctx', 0, 0, tiled=True)  22.6 us
    all_to_all x1, starting transfers between devices, arrive(): lax.all_to_all(sending, 'ctx', 0, 0, tiled=True)  19.2 us
    all_gather x1, blocking collectives, shards(): every = lax.all_gather(flat, 'ch')  14.3 us
    all_gather x1, blocking collectives, shards(): gathered = lax.all_gather(local_state[chunks - 1], 'ch')  13 us
    ppermute x1, starting transfers between devices, arrive(): lax.ppermute(ordered[span - 2:, :], 'ch', [(i, i + 1) for i in range(n_ch...  7.71 us
    all_to_all x1, starting transfers between devices, shards(): lax.all_to_all(sending, 'ctx', 0, 0, tiled=True)  5.99 us
    dot_general x1, matrix products, shards(): jnp.dot(placer.T, mixed, preferred_element_type=jnp.float32)  5.6 us
  transfers between devices with their start and end apart: 4, of which 3 were waited for; matrix products, arithmetic and copies ran while one was open for 18% of the time, Pallas kernels for 0%

profile of v6, /device:TPU:1, one launch (start us, length us, event | category | flops | bytes accessed | tf_op | source)
XLA Modules:
  0.0 185.2 jit_solution(15359323650768155176)
XLA Ops:
  0.0 1.2 slice-done
  1.2 0.3 copy.89
  1.5 1.1 copy.99
  2.6 1.5 reshape.316
  4.1 19.2 %all-to-all-start = ((bf16[64,32,256]{2,1,0:T(8,128)(2,1)}), bf16[64,32,256]{2,1,0:T(8,128)(2,1)S(1)}, u32[]{:S(2)}, u32[]{:S(2)}) async-start(bf16[64,32,256]{2,1,0:T(8,128)(2,1)} %reshape.316), calls=%async_computation | async-start | bytes 2097152 | tf_op jit(solution)/shard_map/all_to_all | solution.py:61
  23.5 0.2 reduce-window.8
  23.6 0.1 convert_reduce_fusion
  23.9 0.6 slice.205
  25.0 14.3 %all-gather = f32[98304]{0:T(1024)S(1)} all-gather(f32[12288]{0:T(1024)S(1)} %pad_maximum_fusion), channel_id=2, replica_groups=mesh['ctx'=64,'ch'=8] {'ch'}, dimensions={0}, use_global_device_ids=true | all-gather | bytes 442368 | tf_op jit(solution)/shard_map/all_gather | solution.py:36
  39.4 0.1 reshape.323
  39.5 0.1 reshape.324
  39.7 0.2 reshape.314
  39.9 0.2 slice_reduce_fusion.1
  40.2 0.7 compare_convert_fusion.2
  40.9 0.7 exponential_multiply_fusion
  41.6 0.6 copy.73
  42.2 0.6 fusion.65
  42.8 0.5 slice.195
  43.3 0.5 slice.193
  43.8 0.6 dynamic_slice.19
  44.4 0.2 slice_reduce_fusion
  44.6 0.7 pad_add_fusion
  45.4 0.6 iota_add_fusion.1
  45.9 0.6 fusion.69
  46.7 0.6 iota_compare_fusion.15
  47.3 0.7 compare_convert_fusion
  48.0 0.2 exponential_select_fusion
  48.2 3.0 %subtract_convert_fusion = (bf16[8,256,256]{1,2,0:T(8,128)(2,1)}, bf16[8,256,256]{1,2,0:T(8,128)(2,1)S(1)}) fusion(pred[256,256]{0,1:T(8,128)(4,1)S(1)} %iota_compare_fusion.14, f32[8,16]{1,0:T(8,128)S(1)} %get-tuple-element.8, f32[8,16]{1,0:T(8,128)S(1)} %neg.12, f32[8,16]{1,0:T(8,128)S(1)} %get-tuple-element.7), kind=kOutput, calls=%fused_computation.21 | convolution fusion | flops 103907328 | bytes 2164224 | tf_op jit(solution)/shard_map/gtm,gms->gts/dot_general | solution.py:91
  51.3 1.2 select_convert_fusion
  52.4 22.6 %all-to-all-done = bf16[64,32,256]{2,1,0:T(8,128)(2,1)S(1)} async-done(((bf16[64,32,256]{2,1,0:T(8,128)(2,1)}), bf16[64,32,256]{2,1,0:T(8,128)(2,1)S(1)}, u32[]{:S(2)}, u32[]{:S(2)}) %all-to-all-start) | async-done | bytes 1048608 | tf_op jit(solution)/shard_map/all_to_all | solution.py:61
  75.0 3.2 %fusion.10 = bf16[2048,256]{1,0:T(8,128)(2,1)S(1)} fusion(bf16[2048,256]{1,0:T(8,128)(2,1)S(1)} %bitcast.107, s32[2048]{0:T(1024)S(1)} %sub.77), kind=kOutput, calls=%fused_computation.13 | convolution fusion | flops 2152202240 | bytes 2105344 | tf_op jit(solution)/shard_map/dot_general | solution.py:63
  78.2 7.7 %collective-permute-start.1 = (bf16[2,256]{1,0:T(2,128)(2,1)S(1)}, bf16[2,256]{1,0:T(2,128)(2,1)S(1)}, u32[]{:S(2)}, u32[]{:S(2)}) collective-permute-start(bf16[2,256]{1,0:T(2,128)(2,1)S(1)} %slice.196), channel_id=1, source_target_pairs={{0,1},{1,2},{2,3},{3,4},{4,5},{5,6},{6,7},{8,9},{9,10},{10,11},{11... | collective-permute-start | bytes 3080 | tf_op jit(solution)/shard_map/ppermute | solution.py:64
  86.0 0.1 copy.91
  86.1 1.2 copy.69
  87.3 6.0 %all-to-all-start.1 = ((bf16[64,32,128]{2,1,0:T(8,128)(2,1)}), bf16[64,32,128]{2,1,0:T(8,128)(2,1)}, u32[]{:S(2)}, u32[]{:S(2)}) async-start(bf16[64,32,128]{2,1,0:T(8,128)(2,1)} %copy.69), calls=%async_computation.1 | async-start | bytes 1048576 | tf_op jit(solution)/shard_map/all_to_all | solution.py:148
  93.3 0.2 maximum_convert_fusion
  93.6 0.9 fusion.28
  94.5 0.2 copy.70
  94.8 0.1 copy.90
  94.9 0.1 copy.71
  95.1 2.1 %convolution_bitcast_fusion = f32[8,8,16,16]{2,3,0,1:T(8,128)} fusion(f32[8,256,8,16]{1,0,3,2:T(8,128)S(1)} %convert_multiply_fusion, f32[256]{0:T(256)S(1)} %iota_subtract_fusion, f32[8,16]{1,0:T(8,128)S(1)} %neg.12), kind=kOutput, calls=%fused_computation.27 | convolution fusion | flops 50364416 | bytes 1115648 | tf_op jit(solution)/shard_map/gms,ksgc->kgmc/dot_general | solution.py:109
  97.2 1.2 copy.75
  98.4 1.3 multiply_reduce_fusion
  99.8 0.6 slice.207
  100.4 0.2 copy.87
  100.6 13.0 %all_gather.11 = f32[8,8,16,16]{3,2,1,0:T(8,128)S(1)} all-gather(f32[1,8,16,16]{3,2,1,0:T(8,128)} %slice.207), channel_id=1, replica_groups=mesh['ctx'=64,'ch'=8] {'ch'}, dimensions={0}, use_global_device_ids=true | all-gather | bytes 73728 | tf_op jit(solution)/shard_map/all_gather | solution.py:123
  113.6 1.0 multiply_reduce_fusion.1
  114.7 1.0 multiply_add_fusion.1
  115.6 0.2 broadcast_select_fusion
  115.9 0.3 copy-done.37
  116.2 1.5 select_reduce_fusion
  117.8 1.1 fusion.18
  118.8 0.6 copy.79
  119.5 1.3 copy.92
  120.9 1.5 copy.80
  122.5 1.8 multiply_add_fusion
  124.3 0.7 all-to-all-done.1
  125.0 4.1 %fusion.11 = bf16[2048,128]{1,0:T(8,128)(2,1)S(1)} fusion(bf16[2048,128]{1,0:T(8,128)(2,1)} %bitcast.7, s32[2048]{0:T(1024)S(1)} %copy-done.11), kind=kOutput, calls=%fused_computation.14 | convolution fusion | flops 1078198272 | bytes 1056768 | tf_op jit(solution)/shard_map/dot_general | solution.py:149
  129.2 3.8 %collective-permute-start = (bf16[2,128]{1,0:T(2,128)(2,1)S(1)}, bf16[2,128]{1,0:T(2,128)(2,1)S(1)}, u32[]{:S(2)}, u32[]{:S(2)}) collective-permute-start(bf16[2,128]{1,0:T(2,128)(2,1)S(1)} %get-tuple-element.9), channel_id=1, source_target_pairs={{0,1},{1,2},{2,3},{3,4},{4,5},{5,6},{6,7},{8,9},{9,10},{10,11},{11... | collective-permute-start | bytes 1544 | tf_op jit(solution)/shard_map/ppermute | solution.py:150
  132.9 0.1 pad_convert_fusion
  133.0 0.4 collective-permute-done
  133.6 5.6 %fusion.14 = bf16[2048,128]{1,0:T(8,128)(2,1)S(1)} fusion(s32[2048]{0:T(1024)S(1)} %copy-done.11, pred[2048]{0:T(1024)(128)(4,1)S(1)} %copy-done.30, pred[2048]{0:T(1024)(128)(4,1)S(1)} %copy-done.31, f32[2048,128]{1,0:T(8,128)S(1)} %copy-done, f32[2050,128]{1,0:T(8,128)S(1)} %pad_convert_fusion, f32[128]{0:T(128)S(1)} %copy-done.28, ...), kind=kOutput, calls=%fused_computation.17 | convolution fusion | flops 1081081856 | bytes 4749824 | tf_op jit(solution)/shard_map/dot_general | solution.py:161
  139.2 45.2 %all_to_all.15 = bf16[64,32,128]{2,1,0:T(8,128)(2,1)S(1)} all-to-all(bf16[64,32,128]{2,1,0:T(8,128)(2,1)S(1)} %bitcast.109), channel_id=1, replica_groups=mesh['ctx'=64,'ch'=8] {'ctx'}, dimensions={0} | all-to-all | bytes 1048576 | tf_op jit(solution)/shard_map/all_to_all | solution.py:164
  184.4 0.8 copy_bitcast_fusion.1
  (114 shorter events, 1.6 us)
Async XLA Ops:
  0.0 1.2 slice-start
  2.6 20.8 %copy-start.6 = (s32[16384]{0:T(1024)S(1)}, s32[16384]{0:T(1024)}, u32[]{:S(2)}) copy-start(s32[16384]{0:T(1024)} %param.8) | copy-start | bytes 196612
  2.6 20.9 %copy-start.36 = (s32[4]{0:T(128)S(1)}, s32[4]{0:T(128)}, u32[]{:S(2)}) copy-start(s32[4]{0:T(128)} %param.9) | copy-start | bytes 52
  4.1 20.5 %copy-start.12 = (f32[64,16]{0,1:T(8,128)S(1)}, f32[64,16]{0,1:T(8,128)}, u32[]{:S(2)}) copy-start(f32[64,16]{0,1:T(8,128)} %param.12) | copy-start | bytes 12292
  4.1 20.6 %copy-start.13 = (f32[64,16]{0,1:T(8,128)S(1)}, f32[64,16]{0,1:T(8,128)}, u32[]{:S(2)}) copy-start(f32[64,16]{0,1:T(8,128)} %param.11) | copy-start | bytes 12292
  4.1 20.8 %copy-start.7 = (f32[3,3,1024]{2,1,0:T(4,128)S(1)}, f32[3,3,1024]{2,1,0:T(4,128)}, u32[]{:S(2)}) copy-start(f32[3,3,1024]{2,1,0:T(4,128)} %param.10) | copy-start | bytes 110596
  4.1 20.8 %copy-start.26 = (f32[1024]{0:T(1024)S(1)}, f32[1024]{0:T(1024)}, u32[]{:S(2)}) copy-start(f32[1024]{0:T(1024)} %param.13) | copy-start | bytes 12292
  4.1 70.9 %all-to-all-start = ((bf16[64,32,256]{2,1,0:T(8,128)(2,1)}), bf16[64,32,256]{2,1,0:T(8,128)(2,1)S(1)}, u32[]{:S(2)}, u32[]{:S(2)}) async-start(bf16[64,32,256]{2,1,0:T(8,128)(2,1)} %reshape.316), calls=%async_computation | async-start | bytes 2097152 | tf_op jit(solution)/shard_map/all_to_all | solution.py:61
  24.6 50.4 %copy-start.10 = (s32[2048]{0:T(1024)}, s32[2048]{0:T(1024)S(1)}, u32[]{:S(2)}) copy-start(s32[2048]{0:T(1024)S(1)} %sub.77) | copy-start | bytes 24580
  42.8 50.7 %copy-start.2 = (f32[2048]{0:T(1024)}, f32[2048]{0:T(1024)S(1)}, u32[]{:S(2)}) copy-start(f32[2048]{0:T(1024)S(1)} %get-tuple-element.23) | copy-start | bytes 24580
  42.8 50.7 %copy-start.4 = (f32[2048]{0:T(1024)}, f32[2048]{0:T(1024)S(1)}, u32[]{:S(2)}) copy-start(f32[2048]{0:T(1024)S(1)} %get-tuple-element.24) | copy-start | bytes 24580
  46.6 47.0 %copy-start.14 = (f32[128]{0:T(128)}, f32[128]{0:T(128)S(1)}, u32[]{:S(2)}) copy-start(f32[128]{0:T(128)S(1)} %get-tuple-element.12) | copy-start | bytes 1540
  46.6 47.0 %copy-start.16 = (f32[128]{0:T(128)}, f32[128]{0:T(128)S(1)}, u32[]{:S(2)}) copy-start(f32[128]{0:T(128)S(1)} %get-tuple-element.13) | copy-start | bytes 1540
  46.6 47.0 %copy-start.18 = (f32[128]{0:T(128)}, f32[128]{0:T(128)S(1)}, u32[]{:S(2)}) copy-start(f32[128]{0:T(128)S(1)} %get-tuple-element.14) | copy-start | bytes 1540
  46.6 47.0 %copy-start.20 = (f32[128]{0:T(128)}, f32[128]{0:T(128)S(1)}, u32[]{:S(2)}) copy-start(f32[128]{0:T(128)S(1)} %get-tuple-element.15) | copy-start | bytes 1540
  46.6 47.0 %copy-start.22 = (f32[128]{0:T(128)}, f32[128]{0:T(128)S(1)}, u32[]{:S(2)}) copy-start(f32[128]{0:T(128)S(1)} %get-tuple-element.16) | copy-start | bytes 1540
  46.6 47.0 %copy-start.24 = (f32[128]{0:T(128)}, f32[128]{0:T(128)S(1)}, u32[]{:S(2)}) copy-start(f32[128]{0:T(128)S(1)} %get-tuple-element.19) | copy-start | bytes 1540
  75.0 10.9 %slice-start.1 = ((bf16[3,32,8192]{2,1,0:T(8,128)(2,1)}), bf16[1,32,8192]{2,1,0:T(8,128)(2,1)S(1)}, s32[]{:S(2)}) async-start(bf16[3,32,8192]{2,1,0:T(8,128)(2,1)} %param.7), calls=%async_computation.4 | async-start | bytes 1048576 | tf_op jit(solution)/shard_map/slice | solution.py:145
  78.2 15.1 %collective-permute-start.1 = (bf16[2,256]{1,0:T(2,128)(2,1)S(1)}, bf16[2,256]{1,0:T(2,128)(2,1)S(1)}, u32[]{:S(2)}, u32[]{:S(2)}) collective-permute-start(bf16[2,256]{1,0:T(2,128)(2,1)S(1)} %slice.196), channel_id=1, source_target_pairs={{0,1},{1,2},{2,3},{3,4},{4,5},{5,6},{6,7},{8,9},{9,10},{10,11},{11... | collective-permute-start | bytes 3080 | tf_op jit(solution)/shard_map/ppermute | solution.py:64
  87.3 37.7 %all-to-all-start.1 = ((bf16[64,32,128]{2,1,0:T(8,128)(2,1)}), bf16[64,32,128]{2,1,0:T(8,128)(2,1)}, u32[]{:S(2)}, u32[]{:S(2)}) async-start(bf16[64,32,128]{2,1,0:T(8,128)(2,1)} %copy.69), calls=%async_computation.1 | async-start | bytes 1048576 | tf_op jit(solution)/shard_map/all_to_all | solution.py:148
  100.6 15.0 %copy-start.9 = (pred[4,8,256]{2,1,0:T(8,128)(4,1)S(1)}, pred[4,8,256]{2,1,0:T(8,128)(4,1)}, u32[]{:S(2)}) copy-start(pred[4,8,256]{2,1,0:T(8,128)(4,1)} %iota_compare_fusion.15) | copy-start | bytes 24580
  114.6 1.3 copy-start.1
  114.7 1.6 copy-start.37
  116.2 1.5 copy-start.8
  116.2 1.5 copy-start.32
  119.5 3.0 %copy-start.3 = (f32[2048]{0:T(1024)S(1)}, f32[2048]{0:T(1024)}, u32[]{:S(2)}) copy-start(f32[2048]{0:T(1024)} %copy-done.2) | copy-start | bytes 24580
  119.5 3.0 %copy-start.5 = (f32[2048]{0:T(1024)S(1)}, f32[2048]{0:T(1024)}, u32[]{:S(2)}) copy-start(f32[2048]{0:T(1024)} %copy-done.4) | copy-start | bytes 24580
  119.5 3.0 %copy-start.15 = (f32[128]{0:T(128)S(1)}, f32[128]{0:T(128)}, u32[]{:S(2)}) copy-start(f32[128]{0:T(128)} %copy-done.14) | copy-start | bytes 1540
  119.5 3.0 %copy-start.17 = (f32[128]{0:T(128)S(1)}, f32[128]{0:T(128)}, u32[]{:S(2)}) copy-start(f32[128]{0:T(128)} %copy-done.16) | copy-start | bytes 1540
  119.5 3.0 %copy-start.19 = (f32[128]{0:T(128)S(1)}, f32[128]{0:T(128)}, u32[]{:S(2)}) copy-start(f32[128]{0:T(128)} %copy-done.18) | copy-start | bytes 1540
  119.5 3.0 %copy-start.21 = (f32[128]{0:T(128)S(1)}, f32[128]{0:T(128)}, u32[]{:S(2)}) copy-start(f32[128]{0:T(128)} %copy-done.20) | copy-start | bytes 1540
  119.5 3.0 %copy-start.23 = (f32[128]{0:T(128)S(1)}, f32[128]{0:T(128)}, u32[]{:S(2)}) copy-start(f32[128]{0:T(128)} %copy-done.22) | copy-start | bytes 1540
  119.5 3.0 %copy-start.25 = (f32[128]{0:T(128)S(1)}, f32[128]{0:T(128)}, u32[]{:S(2)}) copy-start(f32[128]{0:T(128)} %copy-done.24) | copy-start | bytes 1540
  119.5 3.0 %copy-start.33 = (f32[128]{0:T(128)S(1)}, f32[128]{0:T(128)}, u32[]{:S(2)}) copy-start(f32[128]{0:T(128)} %dynamic_slice.19) | copy-start | bytes 1540
  122.5 2.5 %copy-start.11 = (s32[2048]{0:T(1024)S(1)}, s32[2048]{0:T(1024)}, u32[]{:S(2)}) copy-start(s32[2048]{0:T(1024)} %copy-done.10) | copy-start | bytes 24580
  125.0 8.4 %copy-start = (f32[2048,128]{1,0:T(8,128)S(1)}, f32[2048,128]{1,0:T(8,128)}, u32[]{:S(2)}) copy-start(f32[2048,128]{1,0:T(8,128)} %multiply_add_fusion) | copy-start | bytes 3145732
  125.0 8.4 %copy-start.27 = (f32[128]{0:T(128)S(1)}, f32[128]{0:T(128)}, u32[]{:S(2)}) copy-start(f32[128]{0:T(128)} %get-tuple-element.11) | copy-start | bytes 1540
  125.0 8.5 %copy-start.28 = (f32[128]{0:T(128)S(1)}, f32[128]{0:T(128)}, u32[]{:S(2)}) copy-start(f32[128]{0:T(128)} %get-tuple-element.17) | copy-start | bytes 1540
  125.0 8.5 %copy-start.29 = (f32[128]{0:T(128)S(1)}, f32[128]{0:T(128)}, u32[]{:S(2)}) copy-start(f32[128]{0:T(128)} %get-tuple-element.18) | copy-start | bytes 1540
  125.0 8.5 %copy-start.34 = (f32[2]{0:T(128)S(1)}, f32[2]{0:T(128)}, u32[]{:S(2)}) copy-start(f32[2]{0:T(128)} %slice.195) | copy-start | bytes 28
  125.0 8.5 %copy-start.35 = (f32[2]{0:T(128)S(1)}, f32[2]{0:T(128)}, u32[]{:S(2)}) copy-start(f32[2]{0:T(128)} %slice.193) | copy-start | bytes 28
  125.0 8.5 %copy-start.30 = (pred[2048]{0:T(1024)(128)(4,1)S(1)}, pred[2048]{0:T(1024)(128)(4,1)}, u32[]{:S(2)}) copy-start(pred[2048]{0:T(1024)(128)(4,1)} %get-tuple-element.39) | copy-start | bytes 6148
  125.0 8.5 %copy-start.31 = (pred[2048]{0:T(1024)(128)(4,1)S(1)}, pred[2048]{0:T(1024)(128)(4,1)}, u32[]{:S(2)}) copy-start(pred[2048]{0:T(1024)(128)(4,1)} %get-tuple-element.40) | copy-start | bytes 6148
  129.2 4.2 %collective-permute-start = (bf16[2,128]{1,0:T(2,128)(2,1)S(1)}, bf16[2,128]{1,0:T(2,128)(2,1)S(1)}, u32[]{:S(2)}, u32[]{:S(2)}) collective-permute-start(bf16[2,128]{1,0:T(2,128)(2,1)S(1)} %get-tuple-element.9), channel_id=1, source_target_pairs={{0,1},{1,2},{2,3},{3,4},{4,5},{5,6},{6,7},{8,9},{9,10},{10,11},{11... | collective-permute-start | bytes 1544 | tf_op jit(solution)/shard_map/ppermute | solution.py:150

commit v7 on v4

--- a/solution.py
+++ b/solution.py
@@ -2,6 +2,7 @@
 import jax.numpy as jnp
 from jax import lax
 from jax.sharding import PartitionSpec as P
+
 
 highest = lax.Precision.HIGHEST
 
@@ -11,12 +12,12 @@
     return jnp.where(positions >= 0, found, -1)
 
 
-def shards(projections, attention_order, doc_lengths, short_filter, decay_rate, residue, skip_gain):
+def layer(projections, attention_order, doc_lengths, short_filter, decay_rate, residue, skip_gain):
     n_ctx = lax.axis_size("ctx")
     n_ch = lax.axis_size("ch")
     here_ctx = lax.axis_index("ctx")
     here_ch = lax.axis_index("ch")
-    feeds, rows_here, channels = projections.shape
+    _, rows_here, channels = projections.shape
     tokens = attention_order.shape[0]
     block = tokens // n_ctx
     slot = block // n_ctx
@@ -58,10 +59,12 @@
         count = part.shape[0]
         sending = jnp.transpose(part.reshape(count, rows_here, n_ctx, width), (2, 1, 0, 3))
         sending = sending.reshape(n_ctx, rows_here, count * width)
-        received = lax.all_to_all(sending, "ctx", 0, 0, tiled=True).reshape(n_ctx * rows_here, count * width)
+        received = lax.all_to_all(sending, "ctx", 0, 0, tiled=True)
+        received = received.reshape(n_ctx * rows_here, count * width)
         arrived.append(received)
         ordered = jnp.dot(placer, received, preferred_element_type=jnp.float32).astype(jnp.bfloat16)
-        earlier = lax.ppermute(ordered[span - 2 :, :], "ch", [(i, i + 1) for i in range(n_ch - 1)])
+        tail = jnp.dot(placer[span - 2 :], received, preferred_element_type=jnp.float32).astype(jnp.bfloat16)
+        earlier = lax.ppermute(tail, "ch", [(i, i + 1) for i in range(n_ch - 1)])
         widened = jnp.concatenate([earlier, ordered], axis=0).astype(jnp.float32)
         return [widened[:, p * width : (p + 1) * width] for p in range(count)]
 
@@ -161,6 +164,4 @@
         P("ch", None),
         P("ch"),
     )
-    return jax.shard_map(
-        shards, mesh=mesh, in_specs=placed, out_specs=P(("ctx", "ch"), None), check_vma=False
-    )
+    return jax.shard_map(layer, mesh=mesh, in_specs=placed, out_specs=P(("ctx", "ch"), None), check_vma=False)

time: 180 us -> 179 us (level)
  waiting for transfers between devices: 38.9 us -> 30.1 us
  other arithmetic: 6.76 us -> 12.4 us
    all_to_all x2, waiting for transfers between devices: 38.9 us -> 30.1 us  [arrive(): received = lax.all_to_all(sending, 'ctx', 0, 0, tiled=True)]
    eq x1 -> x2, other arithmetic: 0.01 us -> 5.67 us  [the longest x1 5.66 us: layer(): (mine - here_ch * span)[None, :]]
    dot_general x5 -> x7, matrix products: 13.5 us -> 15.3 us  [the longest x1 5.22 us: layer(): jnp.dot(placer.T, mixed, preferred_element_type=jnp.float32)]
  transfers between devices with their start and end apart: 4 -> 4, of which waited for: 2 -> 2; matrix products, arithmetic and copies ran while one was open for 11% -> 17% of each run, Pallas kernels for 0% -> 0%
where the time goes in v7:
time: 179 us; the launch traced here: 178 us
  blocking collectives  65.7 us (37%)
  starting transfers between devices  36.3 us (20%)
  waiting for transfers between devices  30.1 us (17%)
  matrix products  21.5 us (12%)
  other arithmetic  12.4 us (7%)
  local copies, waits for them, and re-layouts  11.7 us (7%)
    all_to_all x1, blocking collectives, layer(): lax.all_to_all(back.reshape(n_ctx, rows_here, width), 'ctx', 0, 0, tiled=...  38.4 us
    all_to_all x2, waiting for transfers between devices, arrive(): received = lax.all_to_all(sending, 'ctx', 0, 0, tiled=True)  30.1 us
    all_to_all x2, starting transfers between devices, arrive(): received = lax.all_to_all(sending, 'ctx', 0, 0, tiled=True)  24.6 us
    all_gather x1, blocking collectives, layer(): every = lax.all_gather(flat, 'ch')  14.5 us
    all_gather x1, blocking collectives, layer(): gathered = lax.all_gather(local_state[chunks - 1], 'ch')  12.8 us
    ppermute x2, starting transfers between devices, arrive(): earlier = lax.ppermute(tail, 'ch', [(i, i + 1) for i in range(n_ch - 1)])  11.6 us
    dot_general x2, matrix products, arrive(): jnp.dot(placer, received, preferred_element_type=jnp.float32)  6.16 us
    eq x1, other arithmetic, layer(): (mine - here_ch * span)[None, :]  5.66 us
  transfers between devices with their start and end apart: 4, of which 2 were waited for; matrix products, arithmetic and copies ran while one was open for 17% of the time, Pallas kernels for 0%

profile of v7, /device:TPU:1, one launch (start us, length us, event | category | flops | bytes accessed | tf_op | source)
XLA Modules:
  0.0 178.2 jit_solution(140306423654421584)
XLA Ops:
  0.0 1.3 slice.113
  1.4 0.3 copy.89
  1.6 1.1 copy.99
  2.7 1.5 reshape.300
  4.2 19.1 %all-to-all-start = ((bf16[64,32,256]{2,1,0:T(8,128)(2,1)}), bf16[64,32,256]{2,1,0:T(8,128)(2,1)S(1)}, u32[]{:S(2)}, u32[]{:S(2)}) async-start(bf16[64,32,256]{2,1,0:T(8,128)(2,1)} %reshape.300), calls=%async_computation | async-start | bytes 2097152 | tf_op jit(solution)/shard_map/all_to_all | solution.py:62
  23.4 0.2 reduce-window.8
  23.6 0.1 convert_reduce_fusion
  23.8 0.2 slice_reduce_fusion.1
  23.9 0.1 copy.66
  24.0 0.1 reshape.295
  24.1 0.1 copy.67
  24.2 0.1 reshape.296
  24.4 14.5 %all-gather = f32[98304]{0:T(1024)S(1)} all-gather(f32[12288]{0:T(1024)S(1)} %pad_maximum_fusion), channel_id=2, replica_groups=mesh['ctx'=64,'ch'=8] {'ch'}, dimensions={0}, use_global_device_ids=true | all-gather | bytes 442368 | tf_op jit(solution)/shard_map/all_gather | solution.py:37
  38.8 0.1 reshape.313
  38.9 0.1 reshape.308
  39.1 0.1 reshape.307
  39.2 0.1 dynamic-slice_subtract_fusion
  39.3 0.6 slice.160
  40.0 0.2 reshape.298
  40.2 0.1 convert_reduce_fusion.1
  40.3 0.7 compare_convert_fusion.2
  41.0 0.1 exponential_multiply_fusion
  41.1 0.1 dynamic_slice.19
  41.2 0.2 slice_reduce_fusion
  41.3 0.7 pad_add_fusion
  42.1 0.1 fusion.68
  42.5 0.2 exponential_select_fusion
  42.7 3.0 %subtract_convert_fusion = (bf16[8,256,256]{1,2,0:T(8,128)(2,1)}, bf16[8,256,256]{1,2,0:T(8,128)(2,1)S(1)}) fusion(pred[256,256]{0,1:T(8,128)(4,1)S(1)} %iota_compare_fusion.10, f32[8,16]{1,0:T(8,128)S(1)} %get-tuple-element.8, f32[8,16]{1,0:T(8,128)S(1)} %neg.12, f32[8,16]{1,0:T(8,128)S(1)} %get-tuple-element.7), kind=kOutput, calls=%fused_computation.19 | convolution fusion | flops 103907328 | bytes 2164224 | tf_op jit(solution)/shard_map/gtm,gms->gts/dot_general | solution.py:94
  45.7 1.2 select_convert_fusion
  46.9 5.7 %iota_compare_fusion = pred[2048,2048]{1,0:T(8,128)(4,1)} fusion(s32[2048]{0:T(1024)S(1)} %sub.68), kind=kLoop, calls=%fused_computation | loop fusion | flops 4194304 | bytes 4202496 | tf_op jit(solution)/shard_map/eq | solution.py:53
  52.6 22.4 %all-to-all-done = bf16[64,32,256]{2,1,0:T(8,128)(2,1)S(1)} async-done(((bf16[64,32,256]{2,1,0:T(8,128)(2,1)}), bf16[64,32,256]{2,1,0:T(8,128)(2,1)S(1)}, u32[]{:S(2)}, u32[]{:S(2)}) %all-to-all-start) | async-done | bytes 1048608 | tf_op jit(solution)/shard_map/all_to_all | solution.py:62
  75.0 3.2 %fusion.10 = bf16[2048,256]{1,0:T(8,128)(2,1)S(1)} fusion(bf16[2048,256]{1,0:T(8,128)(2,1)S(1)} %bitcast.96, s32[2048]{0:T(1024)S(1)} %sub.68), kind=kOutput, calls=%fused_computation.13 | convolution fusion | flops 2152202240 | bytes 2105344 | tf_op jit(solution)/shard_map/dot_general | solution.py:65
  78.2 0.1 copy.91
  78.3 1.0 convolution_convert_fusion
  79.3 7.7 %collective-permute-start.1 = (bf16[2,256]{1,0:T(2,128)(2,1)S(1)}, bf16[2,256]{1,0:T(2,128)(2,1)S(1)}, u32[]{:S(2)}, u32[]{:S(2)}) collective-permute-start(bf16[2,256]{1,0:T(2,128)(2,1)S(1)} %convolution_convert_fusion), channel_id=1, source_target_pairs={{0,1},{1,2},{2,3},{3,4},{4,5},{5,6},{6,7},{8,9},{9,10},{10,11},{11... | collective-permute-start | bytes 3080 | tf_op jit(solution)/shard_map/ppermute | solution.py:67
  87.0 1.1 copy.69
  88.2 5.5 %all-to-all-start.1 = ((bf16[64,32,128]{2,1,0:T(8,128)(2,1)}), bf16[64,32,128]{2,1,0:T(8,128)(2,1)S(1)}, u32[]{:S(2)}, u32[]{:S(2)}) async-start(bf16[64,32,128]{2,1,0:T(8,128)(2,1)} %copy.69), calls=%async_computation.1 | async-start | bytes 1048576 | tf_op jit(solution)/shard_map/all_to_all | solution.py:62
  93.7 0.2 maximum_convert_fusion
  93.9 0.9 fusion.20
  94.9 0.2 copy.70
  95.1 0.1 copy.90
  95.2 0.1 convert_multiply_fusion
  95.3 0.1 copy.71
  95.4 1.3 convolution_bitcast_fusion
  96.7 0.2 copy.75
  96.9 1.3 multiply_reduce_fusion
  98.3 0.2 copy.87
  98.5 12.8 %all_gather.11 = f32[8,8,16,16]{3,2,1,0:T(8,128)S(1)} all-gather(f32[1,8,16,16]{3,2,1,0:T(8,128)S(1)} %slice.162), channel_id=1, replica_groups=mesh['ctx'=64,'ch'=8] {'ch'}, dimensions={0}, use_global_device_ids=true | all-gather | bytes 73728 | tf_op jit(solution)/shard_map/all_gather | solution.py:126
  111.3 0.2 multiply_reduce_fusion.1
  111.5 0.1 copy.76
  111.6 0.2 broadcast_select_fusion
  111.8 2.9 %select_reduce_fusion = f32[8,8,16,256]{3,2,1,0:T(8,128)S(1)} fusion(pred[4,8,256]{2,1,0:T(8,128)(4,1)S(1)} %iota_compare_fusion.11, bf16[8,256,256]{1,2,0:T(8,128)(2,1)} %get-tuple-element.27, bf16[8,256,256]{1,2,0:T(8,128)(2,1)} %select_convert_fusion, bf16[4,8,256,8,16]{2,4,1,0,3:T(8,128)(2,1)S(1)} %broadcast_select_fusion), kind=kOutput, calls=%fused_computation.12 | convolution fusion | flops 1088159744 | bytes 5251072 | tf_op jit(solution)/shard_map/gts,dksgc->dktgc/dot_general | solution.py:105
  114.7 1.1 fusion.16
  115.7 0.6 copy.79
  116.4 0.3 copy.92
  116.7 1.3 copy.80
  118.0 7.7 %all-to-all-done.1 = bf16[64,32,128]{2,1,0:T(8,128)(2,1)S(1)} async-done(((bf16[64,32,128]{2,1,0:T(8,128)(2,1)}), bf16[64,32,128]{2,1,0:T(8,128)(2,1)S(1)}, u32[]{:S(2)}, u32[]{:S(2)}) %all-to-all-start.1) | async-done | bytes 524320 | tf_op jit(solution)/shard_map/all_to_all | solution.py:62
  125.7 0.9 convolution_convert_fusion.1
  126.6 3.9 %collective-permute-start = (bf16[2,128]{1,0:T(2,128)(2,1)S(1)}, bf16[2,128]{1,0:T(2,128)(2,1)S(1)}, u32[]{:S(2)}, u32[]{:S(2)}) collective-permute-start(bf16[2,128]{1,0:T(2,128)(2,1)S(1)} %convolution_convert_fusion.1), channel_id=1, source_target_pairs={{0,1},{1,2},{2,3},{3,4},{4,5},{5,6},{6,7},{8,9},{9,10},{10,11},{11... | collective-permute-start | bytes 1544 | tf_op jit(solution)/shard_map/ppermute | solution.py:67
  130.6 3.0 %fusion.11 = bf16[2048,128]{1,0:T(8,128)(2,1)S(1)} fusion(bf16[2048,128]{1,0:T(8,128)(2,1)S(1)} %bitcast.105, s32[2048]{0:T(1024)S(1)} %sub.68), kind=kOutput, calls=%fused_computation.14 | convolution fusion | flops 1078198272 | bytes 1056768 | tf_op jit(solution)/shard_map/dot_general | solution.py:65
  133.6 0.1 maximum_convert_fusion.1
  133.7 5.2 %fusion.12 = bf16[2048,128]{1,0:T(8,128)(2,1)S(1)} fusion(s32[2048]{0:T(1024)S(1)} %sub.68, f32[2050,128]{1,0:T(8,128)S(1)} %maximum_convert_fusion.1, f32[2048,128]{1,0:T(8,128)S(1)} %copy-done, bf16[2048,128]{1,0:T(8,128)(2,1)S(1)} %fusion.20, f32[128]{0:T(128)S(1)} %dynamic_slice.19, f32[2048]{0:T(1024)S(1)} %get-tuple-element.22, ...), kind=kOutput, calls=%fused_computation.15 | convolution fusion | flops 1081344000 | bytes 5269504 | tf_op jit(solution)/shard_map/dot_general | solution.py:152
  138.9 38.4 %all_to_all.15 = bf16[64,32,128]{2,1,0:T(8,128)(2,1)S(1)} all-to-all(bf16[64,32,128]{2,1,0:T(8,128)(2,1)S(1)} %bitcast.110), channel_id=1, replica_groups=mesh['ctx'=64,'ch'=8] {'ctx'}, dimensions={0} | all-to-all | bytes 1048576 | tf_op jit(solution)/shard_map/all_to_all | solution.py:153
  177.3 0.8 copy_bitcast_fusion.1
  (46 shorter events, 0.8 us)
Async XLA Ops:
  1.3 22.1 %copy-start.6 = (s32[4]{0:T(128)S(1)}, s32[4]{0:T(128)}, u32[]{:S(2)}) copy-start(s32[4]{0:T(128)} %param.9) | copy-start | bytes 52
  1.3 22.6 %copy-start.3 = (f32[64,16]{0,1:T(8,128)S(1)}, f32[64,16]{0,1:T(8,128)}, u32[]{:S(2)}) copy-start(f32[64,16]{0,1:T(8,128)} %param.11) | copy-start | bytes 12292
  1.3 22.8 %copy-start.4 = (f32[64,16]{0,1:T(8,128)S(1)}, f32[64,16]{0,1:T(8,128)}, u32[]{:S(2)}) copy-start(f32[64,16]{0,1:T(8,128)} %param.12) | copy-start | bytes 12292
  1.3 22.9 %copy-start.2 = (f32[3,3,1024]{2,1,0:T(4,128)S(1)}, f32[3,3,1024]{2,1,0:T(4,128)}, u32[]{:S(2)}) copy-start(f32[3,3,1024]{2,1,0:T(4,128)} %param.10) | copy-start | bytes 110596
  1.3 23.0 %copy-start.1 = (s32[16384]{0:T(1024)S(1)}, s32[16384]{0:T(1024)}, u32[]{:S(2)}) copy-start(s32[16384]{0:T(1024)} %param.8) | copy-start | bytes 196612
  1.4 23.0 %copy-start.5 = (f32[1024]{0:T(1024)S(1)}, f32[1024]{0:T(1024)}, u32[]{:S(2)}) copy-start(f32[1024]{0:T(1024)} %param.13) | copy-start | bytes 12292
  4.2 70.7 %all-to-all-start = ((bf16[64,32,256]{2,1,0:T(8,128)(2,1)}), bf16[64,32,256]{2,1,0:T(8,128)(2,1)S(1)}, u32[]{:S(2)}, u32[]{:S(2)}) async-start(bf16[64,32,256]{2,1,0:T(8,128)(2,1)} %reshape.300), calls=%async_computation | async-start | bytes 2097152 | tf_op jit(solution)/shard_map/all_to_all | solution.py:62
  75.0 3.2 %slice-start = ((bf16[3,32,8192]{2,1,0:T(8,128)(2,1)}), bf16[1,32,8192]{2,1,0:T(8,128)(2,1)S(1)}, s32[]{:S(2)}) async-start(bf16[3,32,8192]{2,1,0:T(8,128)(2,1)} %param.7), calls=%async_computation.3 | async-start | bytes 1048576 | tf_op jit(solution)/shard_map/slice | solution.py:148
  79.3 14.5 %collective-permute-start.1 = (bf16[2,256]{1,0:T(2,128)(2,1)S(1)}, bf16[2,256]{1,0:T(2,128)(2,1)S(1)}, u32[]{:S(2)}, u32[]{:S(2)}) collective-permute-start(bf16[2,256]{1,0:T(2,128)(2,1)S(1)} %convolution_convert_fusion), channel_id=1, source_target_pairs={{0,1},{1,2},{2,3},{3,4},{4,5},{5,6},{6,7},{8,9},{9,10},{10,11},{11... | collective-permute-start | bytes 3080 | tf_op jit(solution)/shard_map/ppermute | solution.py:67
  88.2 37.6 %all-to-all-start.1 = ((bf16[64,32,128]{2,1,0:T(8,128)(2,1)}), bf16[64,32,128]{2,1,0:T(8,128)(2,1)S(1)}, u32[]{:S(2)}, u32[]{:S(2)}) async-start(bf16[64,32,128]{2,1,0:T(8,128)(2,1)} %copy.69), calls=%async_computation.1 | async-start | bytes 1048576 | tf_op jit(solution)/shard_map/all_to_all | solution.py:62
  126.6 7.0 %copy-start = (f32[2048,128]{1,0:T(8,128)S(1)}, f32[2048,128]{1,0:T(8,128)}, u32[]{:S(2)}) copy-start(f32[2048,128]{1,0:T(8,128)} %copy.80) | copy-start | bytes 3145732
  126.6 6.9 %collective-permute-start = (bf16[2,128]{1,0:T(2,128)(2,1)S(1)}, bf16[2,128]{1,0:T(2,128)(2,1)S(1)}, u32[]{:S(2)}, u32[]{:S(2)}) collective-permute-start(bf16[2,128]{1,0:T(2,128)(2,1)S(1)} %convolution_convert_fusion.1), channel_id=1, source_target_pairs={{0,1},{1,2},{2,3},{3,4},{4,5},{5,6},{6,7},{8,9},{9,10},{10,11},{11... | collective-permute-start | bytes 1544 | tf_op jit(solution)/shard_map/ppermute | solution.py:67

commit v8 on v7

--- a/solution.py
+++ b/solution.py
@@ -55,10 +55,13 @@
 
     arrived = []
 
-    def arrive(part):
+    def outgoing(part):
         count = part.shape[0]
         sending = jnp.transpose(part.reshape(count, rows_here, n_ctx, width), (2, 1, 0, 3))
-        sending = sending.reshape(n_ctx, rows_here, count * width)
+        return sending.reshape(n_ctx, rows_here, count * width)
+
+    def arrive(sending):
+        count = sending.shape[2] // width
         received = lax.all_to_all(sending, "ctx", 0, 0, tiled=True)
         received = received.reshape(n_ctx * rows_here, count * width)
         arrived.append(received)
@@ -81,7 +84,7 @@
             + sf[p, 2, None, :] * rows[0:span] * keep_two
         )
 
-    key_rows, value_rows = arrive(projections[1:3])
+    key_rows, value_rows = arrive(outgoing(projections[1:3]))
     featured_key = feature(1, key_rows)
     featured_value = feature(2, value_rows)
     gated = (featured_key * featured_value).astype(jnp.bfloat16)
@@ -145,8 +148,8 @@
 
     gated32 = gated.astype(jnp.float32)
     combined = filtered.reshape(span, width) + skip[None, :] * gated32
-    _, query_part = lax.optimization_barrier((arrived[0], projections[0:1]))
-    (query_rows,) = arrive(query_part)
+    _, query_sending = lax.optimization_barrier((arrived[0], outgoing(projections[0:1])))
+    (query_rows,) = arrive(query_sending)
     mixed = (feature(0, query_rows) * combined).astype(jnp.bfloat16)
 
     back = jnp.dot(placer.T, mixed, preferred_element_type=jnp.float32).astype(jnp.bfloat16)

time: 179 us -> 179 us (level)
  waiting for transfers between devices: 30.1 us -> 27.8 us
    all_to_all x2, waiting for transfers between devices: 30.1 us -> 27.8 us  [arrive(): received = lax.all_to_all(sending, 'ctx', 0, 0, tiled=True)]
    reshape x4 -> x3, local copies, waits for them, and re-layouts: 3.77 us -> 2.62 us  [the longest x2 1.54 us: outgoing(): return sending.reshape(n_ctx, rows_here, count * width)]
  transfers between devices with their start and end apart: 4 -> 4, of which waited for: 2 -> 2; matrix products, arithmetic and copies ran while one was open for 17% -> 20% of each run, Pallas kernels for 0% -> 0%
where the time goes in v8:
time: 179 us; the launch traced here: 178 us
  blocking collectives  65.7 us (37%)
  starting transfers between devices  36.3 us (20%)
  waiting for transfers between devices  27.8 us (16%)
  matrix products  21.2 us (12%)
  other arithmetic  13.5 us (8%)
  local copies, waits for them, and re-layouts  12.9 us (7%)
    all_to_all x1, blocking collectives, layer(): lax.all_to_all(back.reshape(n_ctx, rows_here, width), 'ctx', 0, 0, tiled=...  38.5 us
    all_to_all x2, waiting for transfers between devices, arrive(): received = lax.all_to_all(sending, 'ctx', 0, 0, tiled=True)  27.8 us
    all_to_all x2, starting transfers between devices, arrive(): received = lax.all_to_all(sending, 'ctx', 0, 0, tiled=True)  24.7 us
    all_gather x1, blocking collectives, layer(): every = lax.all_gather(flat, 'ch')  14.3 us
    all_gather x1, blocking collectives, layer(): gathered = lax.all_gather(local_state[chunks - 1], 'ch')  12.9 us
    ppermute x2, starting transfers between devices, arrive(): earlier = lax.ppermute(tail, 'ch', [(i, i + 1) for i in range(n_ch - 1)])  11.6 us
    dot_general x2, matrix products, arrive(): jnp.dot(placer, received, preferred_element_type=jnp.float32)  6.15 us
    eq x1, other arithmetic, layer(): (mine - here_ch * span)[None, :]  5.66 us
  transfers between devices with their start and end apart: 4, of which 2 were waited for; matrix products, arithmetic and copies ran while one was open for 20% of the time, Pallas kernels for 0%

profile of v8, /device:TPU:1, one launch (start us, length us, event | category | flops | bytes accessed | tf_op | source)
XLA Modules:
  0.0 178.1 jit_solution(6807830696681641651)
XLA Ops:
  0.0 1.3 slice.113
  1.4 0.3 copy.89
  1.6 1.1 copy.99
  2.7 1.5 reshape.300
  4.2 19.1 %all-to-all-start = ((bf16[64,32,256]{2,1,0:T(8,128)(2,1)}), bf16[64,32,256]{2,1,0:T(8,128)(2,1)S(1)}, u32[]{:S(2)}, u32[]{:S(2)}) async-start(bf16[64,32,256]{2,1,0:T(8,128)(2,1)} %reshape.300), calls=%async_computation | async-start | bytes 2097152 | tf_op jit(solution)/shard_map/all_to_all | solution.py:65
  23.4 0.2 reduce-window.8
  23.6 0.1 convert_reduce_fusion
  23.7 0.6 slice.160
  24.3 0.1 copy.66
  24.4 0.1 reshape.295
  24.5 0.1 copy.67
  24.7 14.3 %all-gather = f32[98304]{0:T(1024)S(1)} all-gather(f32[12288]{0:T(1024)S(1)} %pad_maximum_fusion), channel_id=2, replica_groups=mesh['ctx'=64,'ch'=8] {'ch'}, dimensions={0}, use_global_device_ids=true | all-gather | bytes 442368 | tf_op jit(solution)/shard_map/all_gather | solution.py:37
  39.1 0.1 convert_reduce_fusion.1
  39.2 0.2 slice_reduce_fusion.1
  39.5 0.1 dynamic-slice_subtract_fusion
  39.6 0.2 reshape.298
  39.8 0.1 reshape.308
  40.0 0.1 reshape.307
  40.1 0.7 compare_convert_fusion.2
  40.8 0.1 exponential_multiply_fusion
  40.9 1.1 slice_bitcast_fusion
  42.0 0.1 copy.91
  42.1 0.6 dynamic_slice.19
  42.8 0.2 slice_reduce_fusion
  42.9 0.7 pad_add_fusion
  43.7 0.6 iota_subtract_fusion
  44.2 0.5 iota_add_fusion.1
  44.8 0.7 fusion.68
  45.8 0.2 exponential_select_fusion
  46.0 3.1 %subtract_convert_fusion = (bf16[8,256,256]{1,2,0:T(8,128)(2,1)}, bf16[8,256,256]{1,2,0:T(8,128)(2,1)S(1)}) fusion(pred[256,256]{0,1:T(8,128)(4,1)S(1)} %iota_compare_fusion.10, f32[8,16]{1,0:T(8,128)S(1)} %get-tuple-element.8, f32[8,16]{1,0:T(8,128)S(1)} %neg.12, f32[8,16]{1,0:T(8,128)S(1)} %get-tuple-element.7), kind=kOutput, calls=%fused_computation.19 | convolution fusion | flops 103907328 | bytes 2164224 | tf_op jit(solution)/shard_map/gtm,gms->gts/dot_general | solution.py:97
  49.1 1.2 select_convert_fusion
  50.3 5.7 %iota_compare_fusion = pred[2048,2048]{1,0:T(8,128)(4,1)} fusion(s32[2048]{0:T(1024)S(1)} %sub.68), kind=kLoop, calls=%fused_computation | loop fusion | flops 4194304 | bytes 4202496 | tf_op jit(solution)/shard_map/eq | solution.py:53
  56.0 19.0 %all-to-all-done = bf16[64,32,256]{2,1,0:T(8,128)(2,1)S(1)} async-done(((bf16[64,32,256]{2,1,0:T(8,128)(2,1)}), bf16[64,32,256]{2,1,0:T(8,128)(2,1)S(1)}, u32[]{:S(2)}, u32[]{:S(2)}) %all-to-all-start) | async-done | bytes 1048608 | tf_op jit(solution)/shard_map/all_to_all | solution.py:65
  75.0 1.0 convolution_convert_fusion
  75.9 7.9 %collective-permute-start.1 = (bf16[2,256]{1,0:T(2,128)(2,1)S(1)}, bf16[2,256]{1,0:T(2,128)(2,1)S(1)}, u32[]{:S(2)}, u32[]{:S(2)}) collective-permute-start(bf16[2,256]{1,0:T(2,128)(2,1)S(1)} %convolution_convert_fusion), channel_id=1, source_target_pairs={{0,1},{1,2},{2,3},{3,4},{4,5},{5,6},{6,7},{8,9},{9,10},{10,11},{11... | collective-permute-start | bytes 3080 | tf_op jit(solution)/shard_map/ppermute | solution.py:70
  83.8 3.2 %fusion.10 = bf16[2048,256]{1,0:T(8,128)(2,1)S(1)} fusion(bf16[2048,256]{1,0:T(8,128)(2,1)S(1)} %bitcast.98, s32[2048]{0:T(1024)S(1)} %sub.68), kind=kOutput, calls=%fused_computation.13 | convolution fusion | flops 2152202240 | bytes 2105344 | tf_op jit(solution)/shard_map/dot_general | solution.py:68
  87.0 1.1 copy.69
  88.1 5.6 %all-to-all-start.1 = ((bf16[64,32,128]{2,1,0:T(8,128)(2,1)}), bf16[64,32,128]{2,1,0:T(8,128)(2,1)S(1)}, u32[]{:S(2)}, u32[]{:S(2)}) async-start(bf16[64,32,128]{2,1,0:T(8,128)(2,1)} %copy.69), calls=%async_computation.1 | async-start | bytes 1048576 | tf_op jit(solution)/shard_map/all_to_all | solution.py:65
  93.7 0.2 maximum_convert_fusion
  93.9 0.9 fusion.20
  94.9 0.2 copy.70
  95.1 0.1 copy.90
  95.2 0.1 convert_multiply_fusion
  95.3 0.1 copy.71
  95.5 1.3 convolution_bitcast_fusion
  96.8 0.2 copy.75
  97.0 1.3 multiply_reduce_fusion
  98.3 0.2 copy.87
  98.5 12.9 %all_gather.11 = f32[8,8,16,16]{3,2,1,0:T(8,128)S(1)} all-gather(f32[1,8,16,16]{3,2,1,0:T(8,128)S(1)} %slice.162), channel_id=1, replica_groups=mesh['ctx'=64,'ch'=8] {'ch'}, dimensions={0}, use_global_device_ids=true | all-gather | bytes 73728 | tf_op jit(solution)/shard_map/all_gather | solution.py:129
  111.4 0.2 multiply_reduce_fusion.1
  111.8 0.2 broadcast_select_fusion
  111.9 2.6 %select_reduce_fusion = f32[8,8,16,256]{3,2,1,0:T(8,128)S(1)} fusion(pred[4,8,256]{2,1,0:T(8,128)(4,1)S(1)} %iota_compare_fusion.11, bf16[8,256,256]{1,2,0:T(8,128)(2,1)} %get-tuple-element.27, bf16[8,256,256]{1,2,0:T(8,128)(2,1)S(1)} %copy-done, bf16[4,8,256,8,16]{2,4,1,0,3:T(8,128)(2,1)S(1)} %broadcast_select_fusion), kind=kOutput, calls=%fused_computation.12 | convolution fusion | flops 1088159744 | bytes 5251072 | tf_op jit(solution)/shard_map/gts,dksgc->dktgc/dot_general | solution.py:108
  114.5 1.1 fusion.16
  115.6 0.6 copy.79
  116.2 0.3 copy.92
  116.6 0.3 copy.80
  116.9 8.8 %all-to-all-done.1 = bf16[64,32,128]{2,1,0:T(8,128)(2,1)S(1)} async-done(((bf16[64,32,128]{2,1,0:T(8,128)(2,1)}), bf16[64,32,128]{2,1,0:T(8,128)(2,1)S(1)}, u32[]{:S(2)}, u32[]{:S(2)}) %all-to-all-start.1) | async-done | bytes 524320 | tf_op jit(solution)/shard_map/all_to_all | solution.py:65
  125.7 0.9 convolution_convert_fusion.1
  126.7 3.7 %collective-permute-start = (bf16[2,128]{1,0:T(2,128)(2,1)S(1)}, bf16[2,128]{1,0:T(2,128)(2,1)S(1)}, u32[]{:S(2)}, u32[]{:S(2)}) collective-permute-start(bf16[2,128]{1,0:T(2,128)(2,1)S(1)} %convolution_convert_fusion.1), channel_id=1, source_target_pairs={{0,1},{1,2},{2,3},{3,4},{4,5},{5,6},{6,7},{8,9},{9,10},{10,11},{11... | collective-permute-start | bytes 1544 | tf_op jit(solution)/shard_map/ppermute | solution.py:70
  130.4 3.0 %fusion.11 = bf16[2048,128]{1,0:T(8,128)(2,1)S(1)} fusion(bf16[2048,128]{1,0:T(8,128)(2,1)S(1)} %bitcast.105, s32[2048]{0:T(1024)S(1)} %sub.68), kind=kOutput, calls=%fused_computation.14 | convolution fusion | flops 1078198272 | bytes 1056768 | tf_op jit(solution)/shard_map/dot_general | solution.py:68
  133.4 0.1 maximum_convert_fusion.1
  133.6 5.2 %fusion.12 = bf16[2048,128]{1,0:T(8,128)(2,1)S(1)} fusion(s32[2048]{0:T(1024)S(1)} %sub.68, f32[2050,128]{1,0:T(8,128)S(1)} %maximum_convert_fusion.1, f32[2048,128]{1,0:T(8,128)S(1)} %copy.80, bf16[2048,128]{1,0:T(8,128)(2,1)S(1)} %fusion.20, f32[128]{0:T(128)S(1)} %copy-done.12, f32[2048]{0:T(1024)S(1)} %get-tuple-element.22, f32[128]{0:T(128)S(1)} %copy-done.9, ...), kind=kOutput, calls=%fused_computation.15 | convolution fusion | flops 1081344000 | bytes 5269504 | tf_op jit(solution)/shard_map/dot_general | solution.py:155
  138.8 38.5 %all_to_all.15 = bf16[64,32,128]{2,1,0:T(8,128)(2,1)S(1)} all-to-all(bf16[64,32,128]{2,1,0:T(8,128)(2,1)S(1)} %bitcast.110), channel_id=1, replica_groups=mesh['ctx'=64,'ch'=8] {'ctx'}, dimensions={0} | all-to-all | bytes 1048576 | tf_op jit(solution)/shard_map/all_to_all | solution.py:156
  177.3 0.8 copy_bitcast_fusion.1
  (57 shorter events, 1.0 us)
Async XLA Ops:
  1.3 22.1 %copy-start.11 = (s32[4]{0:T(128)S(1)}, s32[4]{0:T(128)}, u32[]{:S(2)}) copy-start(s32[4]{0:T(128)} %param.9) | copy-start | bytes 52
  1.3 23.0 %copy-start.3 = (f32[64,16]{0,1:T(8,128)S(1)}, f32[64,16]{0,1:T(8,128)}, u32[]{:S(2)}) copy-start(f32[64,16]{0,1:T(8,128)} %param.11) | copy-start | bytes 12292
  1.3 23.2 %copy-start.4 = (f32[64,16]{0,1:T(8,128)S(1)}, f32[64,16]{0,1:T(8,128)}, u32[]{:S(2)}) copy-start(f32[64,16]{0,1:T(8,128)} %param.12) | copy-start | bytes 12292
  1.3 23.3 %copy-start.2 = (f32[3,3,1024]{2,1,0:T(4,128)S(1)}, f32[3,3,1024]{2,1,0:T(4,128)}, u32[]{:S(2)}) copy-start(f32[3,3,1024]{2,1,0:T(4,128)} %param.10) | copy-start | bytes 110596
  1.3 23.4 %copy-start.5 = (f32[1024]{0:T(1024)S(1)}, f32[1024]{0:T(1024)}, u32[]{:S(2)}) copy-start(f32[1024]{0:T(1024)} %param.13) | copy-start | bytes 12292
  1.6 37.8 %copy-start.1 = (s32[16384]{0:T(1024)S(1)}, s32[16384]{0:T(1024)}, u32[]{:S(2)}) copy-start(s32[16384]{0:T(1024)} %param.8) | copy-start | bytes 196612
  4.2 70.7 %all-to-all-start = ((bf16[64,32,256]{2,1,0:T(8,128)(2,1)}), bf16[64,32,256]{2,1,0:T(8,128)(2,1)S(1)}, u32[]{:S(2)}, u32[]{:S(2)}) async-start(bf16[64,32,256]{2,1,0:T(8,128)(2,1)} %reshape.300), calls=%async_computation | async-start | bytes 2097152 | tf_op jit(solution)/shard_map/all_to_all | solution.py:65
  75.9 17.8 %collective-permute-start.1 = (bf16[2,256]{1,0:T(2,128)(2,1)S(1)}, bf16[2,256]{1,0:T(2,128)(2,1)S(1)}, u32[]{:S(2)}, u32[]{:S(2)}) collective-permute-start(bf16[2,256]{1,0:T(2,128)(2,1)S(1)} %convolution_convert_fusion), channel_id=1, source_target_pairs={{0,1},{1,2},{2,3},{3,4},{4,5},{5,6},{6,7},{8,9},{9,10},{10,11},{11... | collective-permute-start | bytes 3080 | tf_op jit(solution)/shard_map/ppermute | solution.py:70
  88.1 37.6 %all-to-all-start.1 = ((bf16[64,32,128]{2,1,0:T(8,128)(2,1)}), bf16[64,32,128]{2,1,0:T(8,128)(2,1)S(1)}, u32[]{:S(2)}, u32[]{:S(2)}) async-start(bf16[64,32,128]{2,1,0:T(8,128)(2,1)} %copy.69), calls=%async_computation.1 | async-start | bytes 1048576 | tf_op jit(solution)/shard_map/all_to_all | solution.py:65
  93.9 1.5 copy-start.7
  98.5 13.4 %copy-start = (bf16[8,256,256]{1,2,0:T(8,128)(2,1)S(1)}, bf16[8,256,256]{1,2,0:T(8,128)(2,1)}, u32[]{:S(2)}) copy-start(bf16[8,256,256]{1,2,0:T(8,128)(2,1)} %select_convert_fusion) | copy-start | bytes 3145732
  111.9 2.6 %copy-start.6 = (f32[256]{0:T(256)S(1)}, f32[256]{0:T(256)}, u32[]{:S(2)}) copy-start(f32[256]{0:T(256)} %iota_add_fusion.1) | copy-start | bytes 3076
  126.6 6.9 %copy-start.8 = (f32[128]{0:T(128)S(1)}, f32[128]{0:T(128)}, u32[]{:S(2)}) copy-start(f32[128]{0:T(128)} %get-tuple-element.9) | copy-start | bytes 1540
  126.6 6.9 %copy-start.9 = (f32[128]{0:T(128)S(1)}, f32[128]{0:T(128)}, u32[]{:S(2)}) copy-start(f32[128]{0:T(128)} %get-tuple-element.15) | copy-start | bytes 1540
  126.6 6.9 %copy-start.10 = (f32[128]{0:T(128)S(1)}, f32[128]{0:T(128)}, u32[]{:S(2)}) copy-start(f32[128]{0:T(128)} %get-tuple-element.16) | copy-start | bytes 1540
  126.6 6.9 %copy-start.12 = (f32[128]{0:T(128)S(1)}, f32[128]{0:T(128)}, u32[]{:S(2)}) copy-start(f32[128]{0:T(128)} %dynamic_slice.19) | copy-start | bytes 1540
  126.7 6.7 %collective-permute-start = (bf16[2,128]{1,0:T(2,128)(2,1)S(1)}, bf16[2,128]{1,0:T(2,128)(2,1)S(1)}, u32[]{:S(2)}, u32[]{:S(2)}) collective-permute-start(bf16[2,128]{1,0:T(2,128)(2,1)S(1)} %convolution_convert_fusion.1), channel_id=1, source_target_pairs={{0,1},{1,2},{2,3},{3,4},{4,5},{5,6},{6,7},{8,9},{9,10},{10,11},{11... | collective-permute-start | bytes 1544 | tf_op jit(solution)/shard_map/ppermute | solution.py:70

commit v9 on v7

--- a/solution.py
+++ b/solution.py
@@ -62,8 +62,8 @@
         received = lax.all_to_all(sending, "ctx", 0, 0, tiled=True)
         received = received.reshape(n_ctx * rows_here, count * width)
         arrived.append(received)
-        ordered = jnp.dot(placer, received, preferred_element_type=jnp.float32).astype(jnp.bfloat16)
-        tail = jnp.dot(placer[span - 2 :], received, preferred_element_type=jnp.float32).astype(jnp.bfloat16)
+        ordered = jnp.dot(placer, received, preferred_element_type=jnp.bfloat16)
+        tail = jnp.dot(placer[span - 2 :], received, preferred_element_type=jnp.bfloat16)
         earlier = lax.ppermute(tail, "ch", [(i, i + 1) for i in range(n_ch - 1)])
         widened = jnp.concatenate([earlier, ordered], axis=0).astype(jnp.float32)
         return [widened[:, p * width : (p + 1) * width] for p in range(count)]
@@ -149,7 +149,7 @@
     (query_rows,) = arrive(query_part)
     mixed = (feature(0, query_rows) * combined).astype(jnp.bfloat16)
 
-    back = jnp.dot(placer.T, mixed, preferred_element_type=jnp.float32).astype(jnp.bfloat16)
+    back = jnp.dot(placer.T, mixed, preferred_element_type=jnp.bfloat16)
     returned = lax.all_to_all(back.reshape(n_ctx, rows_here, width), "ctx", 0, 0, tiled=True)
     return jnp.transpose(returned, (1, 0, 2)).reshape(rows_here, n_ctx * width)
 

time: 179 us -> 179 us (level)
  no operation moved by 1% of the time
where the time goes in v9:
time: 179 us; the launch traced here: 178 us
  blocking collectives  65.7 us (37%)
  starting transfers between devices  36.3 us (20%)
  waiting for transfers between devices  30.1 us (17%)
  matrix products  21.5 us (12%)
  other arithmetic  12.4 us (7%)
  local copies, waits for them, and re-layouts  11.7 us (7%)
    all_to_all x1, blocking collectives, layer(): lax.all_to_all(back.reshape(n_ctx, rows_here, width), 'ctx', 0, 0, tiled=...  38.4 us
    all_to_all x2, waiting for transfers between devices, arrive(): received = lax.all_to_all(sending, 'ctx', 0, 0, tiled=True)  30.1 us
    all_to_all x2, starting transfers between devices, arrive(): received = lax.all_to_all(sending, 'ctx', 0, 0, tiled=True)  24.6 us
    all_gather x1, blocking collectives, layer(): every = lax.all_gather(flat, 'ch')  14.5 us
    all_gather x1, blocking collectives, layer(): gathered = lax.all_gather(local_state[chunks - 1], 'ch')  12.8 us
    ppermute x2, starting transfers between devices, arrive(): earlier = lax.ppermute(tail, 'ch', [(i, i + 1) for i in range(n_ch - 1)])  11.6 us
    dot_general x2, matrix products, arrive(): ordered = jnp.dot(placer, received, preferred_element_type=jnp.bfloat16)  6.16 us
    eq x1, other arithmetic, layer(): (mine - here_ch * span)[None, :]  5.66 us
  transfers between devices with their start and end apart: 4, of which 2 were waited for; matrix products, arithmetic and copies ran while one was open for 17% of the time, Pallas kernels for 0%

profile of v9, /device:TPU:1, one launch (start us, length us, event | category | flops | bytes accessed | tf_op | source)
XLA Modules:
  0.0 178.2 jit_solution(140306423654421584)
XLA Ops:
  0.0 1.3 slice.113
  1.4 0.3 copy.89
  1.6 1.1 copy.99
  2.7 1.5 reshape.300
  4.2 19.1 %all-to-all-start = ((bf16[64,32,256]{2,1,0:T(8,128)(2,1)}), bf16[64,32,256]{2,1,0:T(8,128)(2,1)S(1)}, u32[]{:S(2)}, u32[]{:S(2)}) async-start(bf16[64,32,256]{2,1,0:T(8,128)(2,1)} %reshape.300), calls=%async_computation | async-start | bytes 2097152 | tf_op jit(solution)/shard_map/all_to_all | solution.py:62
  23.4 0.2 reduce-window.8
  23.6 0.1 convert_reduce_fusion
  23.8 0.2 slice_reduce_fusion.1
  23.9 0.1 copy.66
  24.0 0.1 reshape.295
  24.1 0.1 copy.67
  24.2 0.1 reshape.296
  24.4 14.5 %all-gather = f32[98304]{0:T(1024)S(1)} all-gather(f32[12288]{0:T(1024)S(1)} %pad_maximum_fusion), channel_id=2, replica_groups=mesh['ctx'=64,'ch'=8] {'ch'}, dimensions={0}, use_global_device_ids=true | all-gather | bytes 442368 | tf_op jit(solution)/shard_map/all_gather | solution.py:37
  38.8 0.1 reshape.313
  38.9 0.1 reshape.308
  39.1 0.1 reshape.307
  39.2 0.1 dynamic-slice_subtract_fusion
  39.3 0.6 slice.160
  40.0 0.2 reshape.298
  40.2 0.1 convert_reduce_fusion.1
  40.3 0.7 compare_convert_fusion.2
  41.0 0.1 exponential_multiply_fusion
  41.1 0.1 dynamic_slice.19
  41.2 0.2 slice_reduce_fusion
  41.3 0.7 pad_add_fusion
  42.1 0.1 fusion.67
  42.5 0.2 exponential_select_fusion
  42.7 3.0 %subtract_convert_fusion = (bf16[8,256,256]{1,2,0:T(8,128)(2,1)}, bf16[8,256,256]{1,2,0:T(8,128)(2,1)S(1)}) fusion(pred[256,256]{0,1:T(8,128)(4,1)S(1)} %iota_compare_fusion.4, f32[8,16]{1,0:T(8,128)S(1)} %get-tuple-element.8, f32[8,16]{1,0:T(8,128)S(1)} %neg.12, f32[8,16]{1,0:T(8,128)S(1)} %get-tuple-element.7), kind=kOutput, calls=%fused_computation.16 | convolution fusion | flops 103907328 | bytes 2164224 | tf_op jit(solution)/shard_map/gtm,gms->gts/dot_general | solution.py:94
  45.7 1.2 select_convert_fusion
  46.9 5.7 %iota_compare_fusion = pred[2048,2048]{1,0:T(8,128)(4,1)} fusion(s32[2048]{0:T(1024)S(1)} %sub.68), kind=kLoop, calls=%fused_computation | loop fusion | flops 4194304 | bytes 4202496 | tf_op jit(solution)/shard_map/eq | solution.py:53
  52.6 22.4 %all-to-all-done = bf16[64,32,256]{2,1,0:T(8,128)(2,1)S(1)} async-done(((bf16[64,32,256]{2,1,0:T(8,128)(2,1)}), bf16[64,32,256]{2,1,0:T(8,128)(2,1)S(1)}, u32[]{:S(2)}, u32[]{:S(2)}) %all-to-all-start) | async-done | bytes 1048608 | tf_op jit(solution)/shard_map/all_to_all | solution.py:62
  75.0 3.2 %fusion.1 = bf16[2048,256]{1,0:T(8,128)(2,1)S(1)} fusion(bf16[2048,256]{1,0:T(8,128)(2,1)S(1)} %bitcast.96, s32[2048]{0:T(1024)S(1)} %sub.68), kind=kOutput, calls=%fused_computation.2 | convolution fusion | flops 2151677952 | bytes 2105344 | tf_op jit(solution)/shard_map/dot_general | solution.py:65
  78.2 0.1 copy.91
  78.3 1.0 fusion.60
  79.3 7.7 %collective-permute-start.1 = (bf16[2,256]{1,0:T(2,128)(2,1)S(1)}, bf16[2,256]{1,0:T(2,128)(2,1)S(1)}, u32[]{:S(2)}, u32[]{:S(2)}) collective-permute-start(bf16[2,256]{1,0:T(2,128)(2,1)S(1)} %fusion.60), channel_id=1, source_target_pairs={{0,1},{1,2},{2,3},{3,4},{4,5},{5,6},{6,7},{8,9},{9,10},{10,11},{11... | collective-permute-start | bytes 3080 | tf_op jit(solution)/shard_map/ppermute | solution.py:67
  87.0 1.1 copy.69
  88.2 5.5 %all-to-all-start.1 = ((bf16[64,32,128]{2,1,0:T(8,128)(2,1)}), bf16[64,32,128]{2,1,0:T(8,128)(2,1)S(1)}, u32[]{:S(2)}, u32[]{:S(2)}) async-start(bf16[64,32,128]{2,1,0:T(8,128)(2,1)} %copy.69), calls=%async_computation.1 | async-start | bytes 1048576 | tf_op jit(solution)/shard_map/all_to_all | solution.py:62
  93.7 0.2 maximum_convert_fusion
  93.9 0.9 fusion.17
  94.9 0.2 copy.70
  95.1 0.1 copy.90
  95.2 0.1 convert_multiply_fusion
  95.3 0.1 copy.71
  95.4 1.3 convolution_bitcast_fusion
  96.7 0.2 copy.75
  96.9 1.3 multiply_reduce_fusion
  98.3 0.2 copy.87
  98.5 12.8 %all_gather.11 = f32[8,8,16,16]{3,2,1,0:T(8,128)S(1)} all-gather(f32[1,8,16,16]{3,2,1,0:T(8,128)S(1)} %slice.162), channel_id=1, replica_groups=mesh['ctx'=64,'ch'=8] {'ch'}, dimensions={0}, use_global_device_ids=true | all-gather | bytes 73728 | tf_op jit(solution)/shard_map/all_gather | solution.py:126
  111.3 0.2 multiply_reduce_fusion.1
  111.5 0.1 copy.76
  111.6 0.2 broadcast_select_fusion
  111.8 2.9 %select_reduce_fusion = f32[8,8,16,256]{3,2,1,0:T(8,128)S(1)} fusion(pred[4,8,256]{2,1,0:T(8,128)(4,1)S(1)} %iota_compare_fusion.5, bf16[8,256,256]{1,2,0:T(8,128)(2,1)} %get-tuple-element.27, bf16[8,256,256]{1,2,0:T(8,128)(2,1)} %select_convert_fusion, bf16[4,8,256,8,16]{2,4,1,0,3:T(8,128)(2,1)S(1)} %broadcast_select_fusion), kind=kOutput, calls=%fused_computation.12 | convolution fusion | flops 1088159744 | bytes 5251072 | tf_op jit(solution)/shard_map/gts,dksgc->dktgc/dot_general | solution.py:105
  114.7 1.1 fusion.13
  115.7 0.6 copy.79
  116.4 0.3 copy.92
  116.7 1.3 copy.80
  118.0 7.7 %all-to-all-done.1 = bf16[64,32,128]{2,1,0:T(8,128)(2,1)S(1)} async-done(((bf16[64,32,128]{2,1,0:T(8,128)(2,1)}), bf16[64,32,128]{2,1,0:T(8,128)(2,1)S(1)}, u32[]{:S(2)}, u32[]{:S(2)}) %all-to-all-start.1) | async-done | bytes 524320 | tf_op jit(solution)/shard_map/all_to_all | solution.py:62
  125.7 0.9 fusion.62
  126.6 3.9 %collective-permute-start = (bf16[2,128]{1,0:T(2,128)(2,1)S(1)}, bf16[2,128]{1,0:T(2,128)(2,1)S(1)}, u32[]{:S(2)}, u32[]{:S(2)}) collective-permute-start(bf16[2,128]{1,0:T(2,128)(2,1)S(1)} %fusion.62), channel_id=1, source_target_pairs={{0,1},{1,2},{2,3},{3,4},{4,5},{5,6},{6,7},{8,9},{9,10},{10,11},{11... | collective-permute-start | bytes 1544 | tf_op jit(solution)/shard_map/ppermute | solution.py:67
  130.6 3.0 %fusion.2 = bf16[2048,128]{1,0:T(8,128)(2,1)S(1)} fusion(bf16[2048,128]{1,0:T(8,128)(2,1)S(1)} %bitcast.105, s32[2048]{0:T(1024)S(1)} %sub.68), kind=kOutput, calls=%fused_computation.3 | convolution fusion | flops 1077936128 | bytes 1056768 | tf_op jit(solution)/shard_map/dot_general | solution.py:65
  133.6 0.1 maximum_convert_fusion.1
  133.7 5.2 %fusion = bf16[2048,128]{1,0:T(8,128)(2,1)S(1)} fusion(s32[2048]{0:T(1024)S(1)} %sub.68, f32[2050,128]{1,0:T(8,128)S(1)} %maximum_convert_fusion.1, f32[2048,128]{1,0:T(8,128)S(1)} %copy-done, bf16[2048,128]{1,0:T(8,128)(2,1)S(1)} %fusion.17, f32[128]{0:T(128)S(1)} %dynamic_slice.19, f32[2048]{0:T(1024)S(1)} %get-tuple-element.22, ...), kind=kOutput, calls=%fused_computation.1 | convolution fusion | flops 1081081856 | bytes 5269504 | tf_op jit(solution)/shard_map/dot_general | solution.py:152
  138.9 38.4 %all_to_all.15 = bf16[64,32,128]{2,1,0:T(8,128)(2,1)S(1)} all-to-all(bf16[64,32,128]{2,1,0:T(8,128)(2,1)S(1)} %bitcast.110), channel_id=1, replica_groups=mesh['ctx'=64,'ch'=8] {'ctx'}, dimensions={0} | all-to-all | bytes 1048576 | tf_op jit(solution)/shard_map/all_to_all | solution.py:153
  177.3 0.8 copy_bitcast_fusion.1
  (46 shorter events, 0.8 us)
Async XLA Ops:
  1.3 22.1 %copy-start.6 = (s32[4]{0:T(128)S(1)}, s32[4]{0:T(128)}, u32[]{:S(2)}) copy-start(s32[4]{0:T(128)} %param.9) | copy-start | bytes 52
  1.3 22.6 %copy-start.3 = (f32[64,16]{0,1:T(8,128)S(1)}, f32[64,16]{0,1:T(8,128)}, u32[]{:S(2)}) copy-start(f32[64,16]{0,1:T(8,128)} %param.11) | copy-start | bytes 12292
  1.3 22.8 %copy-start.4 = (f32[64,16]{0,1:T(8,128)S(1)}, f32[64,16]{0,1:T(8,128)}, u32[]{:S(2)}) copy-start(f32[64,16]{0,1:T(8,128)} %param.12) | copy-start | bytes 12292
  1.3 22.9 %copy-start.2 = (f32[3,3,1024]{2,1,0:T(4,128)S(1)}, f32[3,3,1024]{2,1,0:T(4,128)}, u32[]{:S(2)}) copy-start(f32[3,3,1024]{2,1,0:T(4,128)} %param.10) | copy-start | bytes 110596
  1.3 23.0 %copy-start.1 = (s32[16384]{0:T(1024)S(1)}, s32[16384]{0:T(1024)}, u32[]{:S(2)}) copy-start(s32[16384]{0:T(1024)} %param.8) | copy-start | bytes 196612
  1.4 23.0 %copy-start.5 = (f32[1024]{0:T(1024)S(1)}, f32[1024]{0:T(1024)}, u32[]{:S(2)}) copy-start(f32[1024]{0:T(1024)} %param.13) | copy-start | bytes 12292
  4.2 70.7 %all-to-all-start = ((bf16[64,32,256]{2,1,0:T(8,128)(2,1)}), bf16[64,32,256]{2,1,0:T(8,128)(2,1)S(1)}, u32[]{:S(2)}, u32[]{:S(2)}) async-start(bf16[64,32,256]{2,1,0:T(8,128)(2,1)} %reshape.300), calls=%async_computation | async-start | bytes 2097152 | tf_op jit(solution)/shard_map/all_to_all | solution.py:62
  75.0 3.2 %slice-start = ((bf16[3,32,8192]{2,1,0:T(8,128)(2,1)}), bf16[1,32,8192]{2,1,0:T(8,128)(2,1)S(1)}, s32[]{:S(2)}) async-start(bf16[3,32,8192]{2,1,0:T(8,128)(2,1)} %param.7), calls=%async_computation.3 | async-start | bytes 1048576 | tf_op jit(solution)/shard_map/slice | solution.py:148
  79.3 14.5 %collective-permute-start.1 = (bf16[2,256]{1,0:T(2,128)(2,1)S(1)}, bf16[2,256]{1,0:T(2,128)(2,1)S(1)}, u32[]{:S(2)}, u32[]{:S(2)}) collective-permute-start(bf16[2,256]{1,0:T(2,128)(2,1)S(1)} %fusion.60), channel_id=1, source_target_pairs={{0,1},{1,2},{2,3},{3,4},{4,5},{5,6},{6,7},{8,9},{9,10},{10,11},{11... | collective-permute-start | bytes 3080 | tf_op jit(solution)/shard_map/ppermute | solution.py:67
  88.2 37.6 %all-to-all-start.1 = ((bf16[64,32,128]{2,1,0:T(8,128)(2,1)}), bf16[64,32,128]{2,1,0:T(8,128)(2,1)S(1)}, u32[]{:S(2)}, u32[]{:S(2)}) async-start(bf16[64,32,128]{2,1,0:T(8,128)(2,1)} %copy.69), calls=%async_computation.1 | async-start | bytes 1048576 | tf_op jit(solution)/shard_map/all_to_all | solution.py:62
  126.6 7.0 %copy-start = (f32[2048,128]{1,0:T(8,128)S(1)}, f32[2048,128]{1,0:T(8,128)}, u32[]{:S(2)}) copy-start(f32[2048,128]{1,0:T(8,128)} %copy.80) | copy-start | bytes 3145732
  126.6 6.9 %collective-permute-start = (bf16[2,128]{1,0:T(2,128)(2,1)S(1)}, bf16[2,128]{1,0:T(2,128)(2,1)S(1)}, u32[]{:S(2)}, u32[]{:S(2)}) collective-permute-start(bf16[2,128]{1,0:T(2,128)(2,1)S(1)} %fusion.62), channel_id=1, source_target_pairs={{0,1},{1,2},{2,3},{3,4},{4,5},{5,6},{6,7},{8,9},{9,10},{10,11},{11... | collective-permute-start | bytes 1544 | tf_op jit(solution)/shard_map/ppermute | solution.py:67
